TPU v7x, 256 devices: a whole 4x4x8 slice. The times are simulated.
256 devices in a mesh: stream: 8 (over z), span: 32 (over y, x, core).
Axes of the slice: x: 4, y: 4, z: 8, core: 2. Of those that a mesh axis runs over, the one named last changes fastest.
Arguments:
- velocity: float32 [3, 64, 512, 1024], P(None, 'stream', 'span'), may hold values from -36 to 36
- coefficient: float32 [64, 512, 1024], P('stream', 'span'), may hold values from 0.5 to 4
- coords: float32 [3, 32768], P(None, ('stream', 'span')), may hold values from -1 to 1
- forces: float32 [3, 32768], P(None, ('stream', 'span')), may hold values from -12 to 12
- line_id: int32 [32768], P(('stream', 'span')), may hold values from 0 to 399
- line_gain: float32 [400], replicated, may hold values from 0.5 to 2
- dest_span: int32 [32768, 1], P(('stream', 'span')), may hold values from 0 to 31; in each aligned block of 128 rows (0 to 127, 128 to 255, ...) at most 8 rows name the same one
- owner_element: int32 [32768], P(('stream', 'span')), may hold values from 0 to 255
Outputs:
- pressure: float32 [64, 512, 1024], P('stream', 'span')
- residual: float32 [64, 512, 1024], P('stream', 'span')
Inputs may be any that keep to these rules, and one draw needn't show every extreme that they name: `dest_span`: of the 128 blade points of one device, at most 8 name the same span index, and in every draw some span index is named by exactly 8 of one device's points. `owner_element`: an element of the device at the point's span index in the same slab, numbered (ex * 2 + ey) * 128 + ez.
All inputs are finite; a program needn't handle non-finite values.
Results may differ from a plain program's by a relative error of at most 0.00019.
Values sent between devices are 32-bit elements; how exact they have to be, the bound alone decides.
No kernel may reach another device: no remote copies, remote signals or barrier semaphores. Data moves between devices by JAX's collectives and lax.ppermute only.
A program may use at most 64 MiB of HBM per device.

v0:
```python
import jax
import jax.numpy as jnp
from jax import lax
from jax.sharding import PartitionSpec as P

POLY = 8
ITERS = 3


kernel_width = 0.45
gll_nodes = [
    -1.0,
    -0.8717401485096066,
    -0.5917001814331423,
    -0.2092992179024789,
    0.2092992179024789,
    0.5917001814331423,
    0.8717401485096066,
    1.0,
]


def with_halo(x, sides, width):
    for axis, dim in sides:
        size, length = (lax.axis_size(axis), x.shape[dim])
        up = [(i, (i + 1) % size) for i in range(size - 1)]
        down = [(j, i) for i, j in up]
        last = lax.slice_in_dim(x, length - width, length, axis=dim)
        first = lax.slice_in_dim(x, 0, width, axis=dim)
        before = lax.ppermute(last, axis, up)
        after = lax.ppermute(first, axis, down)
        x = jnp.concatenate([before, x, after], axis=dim)
    return x


def legendre_value(point, degree):
    previous = 1.0
    current = point
    for order in range(1, degree):
        following = ((2 * order + 1) * point * current - order * previous) / (order + 1)
        previous = current
        current = following
    return current


def gll_tables():
    degree = POLY - 1
    values = [legendre_value(point, degree) for point in gll_nodes]
    weights = [2.0 / (degree * (degree + 1) * value * value) for value in values]
    diffmat = []
    for row_at in range(POLY):
        row_list = []
        for col_at in range(POLY):
            if row_at != col_at:
                row_list.append(
                    values[row_at] / (values[col_at] * (gll_nodes[row_at] - gll_nodes[col_at]))
                )
            elif row_at == 0:
                row_list.append(-degree * (degree + 1) / 4.0)
            elif row_at == degree:
                row_list.append(degree * (degree + 1) / 4.0)
            else:
                row_list.append(0.0)
        diffmat.append(row_list)
    return (
        jnp.asarray(gll_nodes, dtype=jnp.float32),
        jnp.asarray(weights, dtype=jnp.float32),
        jnp.asarray(diffmat, dtype=jnp.float32),
    )


def derive(grid_field, diffmat, axis_at, flipped):
    matrix = diffmat.T if flipped else diffmat
    extent0, extent1, extent2 = grid_field.shape
    highest = lax.Precision.HIGHEST
    if axis_at == 0:
        blocks = grid_field.reshape(extent0 // POLY, POLY, extent1, extent2)
        result = jnp.einsum("ia,xayz->xiyz", matrix, blocks, precision=highest)
    elif axis_at == 1:
        blocks = grid_field.reshape(extent0, extent1 // POLY, POLY, extent2)
        result = jnp.einsum("ib,xybz->xyiz", matrix, blocks, precision=highest)
    else:
        block_width = 128
        tiled_matrix = jnp.kron(jnp.eye(block_width // POLY, dtype=jnp.float32), matrix)
        blocks = grid_field.reshape(extent0, extent1, extent2 // block_width, block_width)
        result = jnp.einsum("xyzc,ic->xyzi", blocks, tiled_matrix, precision=highest)
    return result.reshape(grid_field.shape)


def face_masks(extent):
    node = lax.iota(jnp.int32, extent) % POLY
    return (node == 0, node == POLY - 1)


def assemble(grid_field):
    extent0, extent1, extent2 = grid_field.shape
    first0, last0 = face_masks(extent0)
    first1, last1 = face_masks(extent1)
    first2, last2 = face_masks(extent2)
    first0, last0 = (first0[:, None, None], last0[:, None, None])
    first1, last1 = (first1[None, :, None], last1[None, :, None])
    first2, last2 = (first2[None, None, :], last2[None, None, :])
    nothing = jnp.zeros_like(grid_field)
    padded = with_halo(grid_field, (("stream", 0),), 1)
    running = (
        grid_field + jnp.where(first0, padded[:-2], nothing) + jnp.where(last0, padded[2:], nothing)
    )
    padded = with_halo(running, (("span", 1),), 1)
    running = (
        running
        + jnp.where(first1, padded[:, :-2], nothing)
        + jnp.where(last1, padded[:, 2:], nothing)
    )
    before = jnp.pad(running, ((0, 0), (0, 0), (1, 0)))[:, :, :-1]
    after = jnp.pad(running, ((0, 0), (0, 0), (0, 1)))[:, :, 1:]
    return running + jnp.where(first2, before, nothing) + jnp.where(last2, after, nothing)


def inverse_multiplicity(extent, offset, whole):
    node = lax.iota(jnp.int32, extent) % POLY
    position = offset + lax.iota(jnp.int32, extent)
    inner_face = (node == 0) & (position > 0) | (node == POLY - 1) & (position < whole - 1)
    return jnp.where(inner_face, 0.5, 1.0).astype(jnp.float32)


def mesh_sum(values):
    axes = ("stream", "span")
    count = lax.axis_size(axes)
    spread = jnp.broadcast_to(values[None], (count,) + values.shape)
    gathered = lax.all_to_all(spread, axes, 0, 0, tiled=True)
    return jnp.sum(gathered, axis=0)


def spread_points(arrived, abscissa, extent0, extent1, extent2):
    elems_y, elems_z = (extent1 // POLY, extent2 // POLY)
    kernels = []
    for dimension in range(3):
        kernels.append(
            jnp.exp(
                -(((abscissa[None, :] - arrived[:, dimension : dimension + 1]) / kernel_width) ** 2)
            )
        )
    element = arrived[:, 6].astype(jnp.int32) - 1
    valid = element >= 0
    elem_x = element // (elems_y * elems_z)
    elem_y = (element // elems_z) % elems_y
    elem_z = element % elems_z
    grid0 = lax.iota(jnp.int32, extent0)
    grid1 = lax.iota(jnp.int32, extent1)
    grid2 = lax.iota(jnp.int32, extent2)
    node0 = jnp.tile(kernels[0], (1, extent0 // POLY))
    node1 = jnp.tile(kernels[1], (1, extent1 // POLY))
    node2 = jnp.tile(kernels[2], (1, extent2 // POLY))
    along0 = jnp.where(elem_x[:, None] == grid0[None, :] // POLY, node0, 0.0)
    along1 = jnp.where(elem_y[:, None] == grid1[None, :] // POLY, node1, 0.0)
    along2 = jnp.where(
        valid[:, None] & (elem_z[:, None] == grid2[None, :] // POLY), node2, 0.0
    )
    left = arrived[:, 3:6][:, :, None, None] * (along0[:, None, :, None] * along1[:, None, None, :])
    return jnp.einsum("pcxy,pz->cxyz", left, along2, precision=lax.Precision.HIGHEST)


def project_points(coords, forces, line_id, line_gain, dest_span, owner_element, abscissa, extents):
    points_dev = coords.shape[1]
    spans = lax.axis_size("span")
    capacity = max(2, 2 * points_dev // spans)
    table_ids = lax.iota(jnp.int32, line_gain.shape[0])
    gains = jnp.sum(
        jnp.where(line_id[:, None] == table_ids[None, :], line_gain[None, :], 0.0), axis=1
    )
    scaled = forces * gains[None, :]
    target = dest_span[:, 0]
    owner_code = (owner_element + 1).astype(jnp.float32)
    payload = jnp.concatenate(
        [coords, scaled, owner_code[None, :], target.astype(jnp.float32)[None, :]], axis=0
    ).T
    order = lax.iota(jnp.int32, points_dev)
    earlier = (target[:, None] == target[None, :]) & (order[None, :] < order[:, None])
    ranks = jnp.sum(earlier.astype(jnp.int32), axis=1)
    slot_at = target * capacity + ranks
    outgoing = jnp.zeros((spans * capacity, 8), jnp.float32).at[slot_at].set(payload)
    outgoing = outgoing.reshape(spans, capacity, 8)
    arrived = lax.all_to_all(outgoing, "span", split_axis=0, concat_axis=0, tiled=True).reshape(
        spans * capacity, 8
    )
    return spread_points(arrived, abscissa, extents[0], extents[1], extents[2])


def local_operator(grid_field, weight3, metric, diffmat):
    running = weight3 * grid_field
    for axis_at in range(3):
        running = running + derive(
            metric * derive(grid_field, diffmat, axis_at, False), diffmat, axis_at, True
        )
    return running


def on_device(velocity, coefficient, coords, forces, line_id, line_gain, dest_span, owner_element):
    abscissa, weights, diffmat = gll_tables()
    extent0, extent1, extent2 = coefficient.shape
    tile_zero = jnp.tile(weights, extent0 // POLY)
    tile_one = jnp.tile(weights, extent1 // POLY)
    tile_two = jnp.tile(weights, extent2 // POLY)
    weight3 = tile_zero[:, None, None] * tile_one[None, :, None] * tile_two[None, None, :]
    metric = weight3 * coefficient
    inv_zero = inverse_multiplicity(
        extent0, lax.axis_index("stream") * extent0, extent0 * lax.axis_size("stream")
    )
    inv_one = inverse_multiplicity(
        extent1, lax.axis_index("span") * extent1, extent1 * lax.axis_size("span")
    )
    inv_two = inverse_multiplicity(extent2, 0, extent2)
    inv_mult = inv_zero[:, None, None] * inv_one[None, :, None] * inv_two[None, None, :]
    forcing = project_points(
        coords,
        forces,
        line_id,
        line_gain,
        dest_span,
        owner_element,
        abscissa,
        (extent0, extent1, extent2),
    )
    running = derive(weight3 * (velocity[0] + forcing[0]), diffmat, 0, True)
    running = running + derive(weight3 * (velocity[1] + forcing[1]), diffmat, 1, True)
    running = running + derive(weight3 * (velocity[2] + forcing[2]), diffmat, 2, True)
    rhs = assemble(running)

    def weighted(first_vec, second_vec):
        return jnp.sum(first_vec * second_vec * inv_mult)

    pressure = jnp.zeros_like(rhs)
    residual = rhs
    direction = rhs
    local = local_operator(residual, weight3, metric, diffmat)
    sums = mesh_sum(jnp.stack([weighted(residual, residual), jnp.sum(residual * local)]))
    norm_now, curvature = sums[0], sums[1]
    searched = assemble(local)
    step_len = norm_now / curvature
    for iteration in range(1, ITERS + 1):
        pressure = pressure + step_len * direction
        residual = residual - step_len * searched
        if iteration == ITERS:
            break
        local = local_operator(residual, weight3, metric, diffmat)
        sums = mesh_sum(
            jnp.stack(
                [
                    weighted(residual, residual),
                    jnp.sum(residual * local),
                    weighted(residual, searched),
                ]
            )
        )
        applied = assemble(local)
        norm_next, own_curvature, cross = sums[0], sums[1], sums[2]
        ratio = norm_next / norm_now
        direction = residual + ratio * direction
        searched = applied + ratio * searched
        curvature = own_curvature + 2.0 * ratio * cross + ratio * ratio * curvature
        norm_now = norm_next
        step_len = norm_now / curvature
    return (pressure, residual)


def solution(mesh):
    return jax.shard_map(
        on_device,
        mesh=mesh,
        in_specs=(
            P(None, "stream", "span", None),
            P("stream", "span", None),
            P(None, ("stream", "span")),
            P(None, ("stream", "span")),
            P(("stream", "span")),
            P(),
            P(("stream", "span"), None),
            P(("stream", "span")),
        ),
        out_specs=(P("stream", "span", None), P("stream", "span", None)),
        check_vma=False,
    )
```

profile of v0, /device:TPU:1, one launch (start us, length us, event | category | flops | bytes accessed | tf_op | source)
XLA Modules:
  0.0 185.7 jit_solution(3364920934994511856)
XLA Ops:
  1.3 0.9 convert_reduce_fusion
  2.2 0.7 convert_bitcast_fusion
  3.0 0.8 select_reduce_fusion
  5.3 0.9 scatter_custom_fusion
  6.2 0.8 copy.331
  6.9 8.6 %all-to-all-start = ((f32[32,8,8]{1,2,0:T(8,128)}), f32[32,8,8]{1,2,0:T(8,128)S(1)}, u32[]{:S(2)}, u32[]{:S(2)}) async-start(f32[32,8,8]{1,2,0:T(8,128)} %copy.331), calls=%async_computation | async-start | bytes 262144 | tf_op jit(solution)/shard_map/all_to_all | solution.py:183
  15.6 0.8 broadcast_multiply_fusion.4
  17.1 0.7 broadcast_multiply_fusion.5
  17.9 0.9 broadcast_multiply_fusion
  19.5 3.6 %all-to-all-done = f32[32,8,8]{1,2,0:T(8,128)S(1)} async-done(((f32[32,8,8]{1,2,0:T(8,128)}), f32[32,8,8]{1,2,0:T(8,128)S(1)}, u32[]{:S(2)}, u32[]{:S(2)}) %all-to-all-start) | async-done | bytes 8224 | tf_op jit(solution)/shard_map/all_to_all | solution.py:183
  23.5 1.7 fusion.20
  26.9 0.8 convolution_bitcast_fusion.18
  27.7 0.9 fusion.1
  28.8 3.5 %collective-permute-start = (f32[1,16,1024]{2,0,1:T(1,128)S(1)}, f32[1,16,1024]{2,0,1:T(1,128)S(1)}, u32[]{:S(2)}, u32[]{:S(2)}) collective-permute-start(f32[1,16,1024]{2,0,1:T(1,128)S(1)} %get-tuple-element.53), channel_id=1, source_target_pairs={{0,32},{32,64},{64,96},{96,128},{128,160},{160,192},{192,224},{1,3... | collective-permute-start | bytes 196616 | tf_op jit(solution)/shard_map/ppermute | solution.py:30
  32.3 1.3 collective-permute-start.1
  33.6 3.9 %collective-permute-done.1 = f32[1,16,1024]{2,0,1:T(1,128)S(1)} collective-permute-done((f32[1,16,1024]{2,0,1:T(1,128)S(1)}, f32[1,16,1024]{2,0,1:T(1,128)S(1)}, u32[]{:S(2)}, u32[]{:S(2)}) %collective-permute-start.1) | collective-permute-done | bytes 65568 | tf_op jit(solution)/shard_map/ppermute | solution.py:31
  37.8 3.8 %collective-permute-start.2 = (f32[8,1,1024]{2,0,1:T(8,128)S(1)}, f32[8,1,1024]{2,0,1:T(8,128)S(1)}, u32[]{:S(2)}, u32[]{:S(2)}) collective-permute-start(f32[8,1,1024]{2,0,1:T(8,128)S(1)} %get-tuple-element.51), channel_id=1, source_target_pairs={{0,1},{1,2},{2,3},{3,4},{4,5},{5,6},{6,7},{7,8},{8,9},{9,10},{10,1... | collective-permute-start | bytes 98312 | tf_op jit(solution)/shard_map/ppermute | solution.py:30
  41.6 2.1 %collective-permute-start.3 = (f32[8,1,1024]{2,0,1:T(8,128)S(1)}, f32[8,1,1024]{2,0,1:T(8,128)S(1)}, u32[]{:S(2)}, u32[]{:S(2)}) collective-permute-start(f32[8,1,1024]{2,0,1:T(8,128)S(1)} %get-tuple-element.52), channel_id=1, source_target_pairs={{1,0},{2,1},{3,2},{4,3},{5,4},{6,5},{7,6},{8,7},{9,8},{10,9},{11,1... | collective-permute-start | bytes 98312 | tf_op jit(solution)/shard_map/ppermute | solution.py:31
  44.3 2.5 %collective-permute-done.3 = f32[8,1,1024]{2,0,1:T(8,128)S(1)} collective-permute-done((f32[8,1,1024]{2,0,1:T(8,128)S(1)}, f32[8,1,1024]{2,0,1:T(8,128)S(1)}, u32[]{:S(2)}, u32[]{:S(2)}) %collective-permute-start.3) | collective-permute-done | bytes 32800 | tf_op jit(solution)/shard_map/ppermute | solution.py:31
  47.3 0.9 convolution_bitcast_fusion.15
  48.5 0.9 fusion.2
  49.8 0.9 convolution_bitcast_fusion.14
  51.0 0.7 fusion.15
  53.1 3.5 %collective-permute-start.4 = (f32[1,16,1024]{2,0,1:T(1,128)S(1)}, f32[1,16,1024]{2,0,1:T(1,128)S(1)}, u32[]{:S(2)}, u32[]{:S(2)}) collective-permute-start(f32[1,16,1024]{2,0,1:T(1,128)S(1)} %get-tuple-element.49), channel_id=1, source_target_pairs={{0,32},{32,64},{64,96},{96,128},{128,160},{160,192},{192,224},{1,3... | collective-permute-start | bytes 196616 | tf_op jit(solution)/shard_map/ppermute | solution.py:30
  56.6 1.3 collective-permute-start.5
  58.0 5.0 %collective-permute-done.5 = f32[1,16,1024]{2,0,1:T(1,128)S(1)} collective-permute-done((f32[1,16,1024]{2,0,1:T(1,128)S(1)}, f32[1,16,1024]{2,0,1:T(1,128)S(1)}, u32[]{:S(2)}, u32[]{:S(2)}) %collective-permute-start.5) | collective-permute-done | bytes 65568 | tf_op jit(solution)/shard_map/ppermute | solution.py:31
  63.0 1.1 fusion.45
  64.0 1.4 pad_maximum_fusion.16
  65.4 0.7 broadcast_in_dim.283
  66.1 13.0 %all-to-all-start.1 = ((f32[256,1,2]{2,1,0:T(1,128)}), f32[256,1,2]{2,1,0:T(1,128)S(1)}, u32[]{:S(2)}, u32[]{:S(2)}) async-start(f32[256,1,2]{2,1,0:T(1,128)} %broadcast_in_dim.283), calls=%async_computation.1 | async-start | bytes 262144 | tf_op jit(solution)/shard_map/all_to_all | solution.py:130
  79.1 3.5 %collective-permute-start.6 = (f32[8,1,1024]{2,0,1:T(8,128)S(1)}, f32[8,1,1024]{2,0,1:T(8,128)S(1)}, u32[]{:S(2)}, u32[]{:S(2)}) collective-permute-start(f32[8,1,1024]{2,0,1:T(8,128)S(1)} %get-tuple-element.46), channel_id=1, source_target_pairs={{0,1},{1,2},{2,3},{3,4},{4,5},{5,6},{6,7},{7,8},{8,9},{9,10},{10,1... | collective-permute-start | bytes 98312 | tf_op jit(solution)/shard_map/ppermute | solution.py:30
  82.7 2.1 %collective-permute-start.7 = (f32[8,1,1024]{2,0,1:T(8,128)S(1)}, f32[8,1,1024]{2,0,1:T(8,128)S(1)}, u32[]{:S(2)}, u32[]{:S(2)}) collective-permute-start(f32[8,1,1024]{2,0,1:T(8,128)S(1)} %get-tuple-element.47), channel_id=1, source_target_pairs={{1,0},{2,1},{3,2},{4,3},{5,4},{6,5},{7,6},{8,7},{9,8},{10,9},{11,1... | collective-permute-start | bytes 98312 | tf_op jit(solution)/shard_map/ppermute | solution.py:31
  84.8 7.2 %all-to-all-done.1 = f32[256,1,2]{2,1,0:T(1,128)S(1)} async-done(((f32[256,1,2]{2,1,0:T(1,128)}), f32[256,1,2]{2,1,0:T(1,128)S(1)}, u32[]{:S(2)}, u32[]{:S(2)}) %all-to-all-start.1) | async-done | bytes 2080 | tf_op jit(solution)/shard_map/all_to_all | solution.py:130
  95.0 0.7 fusion.17
  95.8 0.9 fusion.6
  96.6 0.9 convolution_bitcast_fusion.9
  98.2 0.9 convolution_bitcast_fusion.8
  100.8 2.5 %collective-permute-start.8 = (f32[1,16,1024]{2,0,1:T(1,128)S(1)}, f32[1,16,1024]{2,0,1:T(1,128)S(1)}, u32[]{:S(2)}, u32[]{:S(2)}) collective-permute-start(f32[1,16,1024]{2,0,1:T(1,128)S(1)} %get-tuple-element.44), channel_id=1, source_target_pairs={{0,32},{32,64},{64,96},{96,128},{128,160},{160,192},{192,224},{1,3... | collective-permute-start | bytes 196616 | tf_op jit(solution)/shard_map/ppermute | solution.py:30
  103.3 1.3 collective-permute-start.9
  104.6 3.7 %collective-permute-done.9 = f32[1,16,1024]{2,0,1:T(1,128)S(1)} collective-permute-done((f32[1,16,1024]{2,0,1:T(1,128)S(1)}, f32[1,16,1024]{2,0,1:T(1,128)S(1)}, u32[]{:S(2)}, u32[]{:S(2)}) %collective-permute-start.9) | collective-permute-done | bytes 65568 | tf_op jit(solution)/shard_map/ppermute | solution.py:31
  108.3 1.1 fusion.46
  109.4 1.9 %pad_maximum_fusion.17 = f32[3]{0:T(128)S(1)} fusion(f32[1]{0:T(128)} %bitcast.72, f32[1]{0:T(128)} %bitcast.71, f32[1]{0:T(128)} %bitcast.52), kind=kLoop, calls=%fused_computation.254 | loop fusion | flops 6 | bytes 24 | tf_op jit(solution)/shard_map/stack | solution.py:247
  111.3 0.7 broadcast_in_dim.284
  112.0 9.3 %all-to-all-start.2 = ((f32[256,1,3]{2,1,0:T(1,128)}), f32[256,1,3]{2,1,0:T(1,128)S(1)}, u32[]{:S(2)}, u32[]{:S(2)}) async-start(f32[256,1,3]{2,1,0:T(1,128)} %broadcast_in_dim.284), calls=%async_computation.2 | async-start | bytes 262144 | tf_op jit(solution)/shard_map/all_to_all | solution.py:130
  121.4 3.5 %collective-permute-start.10 = (f32[8,1,1024]{2,0,1:T(8,128)S(1)}, f32[8,1,1024]{2,0,1:T(8,128)S(1)}, u32[]{:S(2)}, u32[]{:S(2)}) collective-permute-start(f32[8,1,1024]{2,0,1:T(8,128)S(1)} %get-tuple-element.41), channel_id=1, source_target_pairs={{0,1},{1,2},{2,3},{3,4},{4,5},{5,6},{6,7},{7,8},{8,9},{9,10},{10,1... | collective-permute-start | bytes 98312 | tf_op jit(solution)/shard_map/ppermute | solution.py:30
  124.9 2.2 %collective-permute-start.11 = (f32[8,1,1024]{2,0,1:T(8,128)S(1)}, f32[8,1,1024]{2,0,1:T(8,128)S(1)}, u32[]{:S(2)}, u32[]{:S(2)}) collective-permute-start(f32[8,1,1024]{2,0,1:T(8,128)S(1)} %get-tuple-element.42), channel_id=1, source_target_pairs={{1,0},{2,1},{3,2},{4,3},{5,4},{6,5},{7,6},{8,7},{9,8},{10,9},{11,1... | collective-permute-start | bytes 98312 | tf_op jit(solution)/shard_map/ppermute | solution.py:31
  127.1 7.2 %all-to-all-done.2 = f32[256,1,3]{2,1,0:T(1,128)S(1)} async-done(((f32[256,1,3]{2,1,0:T(1,128)}), f32[256,1,3]{2,1,0:T(1,128)S(1)}, u32[]{:S(2)}, u32[]{:S(2)}) %all-to-all-start.2) | async-done | bytes 3104 | tf_op jit(solution)/shard_map/all_to_all | solution.py:130
  139.5 0.8 fusion.19
  140.3 0.9 fusion.10
  141.7 0.9 convolution_bitcast_fusion.3
  143.3 0.9 convolution_bitcast_fusion.2
  144.5 0.7 fusion.13
  145.3 2.5 %collective-permute-start.12 = (f32[1,16,1024]{2,0,1:T(1,128)S(1)}, f32[1,16,1024]{2,0,1:T(1,128)S(1)}, u32[]{:S(2)}, u32[]{:S(2)}) collective-permute-start(f32[1,16,1024]{2,0,1:T(1,128)S(1)} %get-tuple-element.39), channel_id=1, source_target_pairs={{0,32},{32,64},{64,96},{96,128},{128,160},{160,192},{192,224},{1,3... | collective-permute-start | bytes 196616 | tf_op jit(solution)/shard_map/ppermute | solution.py:30
  147.8 1.3 collective-permute-start.13
  149.2 3.7 %collective-permute-done.13 = f32[1,16,1024]{2,0,1:T(1,128)S(1)} collective-permute-done((f32[1,16,1024]{2,0,1:T(1,128)S(1)}, f32[1,16,1024]{2,0,1:T(1,128)S(1)}, u32[]{:S(2)}, u32[]{:S(2)}) %collective-permute-start.13) | collective-permute-done | bytes 65568 | tf_op jit(solution)/shard_map/ppermute | solution.py:31
  152.9 1.1 fusion.48
  153.9 2.0 %pad_maximum_fusion.18 = f32[3]{0:T(128)S(1)} fusion(f32[1]{0:T(128)} %bitcast.96, f32[1]{0:T(128)} %bitcast.95, f32[1]{0:T(128)} %bitcast.76), kind=kLoop, calls=%fused_computation.255 | loop fusion | flops 6 | bytes 24 | tf_op jit(solution)/shard_map/stack | solution.py:247
  155.9 0.7 broadcast_in_dim.285
  156.6 9.0 %all-to-all-start.3 = ((f32[256,1,3]{2,1,0:T(1,128)}), f32[256,1,3]{2,1,0:T(1,128)S(1)}, u32[]{:S(2)}, u32[]{:S(2)}) async-start(f32[256,1,3]{2,1,0:T(1,128)} %broadcast_in_dim.285), calls=%async_computation.3 | async-start | bytes 262144 | tf_op jit(solution)/shard_map/all_to_all | solution.py:130
  165.6 3.5 %collective-permute-start.14 = (f32[8,1,1024]{2,0,1:T(8,128)S(1)}, f32[8,1,1024]{2,0,1:T(8,128)S(1)}, u32[]{:S(2)}, u32[]{:S(2)}) collective-permute-start(f32[8,1,1024]{2,0,1:T(8,128)S(1)} %get-tuple-element.36), channel_id=1, source_target_pairs={{0,1},{1,2},{2,3},{3,4},{4,5},{5,6},{6,7},{7,8},{8,9},{9,10},{10,1... | collective-permute-start | bytes 98312 | tf_op jit(solution)/shard_map/ppermute | solution.py:30
  169.2 1.9 %collective-permute-start.15 = (f32[8,1,1024]{2,0,1:T(8,128)S(1)}, f32[8,1,1024]{2,0,1:T(8,128)S(1)}, u32[]{:S(2)}, u32[]{:S(2)}) collective-permute-start(f32[8,1,1024]{2,0,1:T(8,128)S(1)} %get-tuple-element.37), channel_id=1, source_target_pairs={{1,0},{2,1},{3,2},{4,3},{5,4},{6,5},{7,6},{8,7},{9,8},{10,9},{11,1... | collective-permute-start | bytes 98312 | tf_op jit(solution)/shard_map/ppermute | solution.py:31
  171.1 7.4 %all-to-all-done.3 = f32[256,1,3]{2,1,0:T(1,128)S(1)} async-done(((f32[256,1,3]{2,1,0:T(1,128)}), f32[256,1,3]{2,1,0:T(1,128)S(1)}, u32[]{:S(2)}, u32[]{:S(2)}) %all-to-all-start.3) | async-done | bytes 3104 | tf_op jit(solution)/shard_map/all_to_all | solution.py:130
  183.5 1.1 copy.374
  184.6 1.1 copy.373
  (96 shorter events, 18.2 us)
Async XLA Ops:
  0.6 18.3 %copy-start.4 = (f32[8]{0:T(128)S(1)}, f32[8]{0:T(128)}, u32[]{:S(2)}) copy-start(f32[8]{0:T(128)} %constant.206.clone) | copy-start | bytes 100
  6.9 16.2 %all-to-all-start = ((f32[32,8,8]{1,2,0:T(8,128)}), f32[32,8,8]{1,2,0:T(8,128)S(1)}, u32[]{:S(2)}, u32[]{:S(2)}) async-start(f32[32,8,8]{1,2,0:T(8,128)} %copy.331), calls=%async_computation | async-start | bytes 262144 | tf_op jit(solution)/shard_map/all_to_all | solution.py:183
  17.9 5.4 %copy-start.5 = (f32[8]{0:T(128)S(1)}, f32[8]{0:T(128)}, u32[]{:S(2)}) copy-start(f32[8]{0:T(128)} %constant.205.clone) | copy-start | bytes 100
  19.5 5.7 %copy-start.1 = (f32[3,8,16,1024]{3,2,1,0:T(8,128)S(1)}, f32[3,8,16,1024]{3,2,1,0:T(8,128)}, u32[]{:S(2)}) copy-start(f32[3,8,16,1024]{3,2,1,0:T(8,128)} %param.11) | copy-start | bytes 4718596
  25.2 0.7 copy-start.3
  25.9 1.8 copy-start.2
  28.8 4.9 %collective-permute-start = (f32[1,16,1024]{2,0,1:T(1,128)S(1)}, f32[1,16,1024]{2,0,1:T(1,128)S(1)}, u32[]{:S(2)}, u32[]{:S(2)}) collective-permute-start(f32[1,16,1024]{2,0,1:T(1,128)S(1)} %get-tuple-element.53), channel_id=1, source_target_pairs={{0,32},{32,64},{64,96},{96,128},{128,160},{160,192},{192,224},{1,3... | collective-permute-start | bytes 196616 | tf_op jit(solution)/shard_map/ppermute | solution.py:30
  32.3 5.2 %collective-permute-start.1 = (f32[1,16,1024]{2,0,1:T(1,128)S(1)}, f32[1,16,1024]{2,0,1:T(1,128)S(1)}, u32[]{:S(2)}, u32[]{:S(2)}) collective-permute-start(f32[1,16,1024]{2,0,1:T(1,128)S(1)} %get-tuple-element.54), channel_id=1, source_target_pairs={{32,0},{64,32},{96,64},{128,96},{160,128},{192,160},{224,192},{33,... | collective-permute-start | bytes 196616 | tf_op jit(solution)/shard_map/ppermute | solution.py:31
  37.8 6.5 %collective-permute-start.2 = (f32[8,1,1024]{2,0,1:T(8,128)S(1)}, f32[8,1,1024]{2,0,1:T(8,128)S(1)}, u32[]{:S(2)}, u32[]{:S(2)}) collective-permute-start(f32[8,1,1024]{2,0,1:T(8,128)S(1)} %get-tuple-element.51), channel_id=1, source_target_pairs={{0,1},{1,2},{2,3},{3,4},{4,5},{5,6},{6,7},{7,8},{8,9},{9,10},{10,1... | collective-permute-start | bytes 98312 | tf_op jit(solution)/shard_map/ppermute | solution.py:30
  41.6 5.2 %collective-permute-start.3 = (f32[8,1,1024]{2,0,1:T(8,128)S(1)}, f32[8,1,1024]{2,0,1:T(8,128)S(1)}, u32[]{:S(2)}, u32[]{:S(2)}) collective-permute-start(f32[8,1,1024]{2,0,1:T(8,128)S(1)} %get-tuple-element.52), channel_id=1, source_target_pairs={{1,0},{2,1},{3,2},{4,3},{5,4},{6,5},{7,6},{8,7},{9,8},{10,9},{11,1... | collective-permute-start | bytes 98312 | tf_op jit(solution)/shard_map/ppermute | solution.py:31
  47.0 1.6 copy-start
  53.1 4.9 %collective-permute-start.4 = (f32[1,16,1024]{2,0,1:T(1,128)S(1)}, f32[1,16,1024]{2,0,1:T(1,128)S(1)}, u32[]{:S(2)}, u32[]{:S(2)}) collective-permute-start(f32[1,16,1024]{2,0,1:T(1,128)S(1)} %get-tuple-element.49), channel_id=1, source_target_pairs={{0,32},{32,64},{64,96},{96,128},{128,160},{160,192},{192,224},{1,3... | collective-permute-start | bytes 196616 | tf_op jit(solution)/shard_map/ppermute | solution.py:30
  56.6 6.3 %collective-permute-start.5 = (f32[1,16,1024]{2,0,1:T(1,128)S(1)}, f32[1,16,1024]{2,0,1:T(1,128)S(1)}, u32[]{:S(2)}, u32[]{:S(2)}) collective-permute-start(f32[1,16,1024]{2,0,1:T(1,128)S(1)} %get-tuple-element.50), channel_id=1, source_target_pairs={{32,0},{64,32},{96,64},{128,96},{160,128},{192,160},{224,192},{33,... | collective-permute-start | bytes 196616 | tf_op jit(solution)/shard_map/ppermute | solution.py:31
  66.1 25.9 %all-to-all-start.1 = ((f32[256,1,2]{2,1,0:T(1,128)}), f32[256,1,2]{2,1,0:T(1,128)S(1)}, u32[]{:S(2)}, u32[]{:S(2)}) async-start(f32[256,1,2]{2,1,0:T(1,128)} %broadcast_in_dim.283), calls=%async_computation.1 | async-start | bytes 262144 | tf_op jit(solution)/shard_map/all_to_all | solution.py:130
  79.1 15.1 %collective-permute-start.6 = (f32[8,1,1024]{2,0,1:T(8,128)S(1)}, f32[8,1,1024]{2,0,1:T(8,128)S(1)}, u32[]{:S(2)}, u32[]{:S(2)}) collective-permute-start(f32[8,1,1024]{2,0,1:T(8,128)S(1)} %get-tuple-element.46), channel_id=1, source_target_pairs={{0,1},{1,2},{2,3},{3,4},{4,5},{5,6},{6,7},{7,8},{8,9},{9,10},{10,1... | collective-permute-start | bytes 98312 | tf_op jit(solution)/shard_map/ppermute | solution.py:30
  82.7 11.6 %collective-permute-start.7 = (f32[8,1,1024]{2,0,1:T(8,128)S(1)}, f32[8,1,1024]{2,0,1:T(8,128)S(1)}, u32[]{:S(2)}, u32[]{:S(2)}) collective-permute-start(f32[8,1,1024]{2,0,1:T(8,128)S(1)} %get-tuple-element.47), channel_id=1, source_target_pairs={{1,0},{2,1},{3,2},{4,3},{5,4},{6,5},{7,6},{8,7},{9,8},{10,9},{11,1... | collective-permute-start | bytes 98312 | tf_op jit(solution)/shard_map/ppermute | solution.py:31
  100.8 3.8 %collective-permute-start.8 = (f32[1,16,1024]{2,0,1:T(1,128)S(1)}, f32[1,16,1024]{2,0,1:T(1,128)S(1)}, u32[]{:S(2)}, u32[]{:S(2)}) collective-permute-start(f32[1,16,1024]{2,0,1:T(1,128)S(1)} %get-tuple-element.44), channel_id=1, source_target_pairs={{0,32},{32,64},{64,96},{96,128},{128,160},{160,192},{192,224},{1,3... | collective-permute-start | bytes 196616 | tf_op jit(solution)/shard_map/ppermute | solution.py:30
  103.3 5.0 %collective-permute-start.9 = (f32[1,16,1024]{2,0,1:T(1,128)S(1)}, f32[1,16,1024]{2,0,1:T(1,128)S(1)}, u32[]{:S(2)}, u32[]{:S(2)}) collective-permute-start(f32[1,16,1024]{2,0,1:T(1,128)S(1)} %get-tuple-element.45), channel_id=1, source_target_pairs={{32,0},{64,32},{96,64},{128,96},{160,128},{192,160},{224,192},{33,... | collective-permute-start | bytes 196616 | tf_op jit(solution)/shard_map/ppermute | solution.py:31
  112.0 22.3 %all-to-all-start.2 = ((f32[256,1,3]{2,1,0:T(1,128)}), f32[256,1,3]{2,1,0:T(1,128)S(1)}, u32[]{:S(2)}, u32[]{:S(2)}) async-start(f32[256,1,3]{2,1,0:T(1,128)} %broadcast_in_dim.284), calls=%async_computation.2 | async-start | bytes 262144 | tf_op jit(solution)/shard_map/all_to_all | solution.py:130
  121.4 17.6 %collective-permute-start.10 = (f32[8,1,1024]{2,0,1:T(8,128)S(1)}, f32[8,1,1024]{2,0,1:T(8,128)S(1)}, u32[]{:S(2)}, u32[]{:S(2)}) collective-permute-start(f32[8,1,1024]{2,0,1:T(8,128)S(1)} %get-tuple-element.41), channel_id=1, source_target_pairs={{0,1},{1,2},{2,3},{3,4},{4,5},{5,6},{6,7},{7,8},{8,9},{9,10},{10,1... | collective-permute-start | bytes 98312 | tf_op jit(solution)/shard_map/ppermute | solution.py:30
  124.9 14.0 %collective-permute-start.11 = (f32[8,1,1024]{2,0,1:T(8,128)S(1)}, f32[8,1,1024]{2,0,1:T(8,128)S(1)}, u32[]{:S(2)}, u32[]{:S(2)}) collective-permute-start(f32[8,1,1024]{2,0,1:T(8,128)S(1)} %get-tuple-element.42), channel_id=1, source_target_pairs={{1,0},{2,1},{3,2},{4,3},{5,4},{6,5},{7,6},{8,7},{9,8},{10,9},{11,1... | collective-permute-start | bytes 98312 | tf_op jit(solution)/shard_map/ppermute | solution.py:31
  145.3 3.9 %collective-permute-start.12 = (f32[1,16,1024]{2,0,1:T(1,128)S(1)}, f32[1,16,1024]{2,0,1:T(1,128)S(1)}, u32[]{:S(2)}, u32[]{:S(2)}) collective-permute-start(f32[1,16,1024]{2,0,1:T(1,128)S(1)} %get-tuple-element.39), channel_id=1, source_target_pairs={{0,32},{32,64},{64,96},{96,128},{128,160},{160,192},{192,224},{1,3... | collective-permute-start | bytes 196616 | tf_op jit(solution)/shard_map/ppermute | solution.py:30
  147.8 5.0 %collective-permute-start.13 = (f32[1,16,1024]{2,0,1:T(1,128)S(1)}, f32[1,16,1024]{2,0,1:T(1,128)S(1)}, u32[]{:S(2)}, u32[]{:S(2)}) collective-permute-start(f32[1,16,1024]{2,0,1:T(1,128)S(1)} %get-tuple-element.40), channel_id=1, source_target_pairs={{32,0},{64,32},{96,64},{128,96},{160,128},{192,160},{224,192},{33,... | collective-permute-start | bytes 196616 | tf_op jit(solution)/shard_map/ppermute | solution.py:31
  156.6 21.9 %all-to-all-start.3 = ((f32[256,1,3]{2,1,0:T(1,128)}), f32[256,1,3]{2,1,0:T(1,128)S(1)}, u32[]{:S(2)}, u32[]{:S(2)}) async-start(f32[256,1,3]{2,1,0:T(1,128)} %broadcast_in_dim.285), calls=%async_computation.3 | async-start | bytes 262144 | tf_op jit(solution)/shard_map/all_to_all | solution.py:130
  165.6 17.0 %collective-permute-start.14 = (f32[8,1,1024]{2,0,1:T(8,128)S(1)}, f32[8,1,1024]{2,0,1:T(8,128)S(1)}, u32[]{:S(2)}, u32[]{:S(2)}) collective-permute-start(f32[8,1,1024]{2,0,1:T(8,128)S(1)} %get-tuple-element.36), channel_id=1, source_target_pairs={{0,1},{1,2},{2,3},{3,4},{4,5},{5,6},{6,7},{7,8},{8,9},{9,10},{10,1... | collective-permute-start | bytes 98312 | tf_op jit(solution)/shard_map/ppermute | solution.py:30
  169.2 13.5 %collective-permute-start.15 = (f32[8,1,1024]{2,0,1:T(8,128)S(1)}, f32[8,1,1024]{2,0,1:T(8,128)S(1)}, u32[]{:S(2)}, u32[]{:S(2)}) collective-permute-start(f32[8,1,1024]{2,0,1:T(8,128)S(1)} %get-tuple-element.37), channel_id=1, source_target_pairs={{1,0},{2,1},{3,2},{4,3},{5,4},{6,5},{7,6},{8,7},{9,8},{10,9},{11,1... | collective-permute-start | bytes 98312 | tf_op jit(solution)/shard_map/ppermute | solution.py:31
where the time goes:
time: 187 us; the launch traced here: 186 us
  starting transfers between devices  79.9 us (43%)
  waiting for transfers between devices  44.3 us (24%)
  other arithmetic  20.8 us (11%)
  matrix products  18 us (10%)
  local copies, waits for them, and re-layouts  13 us (7%)
  between operations  9.69 us (5%)
    all_to_all x3, starting transfers between devices, mesh_sum(): gathered = lax.all_to_all(spread, axes, 0, 0, tiled=True)  31.2 us
    ppermute x8, starting transfers between devices, with_halo(): before = lax.ppermute(last, axis, up)  26.5 us
    all_to_all x3, waiting for transfers between devices, mesh_sum(): gathered = lax.all_to_all(spread, axes, 0, 0, tiled=True)  21.8 us
    ppermute x8, waiting for transfers between devices, with_halo(): after = lax.ppermute(first, axis, down)  18.8 us
    ppermute x8, starting transfers between devices, with_halo(): after = lax.ppermute(first, axis, down)  13.5 us
    all_to_all x1, starting transfers between devices, project_points(): lax.all_to_all(outgoing, 'span', split_axis=0, concat_axis=0, tiled=True)  8.58 us
    dot_general x7, matrix products, derive(): result = jnp.einsum('ib,xybz->xyiz', matrix, blocks, precision=highest)  6 us
    dot_general x7, matrix products, derive(): result = jnp.einsum('ia,xayz->xiyz', matrix, blocks, precision=highest)  5.57 us
  transfers between devices with their start and end apart: 20, of which 9 were waited for; matrix products, arithmetic and copies ran while one was open for 4% of the time, Pallas kernels for 0%

commit v1 on v0

--- a/solution.py
+++ b/solution.py
@@ -233,7 +233,9 @@
     residual = rhs
     direction = rhs
     local = local_operator(residual, weight3, metric, diffmat)
-    sums = mesh_sum(jnp.stack([weighted(residual, residual), jnp.sum(residual * local)]))
+    partial = jnp.stack([weighted(residual, residual), jnp.sum(residual * local)])
+    local, partial = lax.optimization_barrier((local, partial))
+    sums = mesh_sum(partial)
     norm_now, curvature = sums[0], sums[1]
     searched = assemble(local)
     step_len = norm_now / curvature
@@ -243,15 +245,15 @@
         if iteration == ITERS:
             break
         local = local_operator(residual, weight3, metric, diffmat)
-        sums = mesh_sum(
-            jnp.stack(
-                [
-                    weighted(residual, residual),
-                    jnp.sum(residual * local),
-                    weighted(residual, searched),
-                ]
-            )
+        partial = jnp.stack(
+            [
+                weighted(residual, residual),
+                jnp.sum(residual * local),
+                weighted(residual, searched),
+            ]
         )
+        local, partial = lax.optimization_barrier((local, partial))
+        sums = mesh_sum(partial)
         applied = assemble(local)
         norm_next, own_curvature, cross = sums[0], sums[1], sums[2]
         ratio = norm_next / norm_now

time: 187 us -> 195 us (1.043)
  blocking collectives: 0 us -> 76.1 us
  starting transfers between devices: 79.9 us -> 46.2 us
  waiting for transfers between devices: 44.3 us -> 11.2 us
  other arithmetic: 20.8 us -> 18.4 us
  matrix products: 18 us -> 20.2 us
    all_to_all x0 -> x3, blocking collectives: none -> 76.1 us  [mesh_sum(): gathered = lax.all_to_all(spread, axes, 0, 0, tiled=True)]
    all_to_all x3 -> x0, starting transfers between devices: 31.2 us -> none  [mesh_sum(): gathered = lax.all_to_all(spread, axes, 0, 0, tiled=True)]
    all_to_all x3 -> x0, waiting for transfers between devices: 21.8 us -> none  [mesh_sum(): gathered = lax.all_to_all(spread, axes, 0, 0, tiled=True)]
    ppermute x8, waiting for transfers between devices: 18.8 us -> 7.57 us  [with_halo(): after = lax.ppermute(first, axis, down)]
    reduce_sum x3 -> x0, other arithmetic: 3.2 us -> none  [weighted(): return jnp.sum(first_vec * second_vec * inv_mult)]
    ppermute x8, starting transfers between devices: 26.5 us -> 24.2 us  [with_halo(): before = lax.ppermute(last, axis, up)]
    dot_general x7, matrix products: 5.57 us -> 7.72 us  [derive(): result = jnp.einsum('ia,xayz->xiyz', matrix, blocks, precision=highest)]
    broadcast_in_dim x3, local copies, waits for them, and re-layouts: 2.18 us -> 0.21 us  [mesh_sum(): spread = jnp.broadcast_to(values[None], (count,) + values.shape)]
  transfers between devices with their start and end apart: 20 -> 17, of which waited for: 9 -> 4; matrix products, arithmetic and copies ran while one was open for 4% -> 4% of each run, Pallas kernels for 0% -> 0%
where the time goes in v1:
time: 195 us; the launch traced here: 193 us
  blocking collectives  76.1 us (39%)
  starting transfers between devices  46.2 us (24%)
  matrix products  20.2 us (10%)
  other arithmetic  18.4 us (9%)
  waiting for transfers between devices  11.2 us (6%)
  local copies, waits for them, and re-layouts  11.1 us (6%)
  between operations  9.9 us (5%)
    all_to_all x3, blocking collectives, mesh_sum(): gathered = lax.all_to_all(spread, axes, 0, 0, tiled=True)  76.1 us
    ppermute x8, starting transfers between devices, with_halo(): before = lax.ppermute(last, axis, up)  24.2 us
    ppermute x8, starting transfers between devices, with_halo(): after = lax.ppermute(first, axis, down)  13.5 us
    all_to_all x1, starting transfers between devices, project_points(): lax.all_to_all(outgoing, 'span', split_axis=0, concat_axis=0, tiled=True)  8.58 us
    dot_general x7, matrix products, derive(): result = jnp.einsum('ia,xayz->xiyz', matrix, blocks, precision=highest)  7.72 us
    ppermute x8, waiting for transfers between devices, with_halo(): after = lax.ppermute(first, axis, down)  7.57 us
    dot_general x7, matrix products, derive(): result = jnp.einsum('ib,xybz->xyiz', matrix, blocks, precision=highest)  6 us
    dot_general x7, matrix products, derive(): jnp.einsum('xyzc,ic->xyzi', blocks, tiled_matrix, precision=highest)  4.79 us
  transfers between devices with their start and end apart: 17, of which 4 were waited for; matrix products, arithmetic and copies ran while one was open for 4% of the time, Pallas kernels for 0%

profile of v1, /device:TPU:1, one launch (start us, length us, event | category | flops | bytes accessed | tf_op | source)
XLA Modules:
  0.0 193.0 jit_solution(7122902628977607795)
XLA Ops:
  0.6 0.7 convert_bitcast_fusion.1
  1.3 0.9 convert_reduce_fusion
  2.2 0.7 convert_bitcast_fusion
  3.0 0.8 select_reduce_fusion
  3.8 0.7 broadcast_multiply_fusion.6
  4.5 0.7 maximum_bitcast_fusion
  5.3 0.9 scatter_custom_fusion
  6.2 0.8 copy.332
  6.9 8.6 %all-to-all-start = ((f32[32,8,8]{1,2,0:T(8,128)}), f32[32,8,8]{1,2,0:T(8,128)S(1)}, u32[]{:S(2)}, u32[]{:S(2)}) async-start(f32[32,8,8]{1,2,0:T(8,128)} %copy.332), calls=%async_computation | async-start | bytes 262144 | tf_op jit(solution)/shard_map/all_to_all | solution.py:183
  15.6 0.8 broadcast_multiply_fusion.4
  16.4 0.7 tile.12
  17.2 0.7 broadcast_multiply_fusion.5
  18.0 0.9 broadcast_multiply_fusion
  19.5 3.6 %all-to-all-done = f32[32,8,8]{1,2,0:T(8,128)S(1)} async-done(((f32[32,8,8]{1,2,0:T(8,128)}), f32[32,8,8]{1,2,0:T(8,128)S(1)}, u32[]{:S(2)}, u32[]{:S(2)}) %all-to-all-start) | async-done | bytes 8224 | tf_op jit(solution)/shard_map/all_to_all | solution.py:183
  23.5 1.7 fusion.20
  25.9 0.7 convolution_bitcast_fusion.19
  26.9 0.8 convolution_bitcast_fusion.18
  27.7 0.9 fusion.1
  28.8 3.5 %collective-permute-start = (f32[1,16,1024]{2,0,1:T(1,128)S(1)}, f32[1,16,1024]{2,0,1:T(1,128)S(1)}, u32[]{:S(2)}, u32[]{:S(2)}) collective-permute-start(f32[1,16,1024]{2,0,1:T(1,128)S(1)} %get-tuple-element.62), channel_id=1, source_target_pairs={{0,32},{32,64},{64,96},{96,128},{128,160},{160,192},{192,224},{1,3... | collective-permute-start | bytes 196616 | tf_op jit(solution)/shard_map/ppermute | solution.py:30
  32.3 1.3 collective-permute-start.1
  33.6 3.9 %collective-permute-done.1 = f32[1,16,1024]{2,0,1:T(1,128)S(1)} collective-permute-done((f32[1,16,1024]{2,0,1:T(1,128)S(1)}, f32[1,16,1024]{2,0,1:T(1,128)S(1)}, u32[]{:S(2)}, u32[]{:S(2)}) %collective-permute-start.1) | collective-permute-done | bytes 65568 | tf_op jit(solution)/shard_map/ppermute | solution.py:31
  37.8 3.8 %collective-permute-start.2 = (f32[8,1,1024]{2,0,1:T(8,128)S(1)}, f32[8,1,1024]{2,0,1:T(8,128)S(1)}, u32[]{:S(2)}, u32[]{:S(2)}) collective-permute-start(f32[8,1,1024]{2,0,1:T(8,128)S(1)} %get-tuple-element.60), channel_id=1, source_target_pairs={{0,1},{1,2},{2,3},{3,4},{4,5},{5,6},{6,7},{7,8},{8,9},{9,10},{10,1... | collective-permute-start | bytes 98312 | tf_op jit(solution)/shard_map/ppermute | solution.py:30
  41.6 2.1 %collective-permute-start.3 = (f32[8,1,1024]{2,0,1:T(8,128)S(1)}, f32[8,1,1024]{2,0,1:T(8,128)S(1)}, u32[]{:S(2)}, u32[]{:S(2)}) collective-permute-start(f32[8,1,1024]{2,0,1:T(8,128)S(1)} %get-tuple-element.61), channel_id=1, source_target_pairs={{1,0},{2,1},{3,2},{4,3},{5,4},{6,5},{7,6},{8,7},{9,8},{10,9},{11,1... | collective-permute-start | bytes 98312 | tf_op jit(solution)/shard_map/ppermute | solution.py:31
  44.3 2.5 %collective-permute-done.3 = f32[8,1,1024]{2,0,1:T(8,128)S(1)} collective-permute-done((f32[8,1,1024]{2,0,1:T(8,128)S(1)}, f32[8,1,1024]{2,0,1:T(8,128)S(1)}, u32[]{:S(2)}, u32[]{:S(2)}) %collective-permute-start.3) | collective-permute-done | bytes 32800 | tf_op jit(solution)/shard_map/ppermute | solution.py:31
  47.3 0.9 convolution_bitcast_fusion.15
  48.5 0.9 fusion.2
  49.8 0.9 convolution_bitcast_fusion.14
  51.0 0.7 fusion.15
  52.3 1.4 fusion.45
  53.7 1.4 pad_maximum_fusion.16
  55.1 3.5 %collective-permute-start.4 = (f32[1,16,1024]{2,0,1:T(1,128)S(1)}, f32[1,16,1024]{2,0,1:T(1,128)S(1)}, u32[]{:S(2)}, u32[]{:S(2)}) collective-permute-start(f32[1,16,1024]{2,0,1:T(1,128)S(1)} %get-tuple-element.58), channel_id=1, source_target_pairs={{0,32},{32,64},{64,96},{96,128},{128,160},{160,192},{192,224},{1,3... | collective-permute-start | bytes 196616 | tf_op jit(solution)/shard_map/ppermute | solution.py:30
  58.7 1.3 collective-permute-start.5
  60.1 28.9 %all_to_all.23 = f32[256,1,2]{2,1,0:T(1,128)S(1)} all-to-all(f32[256,1,2]{2,1,0:T(1,128)S(1)} %broadcast_in_dim.283), channel_id=1, replica_groups=mesh['stream'=8,'span'=32] {'stream','span'}, dimensions={0} | all-to-all | bytes 4096 | tf_op jit(solution)/shard_map/all_to_all | solution.py:130
  89.5 2.6 %collective-permute-start.6 = (f32[8,1,1024]{2,0,1:T(8,128)S(1)}, f32[8,1,1024]{2,0,1:T(8,128)S(1)}, u32[]{:S(2)}, u32[]{:S(2)}) collective-permute-start(f32[8,1,1024]{2,0,1:T(8,128)S(1)} %get-tuple-element.56), channel_id=1, source_target_pairs={{0,1},{1,2},{2,3},{3,4},{4,5},{5,6},{6,7},{7,8},{8,9},{9,10},{10,1... | collective-permute-start | bytes 98312 | tf_op jit(solution)/shard_map/ppermute | solution.py:30
  92.1 2.1 %collective-permute-start.7 = (f32[8,1,1024]{2,0,1:T(8,128)S(1)}, f32[8,1,1024]{2,0,1:T(8,128)S(1)}, u32[]{:S(2)}, u32[]{:S(2)}) collective-permute-start(f32[8,1,1024]{2,0,1:T(8,128)S(1)} %get-tuple-element.57), channel_id=1, source_target_pairs={{1,0},{2,1},{3,2},{4,3},{5,4},{6,5},{7,6},{8,7},{9,8},{10,9},{11,1... | collective-permute-start | bytes 98312 | tf_op jit(solution)/shard_map/ppermute | solution.py:31
  96.2 1.2 collective-permute-done.7
  97.5 0.6 multiply_subtract_fusion.1
  98.1 0.7 fusion.17
  98.9 0.9 fusion.6
  99.7 0.9 convolution_bitcast_fusion.9
  101.3 0.9 convolution_bitcast_fusion.8
  103.1 1.5 fusion.46
  104.6 2.0 %pad_maximum_fusion.17 = f32[3]{0:T(128)S(1)} fusion(f32[1]{0:T(128)} %bitcast.72, f32[1]{0:T(128)} %bitcast.71, f32[1]{0:T(128)} %bitcast.70), kind=kLoop, calls=%fused_computation.254 | loop fusion | flops 6 | bytes 24 | tf_op jit(solution)/shard_map/stack | solution.py:248
  106.7 2.7 %collective-permute-start.8 = (f32[1,16,1024]{2,0,1:T(1,128)S(1)}, f32[1,16,1024]{2,0,1:T(1,128)S(1)}, u32[]{:S(2)}, u32[]{:S(2)}) collective-permute-start(f32[1,16,1024]{2,0,1:T(1,128)S(1)} %get-tuple-element.54), channel_id=1, source_target_pairs={{0,32},{32,64},{64,96},{96,128},{128,160},{160,192},{192,224},{1,3... | collective-permute-start | bytes 196616 | tf_op jit(solution)/shard_map/ppermute | solution.py:30
  109.4 1.3 collective-permute-start.9
  110.8 24.0 %all_to_all.24 = f32[256,1,3]{2,1,0:T(1,128)S(1)} all-to-all(f32[256,1,3]{2,1,0:T(1,128)S(1)} %broadcast_in_dim.284), channel_id=1, replica_groups=mesh['stream'=8,'span'=32] {'stream','span'}, dimensions={0} | all-to-all | bytes 6144 | tf_op jit(solution)/shard_map/all_to_all | solution.py:130
  135.3 2.6 %collective-permute-start.10 = (f32[8,1,1024]{2,0,1:T(8,128)S(1)}, f32[8,1,1024]{2,0,1:T(8,128)S(1)}, u32[]{:S(2)}, u32[]{:S(2)}) collective-permute-start(f32[8,1,1024]{2,0,1:T(8,128)S(1)} %get-tuple-element.52), channel_id=1, source_target_pairs={{0,1},{1,2},{2,3},{3,4},{4,5},{5,6},{6,7},{7,8},{8,9},{9,10},{10,1... | collective-permute-start | bytes 98312 | tf_op jit(solution)/shard_map/ppermute | solution.py:30
  137.9 2.2 %collective-permute-start.11 = (f32[8,1,1024]{2,0,1:T(8,128)S(1)}, f32[8,1,1024]{2,0,1:T(8,128)S(1)}, u32[]{:S(2)}, u32[]{:S(2)}) collective-permute-start(f32[8,1,1024]{2,0,1:T(8,128)S(1)} %get-tuple-element.53), channel_id=1, source_target_pairs={{1,0},{2,1},{3,2},{4,3},{5,4},{6,5},{7,6},{8,7},{9,8},{10,9},{11,1... | collective-permute-start | bytes 98312 | tf_op jit(solution)/shard_map/ppermute | solution.py:31
  140.1 0.7 fusion.148
  145.3 0.8 fusion.19
  146.1 0.9 fusion.10
  147.5 0.9 convolution_bitcast_fusion.3
  149.1 0.9 convolution_bitcast_fusion.2
  150.3 1.4 fusion.48
  151.7 1.9 pad_maximum_fusion.18
  153.7 2.7 %collective-permute-start.12 = (f32[1,16,1024]{2,0,1:T(1,128)S(1)}, f32[1,16,1024]{2,0,1:T(1,128)S(1)}, u32[]{:S(2)}, u32[]{:S(2)}) collective-permute-start(f32[1,16,1024]{2,0,1:T(1,128)S(1)} %get-tuple-element.50), channel_id=1, source_target_pairs={{0,32},{32,64},{64,96},{96,128},{128,160},{160,192},{192,224},{1,3... | collective-permute-start | bytes 196616 | tf_op jit(solution)/shard_map/ppermute | solution.py:30
  156.5 1.3 collective-permute-start.13
  157.9 23.2 %all_to_all.25 = f32[256,1,3]{2,1,0:T(1,128)S(1)} all-to-all(f32[256,1,3]{2,1,0:T(1,128)S(1)} %broadcast_in_dim.285), channel_id=1, replica_groups=mesh['stream'=8,'span'=32] {'stream','span'}, dimensions={0} | all-to-all | bytes 6144 | tf_op jit(solution)/shard_map/all_to_all | solution.py:130
  181.7 2.6 %collective-permute-start.14 = (f32[8,1,1024]{2,0,1:T(8,128)S(1)}, f32[8,1,1024]{2,0,1:T(8,128)S(1)}, u32[]{:S(2)}, u32[]{:S(2)}) collective-permute-start(f32[8,1,1024]{2,0,1:T(8,128)S(1)} %get-tuple-element.48), channel_id=1, source_target_pairs={{0,1},{1,2},{2,3},{3,4},{4,5},{5,6},{6,7},{7,8},{8,9},{9,10},{10,1... | collective-permute-start | bytes 98312 | tf_op jit(solution)/shard_map/ppermute | solution.py:30
  184.3 1.9 collective-permute-start.15
  186.2 0.6 fusion.147
  190.2 0.7 fusion.42
  190.8 1.1 copy.374
  191.9 1.1 copy.373
  (93 shorter events, 11.9 us)
Async XLA Ops:
  0.6 18.3 %copy-start.4 = (f32[8]{0:T(128)S(1)}, f32[8]{0:T(128)}, u32[]{:S(2)}) copy-start(f32[8]{0:T(128)} %constant.206.clone) | copy-start | bytes 100
  6.9 16.2 %all-to-all-start = ((f32[32,8,8]{1,2,0:T(8,128)}), f32[32,8,8]{1,2,0:T(8,128)S(1)}, u32[]{:S(2)}, u32[]{:S(2)}) async-start(f32[32,8,8]{1,2,0:T(8,128)} %copy.332), calls=%async_computation | async-start | bytes 262144 | tf_op jit(solution)/shard_map/all_to_all | solution.py:183
  18.0 5.4 %copy-start.5 = (f32[8]{0:T(128)S(1)}, f32[8]{0:T(128)}, u32[]{:S(2)}) copy-start(f32[8]{0:T(128)} %constant.205.clone) | copy-start | bytes 100
  19.5 5.7 %copy-start.1 = (f32[3,8,16,1024]{3,2,1,0:T(8,128)S(1)}, f32[3,8,16,1024]{3,2,1,0:T(8,128)}, u32[]{:S(2)}) copy-start(f32[3,8,16,1024]{3,2,1,0:T(8,128)} %param.11) | copy-start | bytes 4718596
  25.2 0.7 copy-start.3
  25.9 1.8 copy-start.2
  28.8 4.9 %collective-permute-start = (f32[1,16,1024]{2,0,1:T(1,128)S(1)}, f32[1,16,1024]{2,0,1:T(1,128)S(1)}, u32[]{:S(2)}, u32[]{:S(2)}) collective-permute-start(f32[1,16,1024]{2,0,1:T(1,128)S(1)} %get-tuple-element.62), channel_id=1, source_target_pairs={{0,32},{32,64},{64,96},{96,128},{128,160},{160,192},{192,224},{1,3... | collective-permute-start | bytes 196616 | tf_op jit(solution)/shard_map/ppermute | solution.py:30
  32.3 5.2 %collective-permute-start.1 = (f32[1,16,1024]{2,0,1:T(1,128)S(1)}, f32[1,16,1024]{2,0,1:T(1,128)S(1)}, u32[]{:S(2)}, u32[]{:S(2)}) collective-permute-start(f32[1,16,1024]{2,0,1:T(1,128)S(1)} %get-tuple-element.63), channel_id=1, source_target_pairs={{32,0},{64,32},{96,64},{128,96},{160,128},{192,160},{224,192},{33,... | collective-permute-start | bytes 196616 | tf_op jit(solution)/shard_map/ppermute | solution.py:31
  37.8 6.5 %collective-permute-start.2 = (f32[8,1,1024]{2,0,1:T(8,128)S(1)}, f32[8,1,1024]{2,0,1:T(8,128)S(1)}, u32[]{:S(2)}, u32[]{:S(2)}) collective-permute-start(f32[8,1,1024]{2,0,1:T(8,128)S(1)} %get-tuple-element.60), channel_id=1, source_target_pairs={{0,1},{1,2},{2,3},{3,4},{4,5},{5,6},{6,7},{7,8},{8,9},{9,10},{10,1... | collective-permute-start | bytes 98312 | tf_op jit(solution)/shard_map/ppermute | solution.py:30
  41.6 5.2 %collective-permute-start.3 = (f32[8,1,1024]{2,0,1:T(8,128)S(1)}, f32[8,1,1024]{2,0,1:T(8,128)S(1)}, u32[]{:S(2)}, u32[]{:S(2)}) collective-permute-start(f32[8,1,1024]{2,0,1:T(8,128)S(1)} %get-tuple-element.61), channel_id=1, source_target_pairs={{1,0},{2,1},{3,2},{4,3},{5,4},{6,5},{7,6},{8,7},{9,8},{10,9},{11,1... | collective-permute-start | bytes 98312 | tf_op jit(solution)/shard_map/ppermute | solution.py:31
  47.0 1.6 copy-start
  55.1 34.1 %collective-permute-start.4 = (f32[1,16,1024]{2,0,1:T(1,128)S(1)}, f32[1,16,1024]{2,0,1:T(1,128)S(1)}, u32[]{:S(2)}, u32[]{:S(2)}) collective-permute-start(f32[1,16,1024]{2,0,1:T(1,128)S(1)} %get-tuple-element.58), channel_id=1, source_target_pairs={{0,32},{32,64},{64,96},{96,128},{128,160},{160,192},{192,224},{1,3... | collective-permute-start | bytes 196616 | tf_op jit(solution)/shard_map/ppermute | solution.py:30
  58.7 30.5 %collective-permute-start.5 = (f32[1,16,1024]{2,0,1:T(1,128)S(1)}, f32[1,16,1024]{2,0,1:T(1,128)S(1)}, u32[]{:S(2)}, u32[]{:S(2)}) collective-permute-start(f32[1,16,1024]{2,0,1:T(1,128)S(1)} %get-tuple-element.59), channel_id=1, source_target_pairs={{32,0},{64,32},{96,64},{128,96},{160,128},{192,160},{224,192},{33,... | collective-permute-start | bytes 196616 | tf_op jit(solution)/shard_map/ppermute | solution.py:31
  89.5 6.7 %collective-permute-start.6 = (f32[8,1,1024]{2,0,1:T(8,128)S(1)}, f32[8,1,1024]{2,0,1:T(8,128)S(1)}, u32[]{:S(2)}, u32[]{:S(2)}) collective-permute-start(f32[8,1,1024]{2,0,1:T(8,128)S(1)} %get-tuple-element.56), channel_id=1, source_target_pairs={{0,1},{1,2},{2,3},{3,4},{4,5},{5,6},{6,7},{7,8},{8,9},{9,10},{10,1... | collective-permute-start | bytes 98312 | tf_op jit(solution)/shard_map/ppermute | solution.py:30
  92.1 5.2 %collective-permute-start.7 = (f32[8,1,1024]{2,0,1:T(8,128)S(1)}, f32[8,1,1024]{2,0,1:T(8,128)S(1)}, u32[]{:S(2)}, u32[]{:S(2)}) collective-permute-start(f32[8,1,1024]{2,0,1:T(8,128)S(1)} %get-tuple-element.57), channel_id=1, source_target_pairs={{1,0},{2,1},{3,2},{4,3},{5,4},{6,5},{7,6},{8,7},{9,8},{10,9},{11,1... | collective-permute-start | bytes 98312 | tf_op jit(solution)/shard_map/ppermute | solution.py:31
  106.7 28.4 %collective-permute-start.8 = (f32[1,16,1024]{2,0,1:T(1,128)S(1)}, f32[1,16,1024]{2,0,1:T(1,128)S(1)}, u32[]{:S(2)}, u32[]{:S(2)}) collective-permute-start(f32[1,16,1024]{2,0,1:T(1,128)S(1)} %get-tuple-element.54), channel_id=1, source_target_pairs={{0,32},{32,64},{64,96},{96,128},{128,160},{160,192},{192,224},{1,3... | collective-permute-start | bytes 196616 | tf_op jit(solution)/shard_map/ppermute | solution.py:30
  109.4 25.7 %collective-permute-start.9 = (f32[1,16,1024]{2,0,1:T(1,128)S(1)}, f32[1,16,1024]{2,0,1:T(1,128)S(1)}, u32[]{:S(2)}, u32[]{:S(2)}) collective-permute-start(f32[1,16,1024]{2,0,1:T(1,128)S(1)} %get-tuple-element.55), channel_id=1, source_target_pairs={{32,0},{64,32},{96,64},{128,96},{160,128},{192,160},{224,192},{33,... | collective-permute-start | bytes 196616 | tf_op jit(solution)/shard_map/ppermute | solution.py:31
  135.3 9.4 %collective-permute-start.10 = (f32[8,1,1024]{2,0,1:T(8,128)S(1)}, f32[8,1,1024]{2,0,1:T(8,128)S(1)}, u32[]{:S(2)}, u32[]{:S(2)}) collective-permute-start(f32[8,1,1024]{2,0,1:T(8,128)S(1)} %get-tuple-element.52), channel_id=1, source_target_pairs={{0,1},{1,2},{2,3},{3,4},{4,5},{5,6},{6,7},{7,8},{8,9},{9,10},{10,1... | collective-permute-start | bytes 98312 | tf_op jit(solution)/shard_map/ppermute | solution.py:30
  137.9 6.8 %collective-permute-start.11 = (f32[8,1,1024]{2,0,1:T(8,128)S(1)}, f32[8,1,1024]{2,0,1:T(8,128)S(1)}, u32[]{:S(2)}, u32[]{:S(2)}) collective-permute-start(f32[8,1,1024]{2,0,1:T(8,128)S(1)} %get-tuple-element.53), channel_id=1, source_target_pairs={{1,0},{2,1},{3,2},{4,3},{5,4},{6,5},{7,6},{8,7},{9,8},{10,9},{11,1... | collective-permute-start | bytes 98312 | tf_op jit(solution)/shard_map/ppermute | solution.py:31
  153.7 27.7 %collective-permute-start.12 = (f32[1,16,1024]{2,0,1:T(1,128)S(1)}, f32[1,16,1024]{2,0,1:T(1,128)S(1)}, u32[]{:S(2)}, u32[]{:S(2)}) collective-permute-start(f32[1,16,1024]{2,0,1:T(1,128)S(1)} %get-tuple-element.50), channel_id=1, source_target_pairs={{0,32},{32,64},{64,96},{96,128},{128,160},{160,192},{192,224},{1,3... | collective-permute-start | bytes 196616 | tf_op jit(solution)/shard_map/ppermute | solution.py:30
  156.5 24.9 %collective-permute-start.13 = (f32[1,16,1024]{2,0,1:T(1,128)S(1)}, f32[1,16,1024]{2,0,1:T(1,128)S(1)}, u32[]{:S(2)}, u32[]{:S(2)}) collective-permute-start(f32[1,16,1024]{2,0,1:T(1,128)S(1)} %get-tuple-element.51), channel_id=1, source_target_pairs={{32,0},{64,32},{96,64},{128,96},{160,128},{192,160},{224,192},{33,... | collective-permute-start | bytes 196616 | tf_op jit(solution)/shard_map/ppermute | solution.py:31
  181.7 8.3 %collective-permute-start.14 = (f32[8,1,1024]{2,0,1:T(8,128)S(1)}, f32[8,1,1024]{2,0,1:T(8,128)S(1)}, u32[]{:S(2)}, u32[]{:S(2)}) collective-permute-start(f32[8,1,1024]{2,0,1:T(8,128)S(1)} %get-tuple-element.48), channel_id=1, source_target_pairs={{0,1},{1,2},{2,3},{3,4},{4,5},{5,6},{6,7},{7,8},{8,9},{9,10},{10,1... | collective-permute-start | bytes 98312 | tf_op jit(solution)/shard_map/ppermute | solution.py:30
  184.3 5.7 %collective-permute-start.15 = (f32[8,1,1024]{2,0,1:T(8,128)S(1)}, f32[8,1,1024]{2,0,1:T(8,128)S(1)}, u32[]{:S(2)}, u32[]{:S(2)}) collective-permute-start(f32[8,1,1024]{2,0,1:T(8,128)S(1)} %get-tuple-element.49), channel_id=1, source_target_pairs={{1,0},{2,1},{3,2},{4,3},{5,4},{6,5},{7,6},{8,7},{9,8},{10,9},{11,1... | collective-permute-start | bytes 98312 | tf_op jit(solution)/shard_map/ppermute | solution.py:31

commit v2 on v0

--- a/solution.py
+++ b/solution.py
@@ -237,11 +237,11 @@
     norm_now, curvature = sums[0], sums[1]
     searched = assemble(local)
     step_len = norm_now / curvature
-    for iteration in range(1, ITERS + 1):
+
+    def iterate(_, state):
+        pressure, residual, direction, searched, norm_now, curvature, step_len = state
         pressure = pressure + step_len * direction
         residual = residual - step_len * searched
-        if iteration == ITERS:
-            break
         local = local_operator(residual, weight3, metric, diffmat)
         sums = mesh_sum(
             jnp.stack(
@@ -258,8 +258,14 @@
         direction = residual + ratio * direction
         searched = applied + ratio * searched
         curvature = own_curvature + 2.0 * ratio * cross + ratio * ratio * curvature
-        norm_now = norm_next
-        step_len = norm_now / curvature
+        step_len = norm_next / curvature
+        return (pressure, residual, direction, searched, norm_next, curvature, step_len)
+
+    state = (pressure, residual, direction, searched, norm_now, curvature, step_len)
+    state = lax.fori_loop(1, ITERS, iterate, state)
+    pressure, residual, direction, searched, norm_now, curvature, step_len = state
+    pressure = pressure + step_len * direction
+    residual = residual - step_len * searched
     return (pressure, residual)
 
 

time: 187 us -> 200 us (1.070)
  loops' own time: 0 us -> 9.22 us
  other arithmetic: 20.8 us -> 28.8 us
  between operations: 9.69 us -> 2.51 us
  starting transfers between devices: 79.9 us -> 85.6 us
  waiting for transfers between devices: 44.3 us -> 40.6 us
    another operation x0 -> x1, loops' own time: none -> 9.22 us  [on_device(): state = lax.fori_loop(1, ITERS, iterate, state)]
    ppermute x8, waiting for transfers between devices: 18.8 us -> 11.4 us  [with_halo(): after = lax.ppermute(first, axis, down)]
    add x0 -> x5, other arithmetic: none -> 5.71 us  [the longest x2 3.29 us: iterate(): direction = residual + ratio * direction]
    mul x2 -> x6, local copies, waits for them, and re-layouts: 0.99 us -> 5.29 us  [derive(): jnp.kron(jnp.eye(block_width // POLY, dtype=jnp.float32), matrix)]
    ppermute x8, starting transfers between devices: 13.5 us -> 17.5 us  [with_halo(): after = lax.ppermute(first, axis, down)]
    all_to_all x1, waiting for transfers between devices: 3.61 us -> 6.9 us  [project_points(): lax.all_to_all(outgoing, 'span', split_axis=0, concat_axis=0, tiled=True)]
    mul x1 -> x3, other arithmetic: 0.92 us -> 3.32 us  [derive(): jnp.kron(jnp.eye(block_width // POLY, dtype=jnp.float32), matrix)]
    unnamed x15 -> x24, local copies, waits for them, and re-layouts: 2.68 us -> 0.53 us
where the time goes in v2:
time: 200 us; the launch traced here: 199 us
  starting transfers between devices  85.6 us (43%)
  waiting for transfers between devices  40.6 us (20%)
  other arithmetic  28.8 us (14%)
  matrix products  17.2 us (9%)
  local copies, waits for them, and re-layouts  14.7 us (7%)
  loops' own time  9.22 us (5%)
  between operations  2.51 us (1%)
    all_to_all x3, starting transfers between devices, mesh_sum(): gathered = lax.all_to_all(spread, axes, 0, 0, tiled=True)  33.3 us
    ppermute x8, starting transfers between devices, with_halo(): before = lax.ppermute(last, axis, up)  26.2 us
    all_to_all x3, waiting for transfers between devices, mesh_sum(): gathered = lax.all_to_all(spread, axes, 0, 0, tiled=True)  21.1 us
    ppermute x8, starting transfers between devices, with_halo(): after = lax.ppermute(first, axis, down)  17.5 us
    ppermute x8, waiting for transfers between devices, with_halo(): after = lax.ppermute(first, axis, down)  11.4 us
    another operation x1, loops' own time, on_device(): state = lax.fori_loop(1, ITERS, iterate, state)  9.22 us
    all_to_all x1, starting transfers between devices, project_points(): lax.all_to_all(outgoing, 'span', split_axis=0, concat_axis=0, tiled=True)  8.59 us
    all_to_all x1, waiting for transfers between devices, project_points(): lax.all_to_all(outgoing, 'span', split_axis=0, concat_axis=0, tiled=True)  6.9 us
  transfers between devices with their start and end apart: 20, of which 9 were waited for; matrix products, arithmetic and copies ran while one was open for 4% of the time, Pallas kernels for 0%

profile of v2, /device:TPU:1, one launch (start us, length us, event | category | flops | bytes accessed | tf_op | source)
XLA Modules:
  0.0 198.7 jit_solution(4113859199647387609)
XLA Ops:
  0.7 0.9 convert_reduce_fusion
  1.6 0.7 convert_bitcast_fusion
  3.0 0.8 select_reduce_fusion
  5.3 0.9 scatter_custom_fusion
  6.2 0.8 copy.265
  7.0 0.8 broadcast_multiply_fusion.6
  8.5 0.7 broadcast_multiply_fusion.7
  9.3 0.9 broadcast_multiply_fusion.2
  10.3 8.6 %all-to-all-start.1 = ((f32[32,8,8]{1,2,0:T(8,128)}), f32[32,8,8]{1,2,0:T(8,128)S(1)}, u32[]{:S(2)}, u32[]{:S(2)}) async-start(f32[32,8,8]{1,2,0:T(8,128)} %copy.265), calls=%async_computation.1 | async-start | bytes 262144 | tf_op jit(solution)/shard_map/all_to_all | solution.py:183
  19.6 6.9 %all-to-all-done.1 = f32[32,8,8]{1,2,0:T(8,128)S(1)} async-done(((f32[32,8,8]{1,2,0:T(8,128)}), f32[32,8,8]{1,2,0:T(8,128)S(1)}, u32[]{:S(2)}, u32[]{:S(2)}) %all-to-all-start.1) | async-done | bytes 8224 | tf_op jit(solution)/shard_map/all_to_all | solution.py:183
  26.9 1.7 fusion.44
  30.3 0.8 convolution_bitcast_fusion.11
  31.1 0.9 fusion.37
  32.1 3.5 %collective-permute-start.4 = (f32[1,16,1024]{2,0,1:T(1,128)S(1)}, f32[1,16,1024]{2,0,1:T(1,128)S(1)}, u32[]{:S(2)}, u32[]{:S(2)}) collective-permute-start(f32[1,16,1024]{2,0,1:T(1,128)S(1)} %get-tuple-element.310), channel_id=1, source_target_pairs={{0,32},{32,64},{64,96},{96,128},{128,160},{160,192},{192,224},{1,3... | collective-permute-start | bytes 196616 | tf_op jit(solution)/shard_map/ppermute | solution.py:30
  35.7 1.3 collective-permute-start.5
  37.0 3.9 %collective-permute-done.5 = f32[1,16,1024]{2,0,1:T(1,128)S(1)} collective-permute-done((f32[1,16,1024]{2,0,1:T(1,128)S(1)}, f32[1,16,1024]{2,0,1:T(1,128)S(1)}, u32[]{:S(2)}, u32[]{:S(2)}) %collective-permute-start.5) | collective-permute-done | bytes 65568 | tf_op jit(solution)/shard_map/ppermute | solution.py:31
  41.1 3.8 %collective-permute-start.6 = (f32[8,1,1024]{2,0,1:T(8,128)S(1)}, f32[8,1,1024]{2,0,1:T(8,128)S(1)}, u32[]{:S(2)}, u32[]{:S(2)}) collective-permute-start(f32[8,1,1024]{2,0,1:T(8,128)S(1)} %get-tuple-element.308), channel_id=1, source_target_pairs={{0,1},{1,2},{2,3},{3,4},{4,5},{5,6},{6,7},{7,8},{8,9},{9,10},{10,1... | collective-permute-start | bytes 98312 | tf_op jit(solution)/shard_map/ppermute | solution.py:30
  44.9 2.1 %collective-permute-start.7 = (f32[8,1,1024]{2,0,1:T(8,128)S(1)}, f32[8,1,1024]{2,0,1:T(8,128)S(1)}, u32[]{:S(2)}, u32[]{:S(2)}) collective-permute-start(f32[8,1,1024]{2,0,1:T(8,128)S(1)} %get-tuple-element.309), channel_id=1, source_target_pairs={{1,0},{2,1},{3,2},{4,3},{5,4},{6,5},{7,6},{8,7},{9,8},{10,9},{11,1... | collective-permute-start | bytes 98312 | tf_op jit(solution)/shard_map/ppermute | solution.py:31
  47.5 2.6 %collective-permute-done.7 = f32[8,1,1024]{2,0,1:T(8,128)S(1)} collective-permute-done((f32[8,1,1024]{2,0,1:T(8,128)S(1)}, f32[8,1,1024]{2,0,1:T(8,128)S(1)}, u32[]{:S(2)}, u32[]{:S(2)}) %collective-permute-start.7) | collective-permute-done | bytes 32800 | tf_op jit(solution)/shard_map/ppermute | solution.py:31
  50.7 0.9 convolution_bitcast_fusion.8
  54.0 0.9 convolution_bitcast_fusion.7
  56.0 3.5 %collective-permute-start.8 = (f32[1,16,1024]{2,0,1:T(1,128)S(1)}, f32[1,16,1024]{2,0,1:T(1,128)S(1)}, u32[]{:S(2)}, u32[]{:S(2)}) collective-permute-start(f32[1,16,1024]{2,0,1:T(1,128)S(1)} %get-tuple-element.306), channel_id=1, source_target_pairs={{0,32},{32,64},{64,96},{96,128},{128,160},{160,192},{192,224},{1,3... | collective-permute-start | bytes 196616 | tf_op jit(solution)/shard_map/ppermute | solution.py:30
  59.6 1.3 collective-permute-start.9
  61.0 4.9 %collective-permute-done.9 = f32[1,16,1024]{2,0,1:T(1,128)S(1)} collective-permute-done((f32[1,16,1024]{2,0,1:T(1,128)S(1)}, f32[1,16,1024]{2,0,1:T(1,128)S(1)}, u32[]{:S(2)}, u32[]{:S(2)}) %collective-permute-start.9) | collective-permute-done | bytes 65568 | tf_op jit(solution)/shard_map/ppermute | solution.py:31
  65.9 1.2 multiply_reduce_fusion.2
  67.1 1.4 pad_maximum_fusion.13
  68.5 0.7 broadcast_in_dim.261
  69.2 13.0 %all-to-all-start.2 = ((f32[256,1,2]{2,1,0:T(1,128)}), f32[256,1,2]{2,1,0:T(1,128)S(1)}, u32[]{:S(2)}, u32[]{:S(2)}) async-start(f32[256,1,2]{2,1,0:T(1,128)} %broadcast_in_dim.261), calls=%async_computation.2 | async-start | bytes 262144 | tf_op jit(solution)/shard_map/all_to_all | solution.py:130
  82.2 3.5 %collective-permute-start.10 = (f32[8,1,1024]{2,0,1:T(8,128)S(1)}, f32[8,1,1024]{2,0,1:T(8,128)S(1)}, u32[]{:S(2)}, u32[]{:S(2)}) collective-permute-start(f32[8,1,1024]{2,0,1:T(8,128)S(1)} %get-tuple-element.304), channel_id=1, source_target_pairs={{0,1},{1,2},{2,3},{3,4},{4,5},{5,6},{6,7},{7,8},{8,9},{9,10},{10,1... | collective-permute-start | bytes 98312 | tf_op jit(solution)/shard_map/ppermute | solution.py:30
  85.8 2.1 %collective-permute-start.11 = (f32[8,1,1024]{2,0,1:T(8,128)S(1)}, f32[8,1,1024]{2,0,1:T(8,128)S(1)}, u32[]{:S(2)}, u32[]{:S(2)}) collective-permute-start(f32[8,1,1024]{2,0,1:T(8,128)S(1)} %get-tuple-element.305), channel_id=1, source_target_pairs={{1,0},{2,1},{3,2},{4,3},{5,4},{6,5},{7,6},{8,7},{9,8},{10,9},{11,1... | collective-permute-start | bytes 98312 | tf_op jit(solution)/shard_map/ppermute | solution.py:31
  87.9 7.2 %all-to-all-done.2 = f32[256,1,2]{2,1,0:T(1,128)S(1)} async-done(((f32[256,1,2]{2,1,0:T(1,128)}), f32[256,1,2]{2,1,0:T(1,128)S(1)}, u32[]{:S(2)}, u32[]{:S(2)}) %all-to-all-start.2) | async-done | bytes 2080 | tf_op jit(solution)/shard_map/all_to_all | solution.py:130
  98.0 97.9 %while.26 = (s32[]{:T(128)}, f32[8,16,1024]{2,0,1:T(8,128)}, f32[8,16,1024]{2,0,1:T(8,128)S(1)}, f32[8,16,1024]{2,0,1:T(8,128)S(1)}, f32[8,16,1024]{2,0,1:T(8,12...) while((s32[]{:T(128)}, f32[8,16,1024]{2,0,1:T(8,128)}, ...), condition=%wide.region_11.12_spmd.clone.clone, body=%wide.region_6.11_spmd.sunk.clone.clone.sunk | while | flops 458532288 | bytes 21588152 | solution.py:265
  98.0 1.2 broadcast_multiply_fusion.10
  99.2 1.6 reshape.792
  101.5 1.1 fusion.178
  104.7 0.8 convolution_bitcast_fusion.16
  105.6 0.7 fusion.180
  106.4 1.3 collective-permute-start
  107.7 4.0 %collective-permute-start.1 = (f32[1,16,1024]{2,0,1:T(1,128)S(1)}, f32[1,16,1024]{2,0,1:T(1,128)S(1)}, u32[]{:S(2)}, u32[]{:S(2)}) collective-permute-start(f32[1,16,1024]{2,0,1:T(1,128)S(1)} %get-tuple-element.435), channel_id=1, source_target_pairs={{0,32},{32,64},{64,96},{96,128},{128,160},{160,192},{192,224},{1,3... | collective-permute-start | bytes 196616 | tf_op jit(solution)/shard_map/while/body/eval_jaxpr/ppermute | solution.py:30
  113.0 1.1 fusion.182
  114.1 2.0 pad_maximum_fusion.15
  116.0 0.7 broadcast_in_dim.328
  116.8 10.2 %all-to-all-start = ((f32[256,1,3]{2,1,0:T(1,128)}), f32[256,1,3]{2,1,0:T(1,128)S(1)}, u32[]{:S(2)}, u32[]{:S(2)}) async-start(f32[256,1,3]{2,1,0:T(1,128)} %broadcast_in_dim.328), calls=%async_computation | async-start | bytes 262144 | tf_op jit(solution)/shard_map/while/body/eval_jaxpr/all_to_all | solution.py:130
  126.9 4.1 %collective-permute-start.2 = (f32[8,1,1024]{2,0,1:T(8,128)S(1)}, f32[8,1,1024]{2,0,1:T(8,128)S(1)}, u32[]{:S(2)}, u32[]{:S(2)}) collective-permute-start(f32[8,1,1024]{2,0,1:T(8,128)S(1)} %get-tuple-element.444), channel_id=1, source_target_pairs={{1,0},{2,1},{3,2},{4,3},{5,4},{6,5},{7,6},{8,7},{9,8},{10,9},{11,1... | collective-permute-start | bytes 98312 | tf_op jit(solution)/shard_map/while/body/eval_jaxpr/ppermute | solution.py:31
  131.0 1.9 collective-permute-start.3
  132.9 6.9 %all-to-all-done = f32[256,1,3]{2,1,0:T(1,128)S(1)} async-done(((f32[256,1,3]{2,1,0:T(1,128)}), f32[256,1,3]{2,1,0:T(1,128)S(1)}, u32[]{:S(2)}, u32[]{:S(2)}) %all-to-all-start) | async-done | bytes 3104 | tf_op jit(solution)/shard_map/while/body/eval_jaxpr/all_to_all | solution.py:130
  141.5 1.1 multiply_add_fusion.2
  146.4 1.2 broadcast_multiply_fusion.10
  147.6 1.6 reshape.792
  149.9 1.1 fusion.178
  153.2 0.8 convolution_bitcast_fusion.16
  154.0 0.7 fusion.180
  154.8 1.3 collective-permute-start
  156.1 4.0 %collective-permute-start.1 = (f32[1,16,1024]{2,0,1:T(1,128)S(1)}, f32[1,16,1024]{2,0,1:T(1,128)S(1)}, u32[]{:S(2)}, u32[]{:S(2)}) collective-permute-start(f32[1,16,1024]{2,0,1:T(1,128)S(1)} %get-tuple-element.435), channel_id=1, source_target_pairs={{0,32},{32,64},{64,96},{96,128},{128,160},{160,192},{192,224},{1,3... | collective-permute-start | bytes 196616 | tf_op jit(solution)/shard_map/while/body/eval_jaxpr/ppermute | solution.py:30
  161.4 1.1 fusion.182
  162.5 2.0 pad_maximum_fusion.15
  164.5 0.7 broadcast_in_dim.328
  165.2 10.2 %all-to-all-start = ((f32[256,1,3]{2,1,0:T(1,128)}), f32[256,1,3]{2,1,0:T(1,128)S(1)}, u32[]{:S(2)}, u32[]{:S(2)}) async-start(f32[256,1,3]{2,1,0:T(1,128)} %broadcast_in_dim.328), calls=%async_computation | async-start | bytes 262144 | tf_op jit(solution)/shard_map/while/body/eval_jaxpr/all_to_all | solution.py:130
  175.4 4.1 %collective-permute-start.2 = (f32[8,1,1024]{2,0,1:T(8,128)S(1)}, f32[8,1,1024]{2,0,1:T(8,128)S(1)}, u32[]{:S(2)}, u32[]{:S(2)}) collective-permute-start(f32[8,1,1024]{2,0,1:T(8,128)S(1)} %get-tuple-element.444), channel_id=1, source_target_pairs={{1,0},{2,1},{3,2},{4,3},{5,4},{6,5},{7,6},{8,7},{9,8},{10,9},{11,1... | collective-permute-start | bytes 98312 | tf_op jit(solution)/shard_map/while/body/eval_jaxpr/ppermute | solution.py:31
  179.4 1.9 collective-permute-start.3
  181.4 6.9 %all-to-all-done = f32[256,1,3]{2,1,0:T(1,128)S(1)} async-done(((f32[256,1,3]{2,1,0:T(1,128)}), f32[256,1,3]{2,1,0:T(1,128)S(1)}, u32[]{:S(2)}, u32[]{:S(2)}) %all-to-all-start) | async-done | bytes 3104 | tf_op jit(solution)/shard_map/while/body/eval_jaxpr/all_to_all | solution.py:130
  189.9 2.2 %multiply_add_fusion.2 = (f32[8,16,1024]{2,0,1:T(8,128)S(1)}, f32[8,16,1024]{2,0,1:T(8,128)}) fusion(f32[8,16,1024]{2,0,1:T(8,128)S(1)} %multiply_subtract_fusion.2, f32[8,16,1024]{2,0,1:T(8,128)S(1)} %get-tuple-element.476, f32[]{:T(128)S(6)} %div.133, f32[]{:T(128)} %get-tuple-element.480, f32[8,16,1024]{2,0,1:T(8,128)} %get-tuple-element.474, ...), kind=kLoop, calls=%fused_computation.44.clone.1 | loop fusion | flops 655360 | bytes 2621449 | tf_op jit(solution)/shard_map/while/body/eval_jaxpr/add | solution.py:258
  195.9 1.4 copy_subtract_fusion
  197.3 1.4 copy_add_fusion
  (123 shorter events, 22.3 us)
Async XLA Ops:
  0.6 18.2 %copy-start.9 = (f32[8]{0:T(128)S(1)}, f32[8]{0:T(128)}, u32[]{:S(2)}) copy-start(f32[8]{0:T(128)} %constant.250.clone) | copy-start | bytes 100
  9.3 17.4 %copy-start.10 = (f32[8]{0:T(128)S(1)}, f32[8]{0:T(128)}, u32[]{:S(2)}) copy-start(f32[8]{0:T(128)} %constant.249.clone) | copy-start | bytes 100
  10.3 16.2 %all-to-all-start.1 = ((f32[32,8,8]{1,2,0:T(8,128)}), f32[32,8,8]{1,2,0:T(8,128)S(1)}, u32[]{:S(2)}, u32[]{:S(2)}) async-start(f32[32,8,8]{1,2,0:T(8,128)} %copy.265), calls=%async_computation.1 | async-start | bytes 262144 | tf_op jit(solution)/shard_map/all_to_all | solution.py:183
  19.5 9.0 %copy-start.1 = (f32[3,8,16,1024]{3,2,1,0:T(8,128)S(1)}, f32[3,8,16,1024]{3,2,1,0:T(8,128)}, u32[]{:S(2)}) copy-start(f32[3,8,16,1024]{3,2,1,0:T(8,128)} %param.13) | copy-start | bytes 4718596
  28.6 0.7 copy-start.8
  29.3 1.8 copy-start.7
  32.1 4.9 %collective-permute-start.4 = (f32[1,16,1024]{2,0,1:T(1,128)S(1)}, f32[1,16,1024]{2,0,1:T(1,128)S(1)}, u32[]{:S(2)}, u32[]{:S(2)}) collective-permute-start(f32[1,16,1024]{2,0,1:T(1,128)S(1)} %get-tuple-element.310), channel_id=1, source_target_pairs={{0,32},{32,64},{64,96},{96,128},{128,160},{160,192},{192,224},{1,3... | collective-permute-start | bytes 196616 | tf_op jit(solution)/shard_map/ppermute | solution.py:30
  35.7 5.2 %collective-permute-start.5 = (f32[1,16,1024]{2,0,1:T(1,128)S(1)}, f32[1,16,1024]{2,0,1:T(1,128)S(1)}, u32[]{:S(2)}, u32[]{:S(2)}) collective-permute-start(f32[1,16,1024]{2,0,1:T(1,128)S(1)} %get-tuple-element.311), channel_id=1, source_target_pairs={{32,0},{64,32},{96,64},{128,96},{160,128},{192,160},{224,192},{33,... | collective-permute-start | bytes 196616 | tf_op jit(solution)/shard_map/ppermute | solution.py:31
  41.1 6.4 %collective-permute-start.6 = (f32[8,1,1024]{2,0,1:T(8,128)S(1)}, f32[8,1,1024]{2,0,1:T(8,128)S(1)}, u32[]{:S(2)}, u32[]{:S(2)}) collective-permute-start(f32[8,1,1024]{2,0,1:T(8,128)S(1)} %get-tuple-element.308), channel_id=1, source_target_pairs={{0,1},{1,2},{2,3},{3,4},{4,5},{5,6},{6,7},{7,8},{8,9},{9,10},{10,1... | collective-permute-start | bytes 98312 | tf_op jit(solution)/shard_map/ppermute | solution.py:30
  44.9 5.2 %collective-permute-start.7 = (f32[8,1,1024]{2,0,1:T(8,128)S(1)}, f32[8,1,1024]{2,0,1:T(8,128)S(1)}, u32[]{:S(2)}, u32[]{:S(2)}) collective-permute-start(f32[8,1,1024]{2,0,1:T(8,128)S(1)} %get-tuple-element.309), channel_id=1, source_target_pairs={{1,0},{2,1},{3,2},{4,3},{5,4},{6,5},{7,6},{8,7},{9,8},{10,9},{11,1... | collective-permute-start | bytes 98312 | tf_op jit(solution)/shard_map/ppermute | solution.py:31
  50.3 1.6 copy-start.2
  56.0 4.9 %collective-permute-start.8 = (f32[1,16,1024]{2,0,1:T(1,128)S(1)}, f32[1,16,1024]{2,0,1:T(1,128)S(1)}, u32[]{:S(2)}, u32[]{:S(2)}) collective-permute-start(f32[1,16,1024]{2,0,1:T(1,128)S(1)} %get-tuple-element.306), channel_id=1, source_target_pairs={{0,32},{32,64},{64,96},{96,128},{128,160},{160,192},{192,224},{1,3... | collective-permute-start | bytes 196616 | tf_op jit(solution)/shard_map/ppermute | solution.py:30
  59.6 6.3 %collective-permute-start.9 = (f32[1,16,1024]{2,0,1:T(1,128)S(1)}, f32[1,16,1024]{2,0,1:T(1,128)S(1)}, u32[]{:S(2)}, u32[]{:S(2)}) collective-permute-start(f32[1,16,1024]{2,0,1:T(1,128)S(1)} %get-tuple-element.307), channel_id=1, source_target_pairs={{32,0},{64,32},{96,64},{128,96},{160,128},{192,160},{224,192},{33,... | collective-permute-start | bytes 196616 | tf_op jit(solution)/shard_map/ppermute | solution.py:31
  67.1 30.8 %copy-start.3 = (f32[8,8,1,1]{1,0,3,2:T(8,128)S(1)}, f32[8,8,1,1]{1,0,3,2:T(8,128)}, u32[]{:S(2)}) copy-start(f32[8,8,1,1]{1,0,3,2:T(8,128)} %constant.471) | copy-start | bytes 772
  67.1 30.8 %copy-start.4 = (f32[8,8,1]{1,0,2:T(8,128)S(1)}, f32[8,8,1]{1,0,2:T(8,128)}, u32[]{:S(2)}) copy-start(f32[8,8,1]{1,0,2:T(8,128)} %constant.472) | copy-start | bytes 772
  67.1 30.8 %copy-start.5 = (f32[8,8]{1,0:T(8,128)S(1)}, f32[8,8]{1,0:T(8,128)}, u32[]{:S(2)}) copy-start(f32[8,8]{1,0:T(8,128)} %constant.271) | copy-start | bytes 772
  67.1 30.8 %copy-start.6 = (f32[8,8]{1,0:T(8,128)S(1)}, f32[8,8]{1,0:T(8,128)}, u32[]{:S(2)}) copy-start(f32[8,8]{1,0:T(8,128)} %constant.251.clone..sunk.3) | copy-start | bytes 772
  69.2 25.9 %all-to-all-start.2 = ((f32[256,1,2]{2,1,0:T(1,128)}), f32[256,1,2]{2,1,0:T(1,128)S(1)}, u32[]{:S(2)}, u32[]{:S(2)}) async-start(f32[256,1,2]{2,1,0:T(1,128)} %broadcast_in_dim.261), calls=%async_computation.2 | async-start | bytes 262144 | tf_op jit(solution)/shard_map/all_to_all | solution.py:130
  82.2 15.2 %collective-permute-start.10 = (f32[8,1,1024]{2,0,1:T(8,128)S(1)}, f32[8,1,1024]{2,0,1:T(8,128)S(1)}, u32[]{:S(2)}, u32[]{:S(2)}) collective-permute-start(f32[8,1,1024]{2,0,1:T(8,128)S(1)} %get-tuple-element.304), channel_id=1, source_target_pairs={{0,1},{1,2},{2,3},{3,4},{4,5},{5,6},{6,7},{7,8},{8,9},{9,10},{10,1... | collective-permute-start | bytes 98312 | tf_op jit(solution)/shard_map/ppermute | solution.py:30
  85.8 11.6 %collective-permute-start.11 = (f32[8,1,1024]{2,0,1:T(8,128)S(1)}, f32[8,1,1024]{2,0,1:T(8,128)S(1)}, u32[]{:S(2)}, u32[]{:S(2)}) collective-permute-start(f32[8,1,1024]{2,0,1:T(8,128)S(1)} %get-tuple-element.305), channel_id=1, source_target_pairs={{1,0},{2,1},{3,2},{4,3},{5,4},{6,5},{7,6},{8,7},{9,8},{10,9},{11,1... | collective-permute-start | bytes 98312 | tf_op jit(solution)/shard_map/ppermute | solution.py:31
  106.4 6.0 %collective-permute-start = (f32[1,16,1024]{2,0,1:T(1,128)S(1)}, f32[1,16,1024]{2,0,1:T(1,128)S(1)}, u32[]{:S(2)}, u32[]{:S(2)}) collective-permute-start(f32[1,16,1024]{2,0,1:T(1,128)S(1)} %get-tuple-element.433), channel_id=1, source_target_pairs={{32,0},{64,32},{96,64},{128,96},{160,128},{192,160},{224,192},{33,... | collective-permute-start | bytes 196616 | tf_op jit(solution)/shard_map/while/body/eval_jaxpr/ppermute | solution.py:31
  107.7 5.3 %collective-permute-start.1 = (f32[1,16,1024]{2,0,1:T(1,128)S(1)}, f32[1,16,1024]{2,0,1:T(1,128)S(1)}, u32[]{:S(2)}, u32[]{:S(2)}) collective-permute-start(f32[1,16,1024]{2,0,1:T(1,128)S(1)} %get-tuple-element.435), channel_id=1, source_target_pairs={{0,32},{32,64},{64,96},{96,128},{128,160},{160,192},{192,224},{1,3... | collective-permute-start | bytes 196616 | tf_op jit(solution)/shard_map/while/body/eval_jaxpr/ppermute | solution.py:30
  116.8 23.1 %all-to-all-start = ((f32[256,1,3]{2,1,0:T(1,128)}), f32[256,1,3]{2,1,0:T(1,128)S(1)}, u32[]{:S(2)}, u32[]{:S(2)}) async-start(f32[256,1,3]{2,1,0:T(1,128)} %broadcast_in_dim.328), calls=%async_computation | async-start | bytes 262144 | tf_op jit(solution)/shard_map/while/body/eval_jaxpr/all_to_all | solution.py:130
  126.9 18.2 %collective-permute-start.2 = (f32[8,1,1024]{2,0,1:T(8,128)S(1)}, f32[8,1,1024]{2,0,1:T(8,128)S(1)}, u32[]{:S(2)}, u32[]{:S(2)}) collective-permute-start(f32[8,1,1024]{2,0,1:T(8,128)S(1)} %get-tuple-element.444), channel_id=1, source_target_pairs={{1,0},{2,1},{3,2},{4,3},{5,4},{6,5},{7,6},{8,7},{9,8},{10,9},{11,1... | collective-permute-start | bytes 98312 | tf_op jit(solution)/shard_map/while/body/eval_jaxpr/ppermute | solution.py:31
  131.0 14.1 %collective-permute-start.3 = (f32[8,1,1024]{2,0,1:T(8,128)S(1)}, f32[8,1,1024]{2,0,1:T(8,128)S(1)}, u32[]{:S(2)}, u32[]{:S(2)}) collective-permute-start(f32[8,1,1024]{2,0,1:T(8,128)S(1)} %get-tuple-element.445), channel_id=1, source_target_pairs={{0,1},{1,2},{2,3},{3,4},{4,5},{5,6},{6,7},{7,8},{8,9},{9,10},{10,1... | collective-permute-start | bytes 98312 | tf_op jit(solution)/shard_map/while/body/eval_jaxpr/ppermute | solution.py:30
  154.8 6.0 %collective-permute-start = (f32[1,16,1024]{2,0,1:T(1,128)S(1)}, f32[1,16,1024]{2,0,1:T(1,128)S(1)}, u32[]{:S(2)}, u32[]{:S(2)}) collective-permute-start(f32[1,16,1024]{2,0,1:T(1,128)S(1)} %get-tuple-element.433), channel_id=1, source_target_pairs={{32,0},{64,32},{96,64},{128,96},{160,128},{192,160},{224,192},{33,... | collective-permute-start | bytes 196616 | tf_op jit(solution)/shard_map/while/body/eval_jaxpr/ppermute | solution.py:31
  156.1 5.3 %collective-permute-start.1 = (f32[1,16,1024]{2,0,1:T(1,128)S(1)}, f32[1,16,1024]{2,0,1:T(1,128)S(1)}, u32[]{:S(2)}, u32[]{:S(2)}) collective-permute-start(f32[1,16,1024]{2,0,1:T(1,128)S(1)} %get-tuple-element.435), channel_id=1, source_target_pairs={{0,32},{32,64},{64,96},{96,128},{128,160},{160,192},{192,224},{1,3... | collective-permute-start | bytes 196616 | tf_op jit(solution)/shard_map/while/body/eval_jaxpr/ppermute | solution.py:30
  165.2 23.1 %all-to-all-start = ((f32[256,1,3]{2,1,0:T(1,128)}), f32[256,1,3]{2,1,0:T(1,128)S(1)}, u32[]{:S(2)}, u32[]{:S(2)}) async-start(f32[256,1,3]{2,1,0:T(1,128)} %broadcast_in_dim.328), calls=%async_computation | async-start | bytes 262144 | tf_op jit(solution)/shard_map/while/body/eval_jaxpr/all_to_all | solution.py:130
  175.4 19.2 %collective-permute-start.2 = (f32[8,1,1024]{2,0,1:T(8,128)S(1)}, f32[8,1,1024]{2,0,1:T(8,128)S(1)}, u32[]{:S(2)}, u32[]{:S(2)}) collective-permute-start(f32[8,1,1024]{2,0,1:T(8,128)S(1)} %get-tuple-element.444), channel_id=1, source_target_pairs={{1,0},{2,1},{3,2},{4,3},{5,4},{6,5},{7,6},{8,7},{9,8},{10,9},{11,1... | collective-permute-start | bytes 98312 | tf_op jit(solution)/shard_map/while/body/eval_jaxpr/ppermute | solution.py:31
  179.4 15.2 %collective-permute-start.3 = (f32[8,1,1024]{2,0,1:T(8,128)S(1)}, f32[8,1,1024]{2,0,1:T(8,128)S(1)}, u32[]{:S(2)}, u32[]{:S(2)}) collective-permute-start(f32[8,1,1024]{2,0,1:T(8,128)S(1)} %get-tuple-element.445), channel_id=1, source_target_pairs={{0,1},{1,2},{2,3},{3,4},{4,5},{5,6},{6,7},{7,8},{8,9},{9,10},{10,1... | collective-permute-start | bytes 98312 | tf_op jit(solution)/shard_map/while/body/eval_jaxpr/ppermute | solution.py:30
  195.9 1.4 copy-start

commit v3 on v0

--- a/solution.py
+++ b/solution.py
@@ -226,14 +226,12 @@
     running = running + derive(weight3 * (velocity[2] + forcing[2]), diffmat, 2, True)
     rhs = assemble(running)
 
-    def weighted(first_vec, second_vec):
-        return jnp.sum(first_vec * second_vec * inv_mult)
-
     pressure = jnp.zeros_like(rhs)
     residual = rhs
     direction = rhs
     local = local_operator(residual, weight3, metric, diffmat)
-    sums = mesh_sum(jnp.stack([weighted(residual, residual), jnp.sum(residual * local)]))
+    terms = jnp.stack([residual * residual * inv_mult, residual * local])
+    sums = mesh_sum(jnp.sum(terms, axis=(1, 2, 3)))
     norm_now, curvature = sums[0], sums[1]
     searched = assemble(local)
     step_len = norm_now / curvature
@@ -243,15 +241,10 @@
         if iteration == ITERS:
             break
         local = local_operator(residual, weight3, metric, diffmat)
-        sums = mesh_sum(
-            jnp.stack(
-                [
-                    weighted(residual, residual),
-                    jnp.sum(residual * local),
-                    weighted(residual, searched),
-                ]
-            )
+        terms = jnp.stack(
+            [residual * residual * inv_mult, residual * local, residual * searched * inv_mult]
         )
+        sums = mesh_sum(jnp.sum(terms, axis=(1, 2, 3)))
         applied = assemble(local)
         norm_next, own_curvature, cross = sums[0], sums[1], sums[2]
         ratio = norm_next / norm_now

time: 187 us -> 180 us (0.963)
  other arithmetic: 20.8 us -> 13.6 us
    another operation x4, other arithmetic: 5.5 us -> 1.37 us  [the longest x2 0.78 us: on_device(): jnp.stack([residual * residual * inv_mult, residual * local, residual * s...]
    reduce_sum x3, other arithmetic: 3.2 us -> 0.73 us  [on_device(): sums = mesh_sum(jnp.sum(terms, axis=(1, 2, 3)))]
where the time goes in v3:
time: 180 us; the launch traced here: 179 us
  starting transfers between devices  79.9 us (44%)
  waiting for transfers between devices  44.3 us (25%)
  matrix products  18 us (10%)
  other arithmetic  13.6 us (8%)
  local copies, waits for them, and re-layouts  13.1 us (7%)
  between operations  10 us (6%)
    all_to_all x3, starting transfers between devices, mesh_sum(): gathered = lax.all_to_all(spread, axes, 0, 0, tiled=True)  31.2 us
    ppermute x8, starting transfers between devices, with_halo(): before = lax.ppermute(last, axis, up)  26.6 us
    all_to_all x3, waiting for transfers between devices, mesh_sum(): gathered = lax.all_to_all(spread, axes, 0, 0, tiled=True)  21.8 us
    ppermute x8, waiting for transfers between devices, with_halo(): after = lax.ppermute(first, axis, down)  18.8 us
    ppermute x8, starting transfers between devices, with_halo(): after = lax.ppermute(first, axis, down)  13.5 us
    all_to_all x1, starting transfers between devices, project_points(): lax.all_to_all(outgoing, 'span', split_axis=0, concat_axis=0, tiled=True)  8.58 us
    dot_general x7, matrix products, derive(): result = jnp.einsum('ib,xybz->xyiz', matrix, blocks, precision=highest)  6.01 us
    dot_general x7, matrix products, derive(): result = jnp.einsum('ia,xayz->xiyz', matrix, blocks, precision=highest)  5.57 us
  transfers between devices with their start and end apart: 20, of which 9 were waited for; matrix products, arithmetic and copies ran while one was open for 4% of the time, Pallas kernels for 0%

profile of v3, /device:TPU:1, one launch (start us, length us, event | category | flops | bytes accessed | tf_op | source)
XLA Modules:
  0.0 178.9 jit_solution(7825209843924576025)
XLA Ops:
  1.3 0.9 convert_reduce_fusion
  2.2 0.7 convert_bitcast_fusion
  3.0 0.8 select_reduce_fusion
  3.8 0.7 broadcast_multiply_fusion.6
  4.5 0.7 maximum_bitcast_fusion
  5.3 0.9 scatter_custom_fusion
  6.2 0.8 copy.331
  6.9 8.6 %all-to-all-start = ((f32[32,8,8]{1,2,0:T(8,128)}), f32[32,8,8]{1,2,0:T(8,128)S(1)}, u32[]{:S(2)}, u32[]{:S(2)}) async-start(f32[32,8,8]{1,2,0:T(8,128)} %copy.331), calls=%async_computation | async-start | bytes 262144 | tf_op jit(solution)/shard_map/all_to_all | solution.py:183
  15.6 0.8 broadcast_multiply_fusion.4
  17.2 0.7 broadcast_multiply_fusion.5
  18.0 0.9 broadcast_multiply_fusion
  19.5 3.6 %all-to-all-done = f32[32,8,8]{1,2,0:T(8,128)S(1)} async-done(((f32[32,8,8]{1,2,0:T(8,128)}), f32[32,8,8]{1,2,0:T(8,128)S(1)}, u32[]{:S(2)}, u32[]{:S(2)}) %all-to-all-start) | async-done | bytes 8224 | tf_op jit(solution)/shard_map/all_to_all | solution.py:183
  23.5 1.7 fusion.20
  25.9 0.7 convolution_bitcast_fusion.19
  26.9 0.8 convolution_bitcast_fusion.18
  27.7 0.9 fusion.1
  28.8 3.5 %collective-permute-start = (f32[1,16,1024]{2,0,1:T(1,128)S(1)}, f32[1,16,1024]{2,0,1:T(1,128)S(1)}, u32[]{:S(2)}, u32[]{:S(2)}) collective-permute-start(f32[1,16,1024]{2,0,1:T(1,128)S(1)} %get-tuple-element.54), channel_id=1, source_target_pairs={{0,32},{32,64},{64,96},{96,128},{128,160},{160,192},{192,224},{1,3... | collective-permute-start | bytes 196616 | tf_op jit(solution)/shard_map/ppermute | solution.py:30
  32.3 1.3 collective-permute-start.1
  33.6 3.9 %collective-permute-done.1 = f32[1,16,1024]{2,0,1:T(1,128)S(1)} collective-permute-done((f32[1,16,1024]{2,0,1:T(1,128)S(1)}, f32[1,16,1024]{2,0,1:T(1,128)S(1)}, u32[]{:S(2)}, u32[]{:S(2)}) %collective-permute-start.1) | collective-permute-done | bytes 65568 | tf_op jit(solution)/shard_map/ppermute | solution.py:31
  37.8 3.8 %collective-permute-start.2 = (f32[8,1,1024]{2,0,1:T(8,128)S(1)}, f32[8,1,1024]{2,0,1:T(8,128)S(1)}, u32[]{:S(2)}, u32[]{:S(2)}) collective-permute-start(f32[8,1,1024]{2,0,1:T(8,128)S(1)} %get-tuple-element.52), channel_id=1, source_target_pairs={{0,1},{1,2},{2,3},{3,4},{4,5},{5,6},{6,7},{7,8},{8,9},{9,10},{10,1... | collective-permute-start | bytes 98312 | tf_op jit(solution)/shard_map/ppermute | solution.py:30
  41.6 2.1 %collective-permute-start.3 = (f32[8,1,1024]{2,0,1:T(8,128)S(1)}, f32[8,1,1024]{2,0,1:T(8,128)S(1)}, u32[]{:S(2)}, u32[]{:S(2)}) collective-permute-start(f32[8,1,1024]{2,0,1:T(8,128)S(1)} %get-tuple-element.53), channel_id=1, source_target_pairs={{1,0},{2,1},{3,2},{4,3},{5,4},{6,5},{7,6},{8,7},{9,8},{10,9},{11,1... | collective-permute-start | bytes 98312 | tf_op jit(solution)/shard_map/ppermute | solution.py:31
  44.3 2.5 %collective-permute-done.3 = f32[8,1,1024]{2,0,1:T(8,128)S(1)} collective-permute-done((f32[8,1,1024]{2,0,1:T(8,128)S(1)}, f32[8,1,1024]{2,0,1:T(8,128)S(1)}, u32[]{:S(2)}, u32[]{:S(2)}) %collective-permute-start.3) | collective-permute-done | bytes 32800 | tf_op jit(solution)/shard_map/ppermute | solution.py:31
  47.3 0.9 convolution_bitcast_fusion.15
  48.6 0.9 fusion.2
  49.8 0.9 convolution_bitcast_fusion.14
  51.0 0.8 fusion.15
  52.4 0.7 fusion.5
  53.1 3.5 %collective-permute-start.4 = (f32[1,16,1024]{2,0,1:T(1,128)S(1)}, f32[1,16,1024]{2,0,1:T(1,128)S(1)}, u32[]{:S(2)}, u32[]{:S(2)}) collective-permute-start(f32[1,16,1024]{2,0,1:T(1,128)S(1)} %get-tuple-element.50), channel_id=1, source_target_pairs={{0,32},{32,64},{64,96},{96,128},{128,160},{160,192},{192,224},{1,3... | collective-permute-start | bytes 196616 | tf_op jit(solution)/shard_map/ppermute | solution.py:30
  56.7 1.3 collective-permute-start.5
  58.0 5.0 %collective-permute-done.5 = f32[1,16,1024]{2,0,1:T(1,128)S(1)} collective-permute-done((f32[1,16,1024]{2,0,1:T(1,128)S(1)}, f32[1,16,1024]{2,0,1:T(1,128)S(1)}, u32[]{:S(2)}, u32[]{:S(2)}) %collective-permute-start.5) | collective-permute-done | bytes 65568 | tf_op jit(solution)/shard_map/ppermute | solution.py:31
  63.5 0.7 broadcast_in_dim.283
  64.3 13.0 %all-to-all-start.1 = ((f32[256,1,2]{2,1,0:T(1,128)}), f32[256,1,2]{2,1,0:T(1,128)S(1)}, u32[]{:S(2)}, u32[]{:S(2)}) async-start(f32[256,1,2]{2,1,0:T(1,128)} %broadcast_in_dim.283), calls=%async_computation.1 | async-start | bytes 262144 | tf_op jit(solution)/shard_map/all_to_all | solution.py:130
  77.2 3.5 %collective-permute-start.6 = (f32[8,1,1024]{2,0,1:T(8,128)S(1)}, f32[8,1,1024]{2,0,1:T(8,128)S(1)}, u32[]{:S(2)}, u32[]{:S(2)}) collective-permute-start(f32[8,1,1024]{2,0,1:T(8,128)S(1)} %get-tuple-element.46), channel_id=1, source_target_pairs={{0,1},{1,2},{2,3},{3,4},{4,5},{5,6},{6,7},{7,8},{8,9},{9,10},{10,1... | collective-permute-start | bytes 98312 | tf_op jit(solution)/shard_map/ppermute | solution.py:30
  80.8 2.1 %collective-permute-start.7 = (f32[8,1,1024]{2,0,1:T(8,128)S(1)}, f32[8,1,1024]{2,0,1:T(8,128)S(1)}, u32[]{:S(2)}, u32[]{:S(2)}) collective-permute-start(f32[8,1,1024]{2,0,1:T(8,128)S(1)} %get-tuple-element.47), channel_id=1, source_target_pairs={{1,0},{2,1},{3,2},{4,3},{5,4},{6,5},{7,6},{8,7},{9,8},{10,9},{11,1... | collective-permute-start | bytes 98312 | tf_op jit(solution)/shard_map/ppermute | solution.py:31
  82.9 7.2 %all-to-all-done.1 = f32[256,1,2]{2,1,0:T(1,128)S(1)} async-done(((f32[256,1,2]{2,1,0:T(1,128)}), f32[256,1,2]{2,1,0:T(1,128)S(1)}, u32[]{:S(2)}, u32[]{:S(2)}) %all-to-all-start.1) | async-done | bytes 2080 | tf_op jit(solution)/shard_map/all_to_all | solution.py:130
  92.9 0.7 fusion.17
  93.7 0.9 fusion.6
  94.5 0.9 convolution_bitcast_fusion.9
  96.1 0.9 convolution_bitcast_fusion.8
  97.9 0.7 fusion.9
  98.7 2.5 %collective-permute-start.8 = (f32[1,16,1024]{2,0,1:T(1,128)S(1)}, f32[1,16,1024]{2,0,1:T(1,128)S(1)}, u32[]{:S(2)}, u32[]{:S(2)}) collective-permute-start(f32[1,16,1024]{2,0,1:T(1,128)S(1)} %get-tuple-element.44), channel_id=1, source_target_pairs={{0,32},{32,64},{64,96},{96,128},{128,160},{160,192},{192,224},{1,3... | collective-permute-start | bytes 196616 | tf_op jit(solution)/shard_map/ppermute | solution.py:30
  101.2 1.3 collective-permute-start.9
  102.5 3.7 %collective-permute-done.9 = f32[1,16,1024]{2,0,1:T(1,128)S(1)} collective-permute-done((f32[1,16,1024]{2,0,1:T(1,128)S(1)}, f32[1,16,1024]{2,0,1:T(1,128)S(1)}, u32[]{:S(2)}, u32[]{:S(2)}) %collective-permute-start.9) | collective-permute-done | bytes 65568 | tf_op jit(solution)/shard_map/ppermute | solution.py:31
  106.8 0.7 broadcast_in_dim.284
  107.6 9.3 %all-to-all-start.2 = ((f32[256,1,3]{2,1,0:T(1,128)}), f32[256,1,3]{2,1,0:T(1,128)S(1)}, u32[]{:S(2)}, u32[]{:S(2)}) async-start(f32[256,1,3]{2,1,0:T(1,128)} %broadcast_in_dim.284), calls=%async_computation.2 | async-start | bytes 262144 | tf_op jit(solution)/shard_map/all_to_all | solution.py:130
  116.9 3.5 %collective-permute-start.10 = (f32[8,1,1024]{2,0,1:T(8,128)S(1)}, f32[8,1,1024]{2,0,1:T(8,128)S(1)}, u32[]{:S(2)}, u32[]{:S(2)}) collective-permute-start(f32[8,1,1024]{2,0,1:T(8,128)S(1)} %get-tuple-element.39), channel_id=1, source_target_pairs={{0,1},{1,2},{2,3},{3,4},{4,5},{5,6},{6,7},{7,8},{8,9},{9,10},{10,1... | collective-permute-start | bytes 98312 | tf_op jit(solution)/shard_map/ppermute | solution.py:30
  120.5 2.2 %collective-permute-start.11 = (f32[8,1,1024]{2,0,1:T(8,128)S(1)}, f32[8,1,1024]{2,0,1:T(8,128)S(1)}, u32[]{:S(2)}, u32[]{:S(2)}) collective-permute-start(f32[8,1,1024]{2,0,1:T(8,128)S(1)} %get-tuple-element.40), channel_id=1, source_target_pairs={{1,0},{2,1},{3,2},{4,3},{5,4},{6,5},{7,6},{8,7},{9,8},{10,9},{11,1... | collective-permute-start | bytes 98312 | tf_op jit(solution)/shard_map/ppermute | solution.py:31
  122.7 7.2 %all-to-all-done.2 = f32[256,1,3]{2,1,0:T(1,128)S(1)} async-done(((f32[256,1,3]{2,1,0:T(1,128)}), f32[256,1,3]{2,1,0:T(1,128)S(1)}, u32[]{:S(2)}, u32[]{:S(2)}) %all-to-all-start.2) | async-done | bytes 3104 | tf_op jit(solution)/shard_map/all_to_all | solution.py:130
  130.1 0.7 fusion.149
  135.4 0.8 fusion.19
  136.1 0.9 fusion.10
  137.6 0.9 convolution_bitcast_fusion.3
  139.1 0.9 convolution_bitcast_fusion.2
  140.4 0.7 fusion.13
  141.1 2.5 %collective-permute-start.12 = (f32[1,16,1024]{2,0,1:T(1,128)S(1)}, f32[1,16,1024]{2,0,1:T(1,128)S(1)}, u32[]{:S(2)}, u32[]{:S(2)}) collective-permute-start(f32[1,16,1024]{2,0,1:T(1,128)S(1)} %get-tuple-element.37), channel_id=1, source_target_pairs={{0,32},{32,64},{64,96},{96,128},{128,160},{160,192},{192,224},{1,3... | collective-permute-start | bytes 196616 | tf_op jit(solution)/shard_map/ppermute | solution.py:30
  143.7 1.3 collective-permute-start.13
  145.0 3.7 %collective-permute-done.13 = f32[1,16,1024]{2,0,1:T(1,128)S(1)} collective-permute-done((f32[1,16,1024]{2,0,1:T(1,128)S(1)}, f32[1,16,1024]{2,0,1:T(1,128)S(1)}, u32[]{:S(2)}, u32[]{:S(2)}) %collective-permute-start.13) | collective-permute-done | bytes 65568 | tf_op jit(solution)/shard_map/ppermute | solution.py:31
  149.3 0.7 broadcast_in_dim.285
  150.0 8.9 %all-to-all-start.3 = ((f32[256,1,3]{2,1,0:T(1,128)}), f32[256,1,3]{2,1,0:T(1,128)S(1)}, u32[]{:S(2)}, u32[]{:S(2)}) async-start(f32[256,1,3]{2,1,0:T(1,128)} %broadcast_in_dim.285), calls=%async_computation.3 | async-start | bytes 262144 | tf_op jit(solution)/shard_map/all_to_all | solution.py:130
  159.0 3.5 %collective-permute-start.14 = (f32[8,1,1024]{2,0,1:T(8,128)S(1)}, f32[8,1,1024]{2,0,1:T(8,128)S(1)}, u32[]{:S(2)}, u32[]{:S(2)}) collective-permute-start(f32[8,1,1024]{2,0,1:T(8,128)S(1)} %get-tuple-element.32), channel_id=1, source_target_pairs={{0,1},{1,2},{2,3},{3,4},{4,5},{5,6},{6,7},{7,8},{8,9},{9,10},{10,1... | collective-permute-start | bytes 98312 | tf_op jit(solution)/shard_map/ppermute | solution.py:30
  162.5 1.9 %collective-permute-start.15 = (f32[8,1,1024]{2,0,1:T(8,128)S(1)}, f32[8,1,1024]{2,0,1:T(8,128)S(1)}, u32[]{:S(2)}, u32[]{:S(2)}) collective-permute-start(f32[8,1,1024]{2,0,1:T(8,128)S(1)} %get-tuple-element.33), channel_id=1, source_target_pairs={{1,0},{2,1},{3,2},{4,3},{5,4},{6,5},{7,6},{8,7},{9,8},{10,9},{11,1... | collective-permute-start | bytes 98312 | tf_op jit(solution)/shard_map/ppermute | solution.py:31
  164.5 7.4 %all-to-all-done.3 = f32[256,1,3]{2,1,0:T(1,128)S(1)} async-done(((f32[256,1,3]{2,1,0:T(1,128)}), f32[256,1,3]{2,1,0:T(1,128)S(1)}, u32[]{:S(2)}, u32[]{:S(2)}) %all-to-all-start.3) | async-done | bytes 3104 | tf_op jit(solution)/shard_map/all_to_all | solution.py:130
  176.7 1.1 copy.374
  177.8 1.1 copy.373
  (96 shorter events, 15.5 us)
Async XLA Ops:
  0.6 18.3 %copy-start.4 = (f32[8]{0:T(128)S(1)}, f32[8]{0:T(128)}, u32[]{:S(2)}) copy-start(f32[8]{0:T(128)} %constant.206.clone) | copy-start | bytes 100
  6.9 16.2 %all-to-all-start = ((f32[32,8,8]{1,2,0:T(8,128)}), f32[32,8,8]{1,2,0:T(8,128)S(1)}, u32[]{:S(2)}, u32[]{:S(2)}) async-start(f32[32,8,8]{1,2,0:T(8,128)} %copy.331), calls=%async_computation | async-start | bytes 262144 | tf_op jit(solution)/shard_map/all_to_all | solution.py:183
  18.0 5.4 %copy-start.5 = (f32[8]{0:T(128)S(1)}, f32[8]{0:T(128)}, u32[]{:S(2)}) copy-start(f32[8]{0:T(128)} %constant.205.clone) | copy-start | bytes 100
  19.5 5.7 %copy-start.1 = (f32[3,8,16,1024]{3,2,1,0:T(8,128)S(1)}, f32[3,8,16,1024]{3,2,1,0:T(8,128)}, u32[]{:S(2)}) copy-start(f32[3,8,16,1024]{3,2,1,0:T(8,128)} %param.11) | copy-start | bytes 4718596
  25.2 0.7 copy-start.3
  25.9 1.8 %copy-start.2 = (f32[8,8,1]{0,1,2:T(8,128)S(1)}, f32[8,8,1]{0,1,2:T(8,128)}, u32[]{:S(2)}) copy-start(f32[8,8,1]{0,1,2:T(8,128)} %constant.232) | copy-start | bytes 772
  28.8 4.9 %collective-permute-start = (f32[1,16,1024]{2,0,1:T(1,128)S(1)}, f32[1,16,1024]{2,0,1:T(1,128)S(1)}, u32[]{:S(2)}, u32[]{:S(2)}) collective-permute-start(f32[1,16,1024]{2,0,1:T(1,128)S(1)} %get-tuple-element.54), channel_id=1, source_target_pairs={{0,32},{32,64},{64,96},{96,128},{128,160},{160,192},{192,224},{1,3... | collective-permute-start | bytes 196616 | tf_op jit(solution)/shard_map/ppermute | solution.py:30
  32.3 5.2 %collective-permute-start.1 = (f32[1,16,1024]{2,0,1:T(1,128)S(1)}, f32[1,16,1024]{2,0,1:T(1,128)S(1)}, u32[]{:S(2)}, u32[]{:S(2)}) collective-permute-start(f32[1,16,1024]{2,0,1:T(1,128)S(1)} %get-tuple-element.55), channel_id=1, source_target_pairs={{32,0},{64,32},{96,64},{128,96},{160,128},{192,160},{224,192},{33,... | collective-permute-start | bytes 196616 | tf_op jit(solution)/shard_map/ppermute | solution.py:31
  37.8 6.5 %collective-permute-start.2 = (f32[8,1,1024]{2,0,1:T(8,128)S(1)}, f32[8,1,1024]{2,0,1:T(8,128)S(1)}, u32[]{:S(2)}, u32[]{:S(2)}) collective-permute-start(f32[8,1,1024]{2,0,1:T(8,128)S(1)} %get-tuple-element.52), channel_id=1, source_target_pairs={{0,1},{1,2},{2,3},{3,4},{4,5},{5,6},{6,7},{7,8},{8,9},{9,10},{10,1... | collective-permute-start | bytes 98312 | tf_op jit(solution)/shard_map/ppermute | solution.py:30
  41.6 5.2 %collective-permute-start.3 = (f32[8,1,1024]{2,0,1:T(8,128)S(1)}, f32[8,1,1024]{2,0,1:T(8,128)S(1)}, u32[]{:S(2)}, u32[]{:S(2)}) collective-permute-start(f32[8,1,1024]{2,0,1:T(8,128)S(1)} %get-tuple-element.53), channel_id=1, source_target_pairs={{1,0},{2,1},{3,2},{4,3},{5,4},{6,5},{7,6},{8,7},{9,8},{10,9},{11,1... | collective-permute-start | bytes 98312 | tf_op jit(solution)/shard_map/ppermute | solution.py:31
  47.0 1.6 copy-start
  53.1 4.9 %collective-permute-start.4 = (f32[1,16,1024]{2,0,1:T(1,128)S(1)}, f32[1,16,1024]{2,0,1:T(1,128)S(1)}, u32[]{:S(2)}, u32[]{:S(2)}) collective-permute-start(f32[1,16,1024]{2,0,1:T(1,128)S(1)} %get-tuple-element.50), channel_id=1, source_target_pairs={{0,32},{32,64},{64,96},{96,128},{128,160},{160,192},{192,224},{1,3... | collective-permute-start | bytes 196616 | tf_op jit(solution)/shard_map/ppermute | solution.py:30
  56.7 6.3 %collective-permute-start.5 = (f32[1,16,1024]{2,0,1:T(1,128)S(1)}, f32[1,16,1024]{2,0,1:T(1,128)S(1)}, u32[]{:S(2)}, u32[]{:S(2)}) collective-permute-start(f32[1,16,1024]{2,0,1:T(1,128)S(1)} %get-tuple-element.51), channel_id=1, source_target_pairs={{32,0},{64,32},{96,64},{128,96},{160,128},{192,160},{224,192},{33,... | collective-permute-start | bytes 196616 | tf_op jit(solution)/shard_map/ppermute | solution.py:31
  64.3 25.9 %all-to-all-start.1 = ((f32[256,1,2]{2,1,0:T(1,128)}), f32[256,1,2]{2,1,0:T(1,128)S(1)}, u32[]{:S(2)}, u32[]{:S(2)}) async-start(f32[256,1,2]{2,1,0:T(1,128)} %broadcast_in_dim.283), calls=%async_computation.1 | async-start | bytes 262144 | tf_op jit(solution)/shard_map/all_to_all | solution.py:130
  77.2 15.1 %collective-permute-start.6 = (f32[8,1,1024]{2,0,1:T(8,128)S(1)}, f32[8,1,1024]{2,0,1:T(8,128)S(1)}, u32[]{:S(2)}, u32[]{:S(2)}) collective-permute-start(f32[8,1,1024]{2,0,1:T(8,128)S(1)} %get-tuple-element.46), channel_id=1, source_target_pairs={{0,1},{1,2},{2,3},{3,4},{4,5},{5,6},{6,7},{7,8},{8,9},{9,10},{10,1... | collective-permute-start | bytes 98312 | tf_op jit(solution)/shard_map/ppermute | solution.py:30
  80.8 11.6 %collective-permute-start.7 = (f32[8,1,1024]{2,0,1:T(8,128)S(1)}, f32[8,1,1024]{2,0,1:T(8,128)S(1)}, u32[]{:S(2)}, u32[]{:S(2)}) collective-permute-start(f32[8,1,1024]{2,0,1:T(8,128)S(1)} %get-tuple-element.47), channel_id=1, source_target_pairs={{1,0},{2,1},{3,2},{4,3},{5,4},{6,5},{7,6},{8,7},{9,8},{10,9},{11,1... | collective-permute-start | bytes 98312 | tf_op jit(solution)/shard_map/ppermute | solution.py:31
  98.7 3.8 %collective-permute-start.8 = (f32[1,16,1024]{2,0,1:T(1,128)S(1)}, f32[1,16,1024]{2,0,1:T(1,128)S(1)}, u32[]{:S(2)}, u32[]{:S(2)}) collective-permute-start(f32[1,16,1024]{2,0,1:T(1,128)S(1)} %get-tuple-element.44), channel_id=1, source_target_pairs={{0,32},{32,64},{64,96},{96,128},{128,160},{160,192},{192,224},{1,3... | collective-permute-start | bytes 196616 | tf_op jit(solution)/shard_map/ppermute | solution.py:30
  101.2 5.0 %collective-permute-start.9 = (f32[1,16,1024]{2,0,1:T(1,128)S(1)}, f32[1,16,1024]{2,0,1:T(1,128)S(1)}, u32[]{:S(2)}, u32[]{:S(2)}) collective-permute-start(f32[1,16,1024]{2,0,1:T(1,128)S(1)} %get-tuple-element.45), channel_id=1, source_target_pairs={{32,0},{64,32},{96,64},{128,96},{160,128},{192,160},{224,192},{33,... | collective-permute-start | bytes 196616 | tf_op jit(solution)/shard_map/ppermute | solution.py:31
  107.6 22.3 %all-to-all-start.2 = ((f32[256,1,3]{2,1,0:T(1,128)}), f32[256,1,3]{2,1,0:T(1,128)S(1)}, u32[]{:S(2)}, u32[]{:S(2)}) async-start(f32[256,1,3]{2,1,0:T(1,128)} %broadcast_in_dim.284), calls=%async_computation.2 | async-start | bytes 262144 | tf_op jit(solution)/shard_map/all_to_all | solution.py:130
  116.9 17.8 %collective-permute-start.10 = (f32[8,1,1024]{2,0,1:T(8,128)S(1)}, f32[8,1,1024]{2,0,1:T(8,128)S(1)}, u32[]{:S(2)}, u32[]{:S(2)}) collective-permute-start(f32[8,1,1024]{2,0,1:T(8,128)S(1)} %get-tuple-element.39), channel_id=1, source_target_pairs={{0,1},{1,2},{2,3},{3,4},{4,5},{5,6},{6,7},{7,8},{8,9},{9,10},{10,1... | collective-permute-start | bytes 98312 | tf_op jit(solution)/shard_map/ppermute | solution.py:30
  120.5 14.3 %collective-permute-start.11 = (f32[8,1,1024]{2,0,1:T(8,128)S(1)}, f32[8,1,1024]{2,0,1:T(8,128)S(1)}, u32[]{:S(2)}, u32[]{:S(2)}) collective-permute-start(f32[8,1,1024]{2,0,1:T(8,128)S(1)} %get-tuple-element.40), channel_id=1, source_target_pairs={{1,0},{2,1},{3,2},{4,3},{5,4},{6,5},{7,6},{8,7},{9,8},{10,9},{11,1... | collective-permute-start | bytes 98312 | tf_op jit(solution)/shard_map/ppermute | solution.py:31
  141.1 3.9 %collective-permute-start.12 = (f32[1,16,1024]{2,0,1:T(1,128)S(1)}, f32[1,16,1024]{2,0,1:T(1,128)S(1)}, u32[]{:S(2)}, u32[]{:S(2)}) collective-permute-start(f32[1,16,1024]{2,0,1:T(1,128)S(1)} %get-tuple-element.37), channel_id=1, source_target_pairs={{0,32},{32,64},{64,96},{96,128},{128,160},{160,192},{192,224},{1,3... | collective-permute-start | bytes 196616 | tf_op jit(solution)/shard_map/ppermute | solution.py:30
  143.7 5.0 %collective-permute-start.13 = (f32[1,16,1024]{2,0,1:T(1,128)S(1)}, f32[1,16,1024]{2,0,1:T(1,128)S(1)}, u32[]{:S(2)}, u32[]{:S(2)}) collective-permute-start(f32[1,16,1024]{2,0,1:T(1,128)S(1)} %get-tuple-element.38), channel_id=1, source_target_pairs={{32,0},{64,32},{96,64},{128,96},{160,128},{192,160},{224,192},{33,... | collective-permute-start | bytes 196616 | tf_op jit(solution)/shard_map/ppermute | solution.py:31
  150.0 21.9 %all-to-all-start.3 = ((f32[256,1,3]{2,1,0:T(1,128)}), f32[256,1,3]{2,1,0:T(1,128)S(1)}, u32[]{:S(2)}, u32[]{:S(2)}) async-start(f32[256,1,3]{2,1,0:T(1,128)} %broadcast_in_dim.285), calls=%async_computation.3 | async-start | bytes 262144 | tf_op jit(solution)/shard_map/all_to_all | solution.py:130
  159.0 17.1 %collective-permute-start.14 = (f32[8,1,1024]{2,0,1:T(8,128)S(1)}, f32[8,1,1024]{2,0,1:T(8,128)S(1)}, u32[]{:S(2)}, u32[]{:S(2)}) collective-permute-start(f32[8,1,1024]{2,0,1:T(8,128)S(1)} %get-tuple-element.32), channel_id=1, source_target_pairs={{0,1},{1,2},{2,3},{3,4},{4,5},{5,6},{6,7},{7,8},{8,9},{9,10},{10,1... | collective-permute-start | bytes 98312 | tf_op jit(solution)/shard_map/ppermute | solution.py:30
  162.5 13.6 %collective-permute-start.15 = (f32[8,1,1024]{2,0,1:T(8,128)S(1)}, f32[8,1,1024]{2,0,1:T(8,128)S(1)}, u32[]{:S(2)}, u32[]{:S(2)}) collective-permute-start(f32[8,1,1024]{2,0,1:T(8,128)S(1)} %get-tuple-element.33), channel_id=1, source_target_pairs={{1,0},{2,1},{3,2},{4,3},{5,4},{6,5},{7,6},{8,7},{9,8},{10,9},{11,1... | collective-permute-start | bytes 98312 | tf_op jit(solution)/shard_map/ppermute | solution.py:31

commit v4 on v3

--- a/solution.py
+++ b/solution.py
@@ -77,8 +77,8 @@
         blocks = grid_field.reshape(extent0 // POLY, POLY, extent1, extent2)
         result = jnp.einsum("ia,xayz->xiyz", matrix, blocks, precision=highest)
     elif axis_at == 1:
-        blocks = grid_field.reshape(extent0, extent1 // POLY, POLY, extent2)
-        result = jnp.einsum("ib,xybz->xyiz", matrix, blocks, precision=highest)
+        tiled_matrix = jnp.kron(jnp.eye(extent1 // POLY, dtype=jnp.float32), matrix)
+        result = jnp.einsum("ib,xbz->xiz", tiled_matrix, grid_field, precision=highest)
     else:
         block_width = 128
         tiled_matrix = jnp.kron(jnp.eye(block_width // POLY, dtype=jnp.float32), matrix)

time: 180 us -> 179 us (level)
  local copies, waits for them, and re-layouts: 13.1 us -> 10.7 us
    transpose x7 -> x0, local copies, waits for them, and re-layouts: 2.16 us -> none  [derive(): result = jnp.einsum('ib,xybz->xyiz', matrix, blocks, precision=highest)]
where the time goes in v4:
time: 179 us; the launch traced here: 178 us
  starting transfers between devices  79.9 us (45%)
  waiting for transfers between devices  44.1 us (25%)
  matrix products  18.9 us (11%)
  other arithmetic  14.3 us (8%)
  local copies, waits for them, and re-layouts  10.7 us (6%)
  between operations  10 us (6%)
    all_to_all x3, starting transfers between devices, mesh_sum(): gathered = lax.all_to_all(spread, axes, 0, 0, tiled=True)  31.2 us
    ppermute x8, starting transfers between devices, with_halo(): before = lax.ppermute(last, axis, up)  26.5 us
    all_to_all x3, waiting for transfers between devices, mesh_sum(): gathered = lax.all_to_all(spread, axes, 0, 0, tiled=True)  21.8 us
    ppermute x8, waiting for transfers between devices, with_halo(): after = lax.ppermute(first, axis, down)  18.7 us
    ppermute x8, starting transfers between devices, with_halo(): after = lax.ppermute(first, axis, down)  13.5 us
    all_to_all x1, starting transfers between devices, project_points(): lax.all_to_all(outgoing, 'span', split_axis=0, concat_axis=0, tiled=True)  8.58 us
    dot_general x7, matrix products, derive(): result = jnp.einsum('ia,xayz->xiyz', matrix, blocks, precision=highest)  6.51 us
    dot_general x7, matrix products, derive(): jnp.einsum('ib,xbz->xiz', tiled_matrix, grid_field, precision=highest)  5.93 us
  transfers between devices with their start and end apart: 20, of which 9 were waited for; matrix products, arithmetic and copies ran while one was open for 4% of the time, Pallas kernels for 0%

profile of v4, /device:TPU:1, one launch (start us, length us, event | category | flops | bytes accessed | tf_op | source)
XLA Modules:
  0.0 177.9 jit_solution(11051533158504585906)
XLA Ops:
  1.3 0.9 convert_reduce_fusion
  2.2 0.7 convert_bitcast_fusion
  3.0 0.8 select_reduce_fusion
  3.8 0.7 broadcast_multiply_fusion.7
  4.5 0.7 maximum_bitcast_fusion
  5.3 0.9 scatter_custom_fusion
  6.2 0.8 copy.305
  6.9 8.6 %all-to-all-start = ((f32[32,8,8]{1,2,0:T(8,128)}), f32[32,8,8]{1,2,0:T(8,128)S(1)}, u32[]{:S(2)}, u32[]{:S(2)}) async-start(f32[32,8,8]{1,2,0:T(8,128)} %copy.305), calls=%async_computation | async-start | bytes 262144 | tf_op jit(solution)/shard_map/all_to_all | solution.py:183
  16.4 0.7 broadcast_multiply_fusion.6
  17.1 0.8 broadcast_multiply_fusion.3
  17.9 0.9 broadcast_multiply_fusion
  19.6 3.5 %all-to-all-done = f32[32,8,8]{1,2,0:T(8,128)S(1)} async-done(((f32[32,8,8]{1,2,0:T(8,128)}), f32[32,8,8]{1,2,0:T(8,128)S(1)}, u32[]{:S(2)}, u32[]{:S(2)}) %all-to-all-start) | async-done | bytes 8224 | tf_op jit(solution)/shard_map/all_to_all | solution.py:183
  23.5 1.7 fusion.20
  25.5 0.7 fusion.46
  26.3 0.8 convolution_bitcast_fusion.12
  27.1 1.2 fusion.1
  28.4 3.5 %collective-permute-start = (f32[1,16,1024]{2,0,1:T(1,128)S(1)}, f32[1,16,1024]{2,0,1:T(1,128)S(1)}, u32[]{:S(2)}, u32[]{:S(2)}) collective-permute-start(f32[1,16,1024]{2,0,1:T(1,128)S(1)} %get-tuple-element.54), channel_id=1, source_target_pairs={{0,32},{32,64},{64,96},{96,128},{128,160},{160,192},{192,224},{1,3... | collective-permute-start | bytes 196616 | tf_op jit(solution)/shard_map/ppermute | solution.py:30
  31.9 1.3 collective-permute-start.1
  33.2 3.9 %collective-permute-done.1 = f32[1,16,1024]{2,0,1:T(1,128)S(1)} collective-permute-done((f32[1,16,1024]{2,0,1:T(1,128)S(1)}, f32[1,16,1024]{2,0,1:T(1,128)S(1)}, u32[]{:S(2)}, u32[]{:S(2)}) %collective-permute-start.1) | collective-permute-done | bytes 65568 | tf_op jit(solution)/shard_map/ppermute | solution.py:31
  37.4 3.8 %collective-permute-start.2 = (f32[8,1,1024]{2,0,1:T(8,128)S(1)}, f32[8,1,1024]{2,0,1:T(8,128)S(1)}, u32[]{:S(2)}, u32[]{:S(2)}) collective-permute-start(f32[8,1,1024]{2,0,1:T(8,128)S(1)} %get-tuple-element.52), channel_id=1, source_target_pairs={{0,1},{1,2},{2,3},{3,4},{4,5},{5,6},{6,7},{7,8},{8,9},{9,10},{10,1... | collective-permute-start | bytes 98312 | tf_op jit(solution)/shard_map/ppermute | solution.py:30
  41.2 2.1 %collective-permute-start.3 = (f32[8,1,1024]{2,0,1:T(8,128)S(1)}, f32[8,1,1024]{2,0,1:T(8,128)S(1)}, u32[]{:S(2)}, u32[]{:S(2)}) collective-permute-start(f32[8,1,1024]{2,0,1:T(8,128)S(1)} %get-tuple-element.53), channel_id=1, source_target_pairs={{1,0},{2,1},{3,2},{4,3},{5,4},{6,5},{7,6},{8,7},{9,8},{10,9},{11,1... | collective-permute-start | bytes 98312 | tf_op jit(solution)/shard_map/ppermute | solution.py:31
  43.9 2.4 %collective-permute-done.3 = f32[8,1,1024]{2,0,1:T(8,128)S(1)} collective-permute-done((f32[8,1,1024]{2,0,1:T(8,128)S(1)}, f32[8,1,1024]{2,0,1:T(8,128)S(1)}, u32[]{:S(2)}, u32[]{:S(2)}) %collective-permute-start.3) | collective-permute-done | bytes 32800 | tf_op jit(solution)/shard_map/ppermute | solution.py:31
  46.9 0.9 fusion.2
  47.8 0.7 fusion.15
  49.1 0.9 fusion.99
  50.6 0.9 fusion.97
  51.5 0.9 fusion.5
  52.5 3.5 %collective-permute-start.4 = (f32[1,16,1024]{2,0,1:T(1,128)S(1)}, f32[1,16,1024]{2,0,1:T(1,128)S(1)}, u32[]{:S(2)}, u32[]{:S(2)}) collective-permute-start(f32[1,16,1024]{2,0,1:T(1,128)S(1)} %get-tuple-element.50), channel_id=1, source_target_pairs={{0,32},{32,64},{64,96},{96,128},{128,160},{160,192},{192,224},{1,3... | collective-permute-start | bytes 196616 | tf_op jit(solution)/shard_map/ppermute | solution.py:30
  56.1 1.3 collective-permute-start.5
  57.4 5.0 %collective-permute-done.5 = f32[1,16,1024]{2,0,1:T(1,128)S(1)} collective-permute-done((f32[1,16,1024]{2,0,1:T(1,128)S(1)}, f32[1,16,1024]{2,0,1:T(1,128)S(1)}, u32[]{:S(2)}, u32[]{:S(2)}) %collective-permute-start.5) | collective-permute-done | bytes 65568 | tf_op jit(solution)/shard_map/ppermute | solution.py:31
  62.9 0.7 broadcast_in_dim.301
  63.6 12.9 %all-to-all-start.1 = ((f32[256,1,2]{2,1,0:T(1,128)}), f32[256,1,2]{2,1,0:T(1,128)S(1)}, u32[]{:S(2)}, u32[]{:S(2)}) async-start(f32[256,1,2]{2,1,0:T(1,128)} %broadcast_in_dim.301), calls=%async_computation.1 | async-start | bytes 262144 | tf_op jit(solution)/shard_map/all_to_all | solution.py:130
  76.6 3.5 %collective-permute-start.6 = (f32[8,1,1024]{2,0,1:T(8,128)S(1)}, f32[8,1,1024]{2,0,1:T(8,128)S(1)}, u32[]{:S(2)}, u32[]{:S(2)}) collective-permute-start(f32[8,1,1024]{2,0,1:T(8,128)S(1)} %get-tuple-element.46), channel_id=1, source_target_pairs={{0,1},{1,2},{2,3},{3,4},{4,5},{5,6},{6,7},{7,8},{8,9},{9,10},{10,1... | collective-permute-start | bytes 98312 | tf_op jit(solution)/shard_map/ppermute | solution.py:30
  80.1 2.1 %collective-permute-start.7 = (f32[8,1,1024]{2,0,1:T(8,128)S(1)}, f32[8,1,1024]{2,0,1:T(8,128)S(1)}, u32[]{:S(2)}, u32[]{:S(2)}) collective-permute-start(f32[8,1,1024]{2,0,1:T(8,128)S(1)} %get-tuple-element.47), channel_id=1, source_target_pairs={{1,0},{2,1},{3,2},{4,3},{5,4},{6,5},{7,6},{8,7},{9,8},{10,9},{11,1... | collective-permute-start | bytes 98312 | tf_op jit(solution)/shard_map/ppermute | solution.py:31
  82.3 7.2 %all-to-all-done.1 = f32[256,1,2]{2,1,0:T(1,128)S(1)} async-done(((f32[256,1,2]{2,1,0:T(1,128)}), f32[256,1,2]{2,1,0:T(1,128)S(1)}, u32[]{:S(2)}, u32[]{:S(2)}) %all-to-all-start.1) | async-done | bytes 2080 | tf_op jit(solution)/shard_map/all_to_all | solution.py:130
  92.3 0.8 fusion.17
  93.0 0.9 fusion.95
  93.9 0.9 fusion.6
  95.9 0.9 fusion.93
  96.8 0.9 fusion.9
  97.8 2.5 %collective-permute-start.8 = (f32[1,16,1024]{2,0,1:T(1,128)S(1)}, f32[1,16,1024]{2,0,1:T(1,128)S(1)}, u32[]{:S(2)}, u32[]{:S(2)}) collective-permute-start(f32[1,16,1024]{2,0,1:T(1,128)S(1)} %get-tuple-element.44), channel_id=1, source_target_pairs={{0,32},{32,64},{64,96},{96,128},{128,160},{160,192},{192,224},{1,3... | collective-permute-start | bytes 196616 | tf_op jit(solution)/shard_map/ppermute | solution.py:30
  100.4 1.3 collective-permute-start.9
  101.7 3.7 %collective-permute-done.9 = f32[1,16,1024]{2,0,1:T(1,128)S(1)} collective-permute-done((f32[1,16,1024]{2,0,1:T(1,128)S(1)}, f32[1,16,1024]{2,0,1:T(1,128)S(1)}, u32[]{:S(2)}, u32[]{:S(2)}) %collective-permute-start.9) | collective-permute-done | bytes 65568 | tf_op jit(solution)/shard_map/ppermute | solution.py:31
  106.0 0.7 broadcast_in_dim.302
  106.7 9.3 %all-to-all-start.2 = ((f32[256,1,3]{2,1,0:T(1,128)}), f32[256,1,3]{2,1,0:T(1,128)S(1)}, u32[]{:S(2)}, u32[]{:S(2)}) async-start(f32[256,1,3]{2,1,0:T(1,128)} %broadcast_in_dim.302), calls=%async_computation.2 | async-start | bytes 262144 | tf_op jit(solution)/shard_map/all_to_all | solution.py:130
  116.1 3.5 %collective-permute-start.10 = (f32[8,1,1024]{2,0,1:T(8,128)S(1)}, f32[8,1,1024]{2,0,1:T(8,128)S(1)}, u32[]{:S(2)}, u32[]{:S(2)}) collective-permute-start(f32[8,1,1024]{2,0,1:T(8,128)S(1)} %get-tuple-element.39), channel_id=1, source_target_pairs={{0,1},{1,2},{2,3},{3,4},{4,5},{5,6},{6,7},{7,8},{8,9},{9,10},{10,1... | collective-permute-start | bytes 98312 | tf_op jit(solution)/shard_map/ppermute | solution.py:30
  119.6 2.2 %collective-permute-start.11 = (f32[8,1,1024]{2,0,1:T(8,128)S(1)}, f32[8,1,1024]{2,0,1:T(8,128)S(1)}, u32[]{:S(2)}, u32[]{:S(2)}) collective-permute-start(f32[8,1,1024]{2,0,1:T(8,128)S(1)} %get-tuple-element.40), channel_id=1, source_target_pairs={{1,0},{2,1},{3,2},{4,3},{5,4},{6,5},{7,6},{8,7},{9,8},{10,9},{11,1... | collective-permute-start | bytes 98312 | tf_op jit(solution)/shard_map/ppermute | solution.py:31
  121.8 7.2 %all-to-all-done.2 = f32[256,1,3]{2,1,0:T(1,128)S(1)} async-done(((f32[256,1,3]{2,1,0:T(1,128)}), f32[256,1,3]{2,1,0:T(1,128)S(1)}, u32[]{:S(2)}, u32[]{:S(2)}) %all-to-all-start.2) | async-done | bytes 3104 | tf_op jit(solution)/shard_map/all_to_all | solution.py:130
  129.3 0.7 fusion.154
  134.5 0.8 fusion.19
  135.3 0.9 fusion.91
  136.2 0.9 fusion.10
  138.2 0.9 fusion.89
  139.1 0.9 fusion.13
  140.1 2.5 %collective-permute-start.12 = (f32[1,16,1024]{2,0,1:T(1,128)S(1)}, f32[1,16,1024]{2,0,1:T(1,128)S(1)}, u32[]{:S(2)}, u32[]{:S(2)}) collective-permute-start(f32[1,16,1024]{2,0,1:T(1,128)S(1)} %get-tuple-element.37), channel_id=1, source_target_pairs={{0,32},{32,64},{64,96},{96,128},{128,160},{160,192},{192,224},{1,3... | collective-permute-start | bytes 196616 | tf_op jit(solution)/shard_map/ppermute | solution.py:30
  142.7 1.3 collective-permute-start.13
  144.0 3.7 %collective-permute-done.13 = f32[1,16,1024]{2,0,1:T(1,128)S(1)} collective-permute-done((f32[1,16,1024]{2,0,1:T(1,128)S(1)}, f32[1,16,1024]{2,0,1:T(1,128)S(1)}, u32[]{:S(2)}, u32[]{:S(2)}) %collective-permute-start.13) | collective-permute-done | bytes 65568 | tf_op jit(solution)/shard_map/ppermute | solution.py:31
  148.3 0.7 broadcast_in_dim.303
  149.0 9.0 %all-to-all-start.3 = ((f32[256,1,3]{2,1,0:T(1,128)}), f32[256,1,3]{2,1,0:T(1,128)S(1)}, u32[]{:S(2)}, u32[]{:S(2)}) async-start(f32[256,1,3]{2,1,0:T(1,128)} %broadcast_in_dim.303), calls=%async_computation.3 | async-start | bytes 262144 | tf_op jit(solution)/shard_map/all_to_all | solution.py:130
  158.0 3.5 %collective-permute-start.14 = (f32[8,1,1024]{2,0,1:T(8,128)S(1)}, f32[8,1,1024]{2,0,1:T(8,128)S(1)}, u32[]{:S(2)}, u32[]{:S(2)}) collective-permute-start(f32[8,1,1024]{2,0,1:T(8,128)S(1)} %get-tuple-element.32), channel_id=1, source_target_pairs={{0,1},{1,2},{2,3},{3,4},{4,5},{5,6},{6,7},{7,8},{8,9},{9,10},{10,1... | collective-permute-start | bytes 98312 | tf_op jit(solution)/shard_map/ppermute | solution.py:30
  161.5 1.9 %collective-permute-start.15 = (f32[8,1,1024]{2,0,1:T(8,128)S(1)}, f32[8,1,1024]{2,0,1:T(8,128)S(1)}, u32[]{:S(2)}, u32[]{:S(2)}) collective-permute-start(f32[8,1,1024]{2,0,1:T(8,128)S(1)} %get-tuple-element.33), channel_id=1, source_target_pairs={{1,0},{2,1},{3,2},{4,3},{5,4},{6,5},{7,6},{8,7},{9,8},{10,9},{11,1... | collective-permute-start | bytes 98312 | tf_op jit(solution)/shard_map/ppermute | solution.py:31
  163.4 7.4 %all-to-all-done.3 = f32[256,1,3]{2,1,0:T(1,128)S(1)} async-done(((f32[256,1,3]{2,1,0:T(1,128)}), f32[256,1,3]{2,1,0:T(1,128)S(1)}, u32[]{:S(2)}, u32[]{:S(2)}) %all-to-all-start.3) | async-done | bytes 3104 | tf_op jit(solution)/shard_map/all_to_all | solution.py:130
  175.7 1.1 copy.346
  176.8 1.1 copy.345
  (90 shorter events, 13.8 us)
Async XLA Ops:
  0.6 18.3 %copy-start.3 = (f32[8]{0:T(128)S(1)}, f32[8]{0:T(128)}, u32[]{:S(2)}) copy-start(f32[8]{0:T(128)} %constant.206.clone) | copy-start | bytes 100
  6.9 16.2 %all-to-all-start = ((f32[32,8,8]{1,2,0:T(8,128)}), f32[32,8,8]{1,2,0:T(8,128)S(1)}, u32[]{:S(2)}, u32[]{:S(2)}) async-start(f32[32,8,8]{1,2,0:T(8,128)} %copy.305), calls=%async_computation | async-start | bytes 262144 | tf_op jit(solution)/shard_map/all_to_all | solution.py:183
  17.9 5.5 %copy-start.4 = (f32[8]{0:T(128)S(1)}, f32[8]{0:T(128)}, u32[]{:S(2)}) copy-start(f32[8]{0:T(128)} %constant.205.clone) | copy-start | bytes 100
  19.6 5.7 %copy-start.1 = (f32[3,8,16,1024]{3,2,1,0:T(8,128)S(1)}, f32[3,8,16,1024]{3,2,1,0:T(8,128)}, u32[]{:S(2)}) copy-start(f32[3,8,16,1024]{3,2,1,0:T(8,128)} %param.11) | copy-start | bytes 4718596
  25.4 1.6 copy-start.2
  28.4 4.9 %collective-permute-start = (f32[1,16,1024]{2,0,1:T(1,128)S(1)}, f32[1,16,1024]{2,0,1:T(1,128)S(1)}, u32[]{:S(2)}, u32[]{:S(2)}) collective-permute-start(f32[1,16,1024]{2,0,1:T(1,128)S(1)} %get-tuple-element.54), channel_id=1, source_target_pairs={{0,32},{32,64},{64,96},{96,128},{128,160},{160,192},{192,224},{1,3... | collective-permute-start | bytes 196616 | tf_op jit(solution)/shard_map/ppermute | solution.py:30
  31.9 5.2 %collective-permute-start.1 = (f32[1,16,1024]{2,0,1:T(1,128)S(1)}, f32[1,16,1024]{2,0,1:T(1,128)S(1)}, u32[]{:S(2)}, u32[]{:S(2)}) collective-permute-start(f32[1,16,1024]{2,0,1:T(1,128)S(1)} %get-tuple-element.55), channel_id=1, source_target_pairs={{32,0},{64,32},{96,64},{128,96},{160,128},{192,160},{224,192},{33,... | collective-permute-start | bytes 196616 | tf_op jit(solution)/shard_map/ppermute | solution.py:31
  37.4 6.6 %collective-permute-start.2 = (f32[8,1,1024]{2,0,1:T(8,128)S(1)}, f32[8,1,1024]{2,0,1:T(8,128)S(1)}, u32[]{:S(2)}, u32[]{:S(2)}) collective-permute-start(f32[8,1,1024]{2,0,1:T(8,128)S(1)} %get-tuple-element.52), channel_id=1, source_target_pairs={{0,1},{1,2},{2,3},{3,4},{4,5},{5,6},{6,7},{7,8},{8,9},{9,10},{10,1... | collective-permute-start | bytes 98312 | tf_op jit(solution)/shard_map/ppermute | solution.py:30
  41.2 5.2 %collective-permute-start.3 = (f32[8,1,1024]{2,0,1:T(8,128)S(1)}, f32[8,1,1024]{2,0,1:T(8,128)S(1)}, u32[]{:S(2)}, u32[]{:S(2)}) collective-permute-start(f32[8,1,1024]{2,0,1:T(8,128)S(1)} %get-tuple-element.53), channel_id=1, source_target_pairs={{1,0},{2,1},{3,2},{4,3},{5,4},{6,5},{7,6},{8,7},{9,8},{10,9},{11,1... | collective-permute-start | bytes 98312 | tf_op jit(solution)/shard_map/ppermute | solution.py:31
  43.9 3.0 %copy-start = (f32[8,16,1024]{2,1,0:T(8,128)S(1)}, f32[8,16,1024]{2,1,0:T(8,128)}, u32[]{:S(2)}) copy-start(f32[8,16,1024]{2,1,0:T(8,128)} %param.12) | copy-start | bytes 1572868
  52.5 4.9 %collective-permute-start.4 = (f32[1,16,1024]{2,0,1:T(1,128)S(1)}, f32[1,16,1024]{2,0,1:T(1,128)S(1)}, u32[]{:S(2)}, u32[]{:S(2)}) collective-permute-start(f32[1,16,1024]{2,0,1:T(1,128)S(1)} %get-tuple-element.50), channel_id=1, source_target_pairs={{0,32},{32,64},{64,96},{96,128},{128,160},{160,192},{192,224},{1,3... | collective-permute-start | bytes 196616 | tf_op jit(solution)/shard_map/ppermute | solution.py:30
  56.1 6.3 %collective-permute-start.5 = (f32[1,16,1024]{2,0,1:T(1,128)S(1)}, f32[1,16,1024]{2,0,1:T(1,128)S(1)}, u32[]{:S(2)}, u32[]{:S(2)}) collective-permute-start(f32[1,16,1024]{2,0,1:T(1,128)S(1)} %get-tuple-element.51), channel_id=1, source_target_pairs={{32,0},{64,32},{96,64},{128,96},{160,128},{192,160},{224,192},{33,... | collective-permute-start | bytes 196616 | tf_op jit(solution)/shard_map/ppermute | solution.py:31
  63.6 25.9 %all-to-all-start.1 = ((f32[256,1,2]{2,1,0:T(1,128)}), f32[256,1,2]{2,1,0:T(1,128)S(1)}, u32[]{:S(2)}, u32[]{:S(2)}) async-start(f32[256,1,2]{2,1,0:T(1,128)} %broadcast_in_dim.301), calls=%async_computation.1 | async-start | bytes 262144 | tf_op jit(solution)/shard_map/all_to_all | solution.py:130
  76.6 15.1 %collective-permute-start.6 = (f32[8,1,1024]{2,0,1:T(8,128)S(1)}, f32[8,1,1024]{2,0,1:T(8,128)S(1)}, u32[]{:S(2)}, u32[]{:S(2)}) collective-permute-start(f32[8,1,1024]{2,0,1:T(8,128)S(1)} %get-tuple-element.46), channel_id=1, source_target_pairs={{0,1},{1,2},{2,3},{3,4},{4,5},{5,6},{6,7},{7,8},{8,9},{9,10},{10,1... | collective-permute-start | bytes 98312 | tf_op jit(solution)/shard_map/ppermute | solution.py:30
  80.1 11.6 %collective-permute-start.7 = (f32[8,1,1024]{2,0,1:T(8,128)S(1)}, f32[8,1,1024]{2,0,1:T(8,128)S(1)}, u32[]{:S(2)}, u32[]{:S(2)}) collective-permute-start(f32[8,1,1024]{2,0,1:T(8,128)S(1)} %get-tuple-element.47), channel_id=1, source_target_pairs={{1,0},{2,1},{3,2},{4,3},{5,4},{6,5},{7,6},{8,7},{9,8},{10,9},{11,1... | collective-permute-start | bytes 98312 | tf_op jit(solution)/shard_map/ppermute | solution.py:31
  97.8 3.9 %collective-permute-start.8 = (f32[1,16,1024]{2,0,1:T(1,128)S(1)}, f32[1,16,1024]{2,0,1:T(1,128)S(1)}, u32[]{:S(2)}, u32[]{:S(2)}) collective-permute-start(f32[1,16,1024]{2,0,1:T(1,128)S(1)} %get-tuple-element.44), channel_id=1, source_target_pairs={{0,32},{32,64},{64,96},{96,128},{128,160},{160,192},{192,224},{1,3... | collective-permute-start | bytes 196616 | tf_op jit(solution)/shard_map/ppermute | solution.py:30
  100.4 5.0 %collective-permute-start.9 = (f32[1,16,1024]{2,0,1:T(1,128)S(1)}, f32[1,16,1024]{2,0,1:T(1,128)S(1)}, u32[]{:S(2)}, u32[]{:S(2)}) collective-permute-start(f32[1,16,1024]{2,0,1:T(1,128)S(1)} %get-tuple-element.45), channel_id=1, source_target_pairs={{32,0},{64,32},{96,64},{128,96},{160,128},{192,160},{224,192},{33,... | collective-permute-start | bytes 196616 | tf_op jit(solution)/shard_map/ppermute | solution.py:31
  106.7 22.3 %all-to-all-start.2 = ((f32[256,1,3]{2,1,0:T(1,128)}), f32[256,1,3]{2,1,0:T(1,128)S(1)}, u32[]{:S(2)}, u32[]{:S(2)}) async-start(f32[256,1,3]{2,1,0:T(1,128)} %broadcast_in_dim.302), calls=%async_computation.2 | async-start | bytes 262144 | tf_op jit(solution)/shard_map/all_to_all | solution.py:130
  116.1 17.8 %collective-permute-start.10 = (f32[8,1,1024]{2,0,1:T(8,128)S(1)}, f32[8,1,1024]{2,0,1:T(8,128)S(1)}, u32[]{:S(2)}, u32[]{:S(2)}) collective-permute-start(f32[8,1,1024]{2,0,1:T(8,128)S(1)} %get-tuple-element.39), channel_id=1, source_target_pairs={{0,1},{1,2},{2,3},{3,4},{4,5},{5,6},{6,7},{7,8},{8,9},{9,10},{10,1... | collective-permute-start | bytes 98312 | tf_op jit(solution)/shard_map/ppermute | solution.py:30
  119.6 14.3 %collective-permute-start.11 = (f32[8,1,1024]{2,0,1:T(8,128)S(1)}, f32[8,1,1024]{2,0,1:T(8,128)S(1)}, u32[]{:S(2)}, u32[]{:S(2)}) collective-permute-start(f32[8,1,1024]{2,0,1:T(8,128)S(1)} %get-tuple-element.40), channel_id=1, source_target_pairs={{1,0},{2,1},{3,2},{4,3},{5,4},{6,5},{7,6},{8,7},{9,8},{10,9},{11,1... | collective-permute-start | bytes 98312 | tf_op jit(solution)/shard_map/ppermute | solution.py:31
  140.1 3.9 %collective-permute-start.12 = (f32[1,16,1024]{2,0,1:T(1,128)S(1)}, f32[1,16,1024]{2,0,1:T(1,128)S(1)}, u32[]{:S(2)}, u32[]{:S(2)}) collective-permute-start(f32[1,16,1024]{2,0,1:T(1,128)S(1)} %get-tuple-element.37), channel_id=1, source_target_pairs={{0,32},{32,64},{64,96},{96,128},{128,160},{160,192},{192,224},{1,3... | collective-permute-start | bytes 196616 | tf_op jit(solution)/shard_map/ppermute | solution.py:30
  142.7 5.0 %collective-permute-start.13 = (f32[1,16,1024]{2,0,1:T(1,128)S(1)}, f32[1,16,1024]{2,0,1:T(1,128)S(1)}, u32[]{:S(2)}, u32[]{:S(2)}) collective-permute-start(f32[1,16,1024]{2,0,1:T(1,128)S(1)} %get-tuple-element.38), channel_id=1, source_target_pairs={{32,0},{64,32},{96,64},{128,96},{160,128},{192,160},{224,192},{33,... | collective-permute-start | bytes 196616 | tf_op jit(solution)/shard_map/ppermute | solution.py:31
  149.0 21.9 %all-to-all-start.3 = ((f32[256,1,3]{2,1,0:T(1,128)}), f32[256,1,3]{2,1,0:T(1,128)S(1)}, u32[]{:S(2)}, u32[]{:S(2)}) async-start(f32[256,1,3]{2,1,0:T(1,128)} %broadcast_in_dim.303), calls=%async_computation.3 | async-start | bytes 262144 | tf_op jit(solution)/shard_map/all_to_all | solution.py:130
  158.0 17.1 %collective-permute-start.14 = (f32[8,1,1024]{2,0,1:T(8,128)S(1)}, f32[8,1,1024]{2,0,1:T(8,128)S(1)}, u32[]{:S(2)}, u32[]{:S(2)}) collective-permute-start(f32[8,1,1024]{2,0,1:T(8,128)S(1)} %get-tuple-element.32), channel_id=1, source_target_pairs={{0,1},{1,2},{2,3},{3,4},{4,5},{5,6},{6,7},{7,8},{8,9},{9,10},{10,1... | collective-permute-start | bytes 98312 | tf_op jit(solution)/shard_map/ppermute | solution.py:30
  161.5 13.6 %collective-permute-start.15 = (f32[8,1,1024]{2,0,1:T(8,128)S(1)}, f32[8,1,1024]{2,0,1:T(8,128)S(1)}, u32[]{:S(2)}, u32[]{:S(2)}) collective-permute-start(f32[8,1,1024]{2,0,1:T(8,128)S(1)} %get-tuple-element.33), channel_id=1, source_target_pairs={{1,0},{2,1},{3,2},{4,3},{5,4},{6,5},{7,6},{8,7},{9,8},{10,9},{11,1... | collective-permute-start | bytes 98312 | tf_op jit(solution)/shard_map/ppermute | solution.py:31

commit v5 on v4

--- a/solution.py
+++ b/solution.py
@@ -179,7 +179,7 @@
     ranks = jnp.sum(earlier.astype(jnp.int32), axis=1)
     slot_at = target * capacity + ranks
     outgoing = jnp.zeros((spans * capacity, 8), jnp.float32).at[slot_at].set(payload)
-    outgoing = outgoing.reshape(spans, capacity, 8)
+    outgoing = outgoing.reshape(spans, capacity * 8)
     arrived = lax.all_to_all(outgoing, "span", split_axis=0, concat_axis=0, tiled=True).reshape(
         spans * capacity, 8
     )

time: 179 us -> 181 us (1.011)
  no operation moved by 1% of the time
where the time goes in v5:
time: 181 us; the launch traced here: 180 us
  starting transfers between devices  80.2 us (44%)
  waiting for transfers between devices  43.4 us (24%)
  matrix products  18.9 us (10%)
  other arithmetic  15.6 us (9%)
  local copies, waits for them, and re-layouts  11.6 us (6%)
  between operations  9.98 us (6%)
    all_to_all x3, starting transfers between devices, mesh_sum(): gathered = lax.all_to_all(spread, axes, 0, 0, tiled=True)  31.3 us
    ppermute x8, starting transfers between devices, with_halo(): before = lax.ppermute(last, axis, up)  26.8 us
    all_to_all x3, waiting for transfers between devices, mesh_sum(): gathered = lax.all_to_all(spread, axes, 0, 0, tiled=True)  21.8 us
    ppermute x8, waiting for transfers between devices, with_halo(): after = lax.ppermute(first, axis, down)  18.7 us
    ppermute x8, starting transfers between devices, with_halo(): after = lax.ppermute(first, axis, down)  13.5 us
    all_to_all x1, starting transfers between devices, project_points(): lax.all_to_all(outgoing, 'span', split_axis=0, concat_axis=0, tiled=True)  8.58 us
    dot_general x7, matrix products, derive(): result = jnp.einsum('ia,xayz->xiyz', matrix, blocks, precision=highest)  6.52 us
    dot_general x7, matrix products, derive(): jnp.einsum('ib,xbz->xiz', tiled_matrix, grid_field, precision=highest)  5.93 us
  transfers between devices with their start and end apart: 20, of which 9 were waited for; matrix products, arithmetic and copies ran while one was open for 4% of the time, Pallas kernels for 0%

profile of v5, /device:TPU:1, one launch (start us, length us, event | category | flops | bytes accessed | tf_op | source)
XLA Modules:
  0.0 179.6 jit_solution(18179112490942267809)
XLA Ops:
  1.3 0.9 convert_reduce_fusion
  2.2 0.7 convert_bitcast_fusion
  3.0 0.8 select_reduce_fusion
  3.8 0.7 broadcast_multiply_fusion.7
  4.5 0.7 maximum_bitcast_fusion
  5.3 0.9 scatter_custom_fusion
  6.2 0.7 all_to_all.18
  6.9 8.6 %all-to-all-start = ((f32[32,1,64]{2,1,0:T(1,128)}), f32[32,1,64]{2,1,0:T(1,128)S(1)}, u32[]{:S(2)}, u32[]{:S(2)}) async-start(f32[32,1,64]{2,1,0:T(1,128)} %bitcast.6), calls=%async_computation | async-start | bytes 32768 | tf_op jit(solution)/shard_map/all_to_all | solution.py:183
  16.3 0.7 broadcast_multiply_fusion.6
  17.0 0.8 broadcast_multiply_fusion.3
  17.8 0.9 broadcast_multiply_fusion
  19.5 2.8 %all-to-all-done = f32[32,1,64]{2,1,0:T(1,128)S(1)} async-done(((f32[32,1,64]{2,1,0:T(1,128)}), f32[32,1,64]{2,1,0:T(1,128)S(1)}, u32[]{:S(2)}, u32[]{:S(2)}) %all-to-all-start) | async-done | bytes 8224 | tf_op jit(solution)/shard_map/all_to_all | solution.py:183
  22.9 0.7 reduce.20
  25.0 1.7 fusion.20
  26.9 0.7 fusion.46
  27.7 0.8 convolution_bitcast_fusion.12
  28.5 1.2 fusion.1
  29.8 3.5 %collective-permute-start = (f32[1,16,1024]{2,0,1:T(1,128)S(1)}, f32[1,16,1024]{2,0,1:T(1,128)S(1)}, u32[]{:S(2)}, u32[]{:S(2)}) collective-permute-start(f32[1,16,1024]{2,0,1:T(1,128)S(1)} %get-tuple-element.56), channel_id=1, source_target_pairs={{0,32},{32,64},{64,96},{96,128},{128,160},{160,192},{192,224},{1,3... | collective-permute-start | bytes 196616 | tf_op jit(solution)/shard_map/ppermute | solution.py:30
  33.3 1.3 collective-permute-start.1
  34.7 3.9 %collective-permute-done.1 = f32[1,16,1024]{2,0,1:T(1,128)S(1)} collective-permute-done((f32[1,16,1024]{2,0,1:T(1,128)S(1)}, f32[1,16,1024]{2,0,1:T(1,128)S(1)}, u32[]{:S(2)}, u32[]{:S(2)}) %collective-permute-start.1) | collective-permute-done | bytes 65568 | tf_op jit(solution)/shard_map/ppermute | solution.py:31
  38.8 4.0 %collective-permute-start.2 = (f32[8,1,1024]{2,0,1:T(8,128)S(1)}, f32[8,1,1024]{2,0,1:T(8,128)S(1)}, u32[]{:S(2)}, u32[]{:S(2)}) collective-permute-start(f32[8,1,1024]{2,0,1:T(8,128)S(1)} %get-tuple-element.54), channel_id=1, source_target_pairs={{0,1},{1,2},{2,3},{3,4},{4,5},{5,6},{6,7},{7,8},{8,9},{9,10},{10,1... | collective-permute-start | bytes 98312 | tf_op jit(solution)/shard_map/ppermute | solution.py:30
  42.8 2.1 %collective-permute-start.3 = (f32[8,1,1024]{2,0,1:T(8,128)S(1)}, f32[8,1,1024]{2,0,1:T(8,128)S(1)}, u32[]{:S(2)}, u32[]{:S(2)}) collective-permute-start(f32[8,1,1024]{2,0,1:T(8,128)S(1)} %get-tuple-element.55), channel_id=1, source_target_pairs={{1,0},{2,1},{3,2},{4,3},{5,4},{6,5},{7,6},{8,7},{9,8},{10,9},{11,1... | collective-permute-start | bytes 98312 | tf_op jit(solution)/shard_map/ppermute | solution.py:31
  45.6 2.4 %collective-permute-done.3 = f32[8,1,1024]{2,0,1:T(8,128)S(1)} collective-permute-done((f32[8,1,1024]{2,0,1:T(8,128)S(1)}, f32[8,1,1024]{2,0,1:T(8,128)S(1)}, u32[]{:S(2)}, u32[]{:S(2)}) %collective-permute-start.3) | collective-permute-done | bytes 32800 | tf_op jit(solution)/shard_map/ppermute | solution.py:31
  48.6 0.9 fusion.2
  49.4 0.7 fusion.15
  50.8 0.9 fusion.99
  52.3 0.9 fusion.97
  53.1 0.9 fusion.5
  54.1 3.6 %collective-permute-start.4 = (f32[1,16,1024]{2,0,1:T(1,128)S(1)}, f32[1,16,1024]{2,0,1:T(1,128)S(1)}, u32[]{:S(2)}, u32[]{:S(2)}) collective-permute-start(f32[1,16,1024]{2,0,1:T(1,128)S(1)} %get-tuple-element.52), channel_id=1, source_target_pairs={{0,32},{32,64},{64,96},{96,128},{128,160},{160,192},{192,224},{1,3... | collective-permute-start | bytes 196616 | tf_op jit(solution)/shard_map/ppermute | solution.py:30
  57.7 1.3 collective-permute-start.5
  59.0 5.0 %collective-permute-done.5 = f32[1,16,1024]{2,0,1:T(1,128)S(1)} collective-permute-done((f32[1,16,1024]{2,0,1:T(1,128)S(1)}, f32[1,16,1024]{2,0,1:T(1,128)S(1)}, u32[]{:S(2)}, u32[]{:S(2)}) %collective-permute-start.5) | collective-permute-done | bytes 65568 | tf_op jit(solution)/shard_map/ppermute | solution.py:31
  64.5 0.7 broadcast_in_dim.301
  65.2 13.0 %all-to-all-start.1 = ((f32[256,1,2]{2,1,0:T(1,128)}), f32[256,1,2]{2,1,0:T(1,128)S(1)}, u32[]{:S(2)}, u32[]{:S(2)}) async-start(f32[256,1,2]{2,1,0:T(1,128)} %broadcast_in_dim.301), calls=%async_computation.1 | async-start | bytes 262144 | tf_op jit(solution)/shard_map/all_to_all | solution.py:130
  78.3 3.5 %collective-permute-start.6 = (f32[8,1,1024]{2,0,1:T(8,128)S(1)}, f32[8,1,1024]{2,0,1:T(8,128)S(1)}, u32[]{:S(2)}, u32[]{:S(2)}) collective-permute-start(f32[8,1,1024]{2,0,1:T(8,128)S(1)} %get-tuple-element.48), channel_id=1, source_target_pairs={{0,1},{1,2},{2,3},{3,4},{4,5},{5,6},{6,7},{7,8},{8,9},{9,10},{10,1... | collective-permute-start | bytes 98312 | tf_op jit(solution)/shard_map/ppermute | solution.py:30
  81.8 2.1 %collective-permute-start.7 = (f32[8,1,1024]{2,0,1:T(8,128)S(1)}, f32[8,1,1024]{2,0,1:T(8,128)S(1)}, u32[]{:S(2)}, u32[]{:S(2)}) collective-permute-start(f32[8,1,1024]{2,0,1:T(8,128)S(1)} %get-tuple-element.49), channel_id=1, source_target_pairs={{1,0},{2,1},{3,2},{4,3},{5,4},{6,5},{7,6},{8,7},{9,8},{10,9},{11,1... | collective-permute-start | bytes 98312 | tf_op jit(solution)/shard_map/ppermute | solution.py:31
  84.0 7.2 %all-to-all-done.1 = f32[256,1,2]{2,1,0:T(1,128)S(1)} async-done(((f32[256,1,2]{2,1,0:T(1,128)}), f32[256,1,2]{2,1,0:T(1,128)S(1)}, u32[]{:S(2)}, u32[]{:S(2)}) %all-to-all-start.1) | async-done | bytes 2080 | tf_op jit(solution)/shard_map/all_to_all | solution.py:130
  94.0 0.8 fusion.17
  94.7 0.9 fusion.95
  95.6 0.9 fusion.6
  97.6 0.9 fusion.93
  98.5 0.9 fusion.9
  99.5 2.5 %collective-permute-start.8 = (f32[1,16,1024]{2,0,1:T(1,128)S(1)}, f32[1,16,1024]{2,0,1:T(1,128)S(1)}, u32[]{:S(2)}, u32[]{:S(2)}) collective-permute-start(f32[1,16,1024]{2,0,1:T(1,128)S(1)} %get-tuple-element.46), channel_id=1, source_target_pairs={{0,32},{32,64},{64,96},{96,128},{128,160},{160,192},{192,224},{1,3... | collective-permute-start | bytes 196616 | tf_op jit(solution)/shard_map/ppermute | solution.py:30
  102.1 1.3 collective-permute-start.9
  103.4 3.7 %collective-permute-done.9 = f32[1,16,1024]{2,0,1:T(1,128)S(1)} collective-permute-done((f32[1,16,1024]{2,0,1:T(1,128)S(1)}, f32[1,16,1024]{2,0,1:T(1,128)S(1)}, u32[]{:S(2)}, u32[]{:S(2)}) %collective-permute-start.9) | collective-permute-done | bytes 65568 | tf_op jit(solution)/shard_map/ppermute | solution.py:31
  107.7 0.7 broadcast_in_dim.302
  108.4 9.3 %all-to-all-start.2 = ((f32[256,1,3]{2,1,0:T(1,128)}), f32[256,1,3]{2,1,0:T(1,128)S(1)}, u32[]{:S(2)}, u32[]{:S(2)}) async-start(f32[256,1,3]{2,1,0:T(1,128)} %broadcast_in_dim.302), calls=%async_computation.2 | async-start | bytes 262144 | tf_op jit(solution)/shard_map/all_to_all | solution.py:130
  117.8 3.5 %collective-permute-start.10 = (f32[8,1,1024]{2,0,1:T(8,128)S(1)}, f32[8,1,1024]{2,0,1:T(8,128)S(1)}, u32[]{:S(2)}, u32[]{:S(2)}) collective-permute-start(f32[8,1,1024]{2,0,1:T(8,128)S(1)} %get-tuple-element.41), channel_id=1, source_target_pairs={{0,1},{1,2},{2,3},{3,4},{4,5},{5,6},{6,7},{7,8},{8,9},{9,10},{10,1... | collective-permute-start | bytes 98312 | tf_op jit(solution)/shard_map/ppermute | solution.py:30
  121.3 2.2 %collective-permute-start.11 = (f32[8,1,1024]{2,0,1:T(8,128)S(1)}, f32[8,1,1024]{2,0,1:T(8,128)S(1)}, u32[]{:S(2)}, u32[]{:S(2)}) collective-permute-start(f32[8,1,1024]{2,0,1:T(8,128)S(1)} %get-tuple-element.42), channel_id=1, source_target_pairs={{1,0},{2,1},{3,2},{4,3},{5,4},{6,5},{7,6},{8,7},{9,8},{10,9},{11,1... | collective-permute-start | bytes 98312 | tf_op jit(solution)/shard_map/ppermute | solution.py:31
  123.5 7.2 %all-to-all-done.2 = f32[256,1,3]{2,1,0:T(1,128)S(1)} async-done(((f32[256,1,3]{2,1,0:T(1,128)}), f32[256,1,3]{2,1,0:T(1,128)S(1)}, u32[]{:S(2)}, u32[]{:S(2)}) %all-to-all-start.2) | async-done | bytes 3104 | tf_op jit(solution)/shard_map/all_to_all | solution.py:130
  136.2 0.8 fusion.19
  137.0 0.9 fusion.91
  137.9 0.9 fusion.10
  139.9 0.9 fusion.89
  140.8 0.9 fusion.13
  141.8 2.5 %collective-permute-start.12 = (f32[1,16,1024]{2,0,1:T(1,128)S(1)}, f32[1,16,1024]{2,0,1:T(1,128)S(1)}, u32[]{:S(2)}, u32[]{:S(2)}) collective-permute-start(f32[1,16,1024]{2,0,1:T(1,128)S(1)} %get-tuple-element.39), channel_id=1, source_target_pairs={{0,32},{32,64},{64,96},{96,128},{128,160},{160,192},{192,224},{1,3... | collective-permute-start | bytes 196616 | tf_op jit(solution)/shard_map/ppermute | solution.py:30
  144.4 1.3 collective-permute-start.13
  145.7 3.7 %collective-permute-done.13 = f32[1,16,1024]{2,0,1:T(1,128)S(1)} collective-permute-done((f32[1,16,1024]{2,0,1:T(1,128)S(1)}, f32[1,16,1024]{2,0,1:T(1,128)S(1)}, u32[]{:S(2)}, u32[]{:S(2)}) %collective-permute-start.13) | collective-permute-done | bytes 65568 | tf_op jit(solution)/shard_map/ppermute | solution.py:31
  150.0 0.7 broadcast_in_dim.303
  150.7 8.9 %all-to-all-start.3 = ((f32[256,1,3]{2,1,0:T(1,128)}), f32[256,1,3]{2,1,0:T(1,128)S(1)}, u32[]{:S(2)}, u32[]{:S(2)}) async-start(f32[256,1,3]{2,1,0:T(1,128)} %broadcast_in_dim.303), calls=%async_computation.3 | async-start | bytes 262144 | tf_op jit(solution)/shard_map/all_to_all | solution.py:130
  159.7 3.5 %collective-permute-start.14 = (f32[8,1,1024]{2,0,1:T(8,128)S(1)}, f32[8,1,1024]{2,0,1:T(8,128)S(1)}, u32[]{:S(2)}, u32[]{:S(2)}) collective-permute-start(f32[8,1,1024]{2,0,1:T(8,128)S(1)} %get-tuple-element.34), channel_id=1, source_target_pairs={{0,1},{1,2},{2,3},{3,4},{4,5},{5,6},{6,7},{7,8},{8,9},{9,10},{10,1... | collective-permute-start | bytes 98312 | tf_op jit(solution)/shard_map/ppermute | solution.py:30
  163.2 1.9 %collective-permute-start.15 = (f32[8,1,1024]{2,0,1:T(8,128)S(1)}, f32[8,1,1024]{2,0,1:T(8,128)S(1)}, u32[]{:S(2)}, u32[]{:S(2)}) collective-permute-start(f32[8,1,1024]{2,0,1:T(8,128)S(1)} %get-tuple-element.35), channel_id=1, source_target_pairs={{1,0},{2,1},{3,2},{4,3},{5,4},{6,5},{7,6},{8,7},{9,8},{10,9},{11,1... | collective-permute-start | bytes 98312 | tf_op jit(solution)/shard_map/ppermute | solution.py:31
  165.1 7.4 %all-to-all-done.3 = f32[256,1,3]{2,1,0:T(1,128)S(1)} async-done(((f32[256,1,3]{2,1,0:T(1,128)}), f32[256,1,3]{2,1,0:T(1,128)S(1)}, u32[]{:S(2)}, u32[]{:S(2)}) %all-to-all-start.3) | async-done | bytes 3104 | tf_op jit(solution)/shard_map/all_to_all | solution.py:130
  177.4 1.1 copy.304
  178.5 1.1 copy.303
  (91 shorter events, 16.0 us)
Async XLA Ops:
  0.6 18.3 %copy-start.3 = (f32[8]{0:T(128)S(1)}, f32[8]{0:T(128)}, u32[]{:S(2)}) copy-start(f32[8]{0:T(128)} %constant.206.clone) | copy-start | bytes 100
  6.9 15.5 %all-to-all-start = ((f32[32,1,64]{2,1,0:T(1,128)}), f32[32,1,64]{2,1,0:T(1,128)S(1)}, u32[]{:S(2)}, u32[]{:S(2)}) async-start(f32[32,1,64]{2,1,0:T(1,128)} %bitcast.6), calls=%async_computation | async-start | bytes 32768 | tf_op jit(solution)/shard_map/all_to_all | solution.py:183
  18.7 6.0 %copy-start.4 = (f32[8]{0:T(128)S(1)}, f32[8]{0:T(128)}, u32[]{:S(2)}) copy-start(f32[8]{0:T(128)} %constant.205.clone) | copy-start | bytes 100
  23.7 3.0 %copy-start.1 = (f32[3,8,16,1024]{3,2,1,0:T(8,128)S(1)}, f32[3,8,16,1024]{3,2,1,0:T(8,128)}, u32[]{:S(2)}) copy-start(f32[3,8,16,1024]{3,2,1,0:T(8,128)} %param.11) | copy-start | bytes 4718596
  26.9 1.6 copy-start.2
  29.8 4.9 %collective-permute-start = (f32[1,16,1024]{2,0,1:T(1,128)S(1)}, f32[1,16,1024]{2,0,1:T(1,128)S(1)}, u32[]{:S(2)}, u32[]{:S(2)}) collective-permute-start(f32[1,16,1024]{2,0,1:T(1,128)S(1)} %get-tuple-element.56), channel_id=1, source_target_pairs={{0,32},{32,64},{64,96},{96,128},{128,160},{160,192},{192,224},{1,3... | collective-permute-start | bytes 196616 | tf_op jit(solution)/shard_map/ppermute | solution.py:30
  33.3 5.2 %collective-permute-start.1 = (f32[1,16,1024]{2,0,1:T(1,128)S(1)}, f32[1,16,1024]{2,0,1:T(1,128)S(1)}, u32[]{:S(2)}, u32[]{:S(2)}) collective-permute-start(f32[1,16,1024]{2,0,1:T(1,128)S(1)} %get-tuple-element.57), channel_id=1, source_target_pairs={{32,0},{64,32},{96,64},{128,96},{160,128},{192,160},{224,192},{33,... | collective-permute-start | bytes 196616 | tf_op jit(solution)/shard_map/ppermute | solution.py:31
  38.8 6.8 %collective-permute-start.2 = (f32[8,1,1024]{2,0,1:T(8,128)S(1)}, f32[8,1,1024]{2,0,1:T(8,128)S(1)}, u32[]{:S(2)}, u32[]{:S(2)}) collective-permute-start(f32[8,1,1024]{2,0,1:T(8,128)S(1)} %get-tuple-element.54), channel_id=1, source_target_pairs={{0,1},{1,2},{2,3},{3,4},{4,5},{5,6},{6,7},{7,8},{8,9},{9,10},{10,1... | collective-permute-start | bytes 98312 | tf_op jit(solution)/shard_map/ppermute | solution.py:30
  42.8 5.2 %collective-permute-start.3 = (f32[8,1,1024]{2,0,1:T(8,128)S(1)}, f32[8,1,1024]{2,0,1:T(8,128)S(1)}, u32[]{:S(2)}, u32[]{:S(2)}) collective-permute-start(f32[8,1,1024]{2,0,1:T(8,128)S(1)} %get-tuple-element.55), channel_id=1, source_target_pairs={{1,0},{2,1},{3,2},{4,3},{5,4},{6,5},{7,6},{8,7},{9,8},{10,9},{11,1... | collective-permute-start | bytes 98312 | tf_op jit(solution)/shard_map/ppermute | solution.py:31
  45.6 3.0 %copy-start = (f32[8,16,1024]{2,1,0:T(8,128)S(1)}, f32[8,16,1024]{2,1,0:T(8,128)}, u32[]{:S(2)}) copy-start(f32[8,16,1024]{2,1,0:T(8,128)} %param.12) | copy-start | bytes 1572868
  54.1 4.9 %collective-permute-start.4 = (f32[1,16,1024]{2,0,1:T(1,128)S(1)}, f32[1,16,1024]{2,0,1:T(1,128)S(1)}, u32[]{:S(2)}, u32[]{:S(2)}) collective-permute-start(f32[1,16,1024]{2,0,1:T(1,128)S(1)} %get-tuple-element.52), channel_id=1, source_target_pairs={{0,32},{32,64},{64,96},{96,128},{128,160},{160,192},{192,224},{1,3... | collective-permute-start | bytes 196616 | tf_op jit(solution)/shard_map/ppermute | solution.py:30
  57.7 6.3 %collective-permute-start.5 = (f32[1,16,1024]{2,0,1:T(1,128)S(1)}, f32[1,16,1024]{2,0,1:T(1,128)S(1)}, u32[]{:S(2)}, u32[]{:S(2)}) collective-permute-start(f32[1,16,1024]{2,0,1:T(1,128)S(1)} %get-tuple-element.53), channel_id=1, source_target_pairs={{32,0},{64,32},{96,64},{128,96},{160,128},{192,160},{224,192},{33,... | collective-permute-start | bytes 196616 | tf_op jit(solution)/shard_map/ppermute | solution.py:31
  65.2 25.9 %all-to-all-start.1 = ((f32[256,1,2]{2,1,0:T(1,128)}), f32[256,1,2]{2,1,0:T(1,128)S(1)}, u32[]{:S(2)}, u32[]{:S(2)}) async-start(f32[256,1,2]{2,1,0:T(1,128)} %broadcast_in_dim.301), calls=%async_computation.1 | async-start | bytes 262144 | tf_op jit(solution)/shard_map/all_to_all | solution.py:130
  78.3 15.1 %collective-permute-start.6 = (f32[8,1,1024]{2,0,1:T(8,128)S(1)}, f32[8,1,1024]{2,0,1:T(8,128)S(1)}, u32[]{:S(2)}, u32[]{:S(2)}) collective-permute-start(f32[8,1,1024]{2,0,1:T(8,128)S(1)} %get-tuple-element.48), channel_id=1, source_target_pairs={{0,1},{1,2},{2,3},{3,4},{4,5},{5,6},{6,7},{7,8},{8,9},{9,10},{10,1... | collective-permute-start | bytes 98312 | tf_op jit(solution)/shard_map/ppermute | solution.py:30
  81.8 11.6 %collective-permute-start.7 = (f32[8,1,1024]{2,0,1:T(8,128)S(1)}, f32[8,1,1024]{2,0,1:T(8,128)S(1)}, u32[]{:S(2)}, u32[]{:S(2)}) collective-permute-start(f32[8,1,1024]{2,0,1:T(8,128)S(1)} %get-tuple-element.49), channel_id=1, source_target_pairs={{1,0},{2,1},{3,2},{4,3},{5,4},{6,5},{7,6},{8,7},{9,8},{10,9},{11,1... | collective-permute-start | bytes 98312 | tf_op jit(solution)/shard_map/ppermute | solution.py:31
  99.5 3.9 %collective-permute-start.8 = (f32[1,16,1024]{2,0,1:T(1,128)S(1)}, f32[1,16,1024]{2,0,1:T(1,128)S(1)}, u32[]{:S(2)}, u32[]{:S(2)}) collective-permute-start(f32[1,16,1024]{2,0,1:T(1,128)S(1)} %get-tuple-element.46), channel_id=1, source_target_pairs={{0,32},{32,64},{64,96},{96,128},{128,160},{160,192},{192,224},{1,3... | collective-permute-start | bytes 196616 | tf_op jit(solution)/shard_map/ppermute | solution.py:30
  102.1 5.0 %collective-permute-start.9 = (f32[1,16,1024]{2,0,1:T(1,128)S(1)}, f32[1,16,1024]{2,0,1:T(1,128)S(1)}, u32[]{:S(2)}, u32[]{:S(2)}) collective-permute-start(f32[1,16,1024]{2,0,1:T(1,128)S(1)} %get-tuple-element.47), channel_id=1, source_target_pairs={{32,0},{64,32},{96,64},{128,96},{160,128},{192,160},{224,192},{33,... | collective-permute-start | bytes 196616 | tf_op jit(solution)/shard_map/ppermute | solution.py:31
  108.4 22.3 %all-to-all-start.2 = ((f32[256,1,3]{2,1,0:T(1,128)}), f32[256,1,3]{2,1,0:T(1,128)S(1)}, u32[]{:S(2)}, u32[]{:S(2)}) async-start(f32[256,1,3]{2,1,0:T(1,128)} %broadcast_in_dim.302), calls=%async_computation.2 | async-start | bytes 262144 | tf_op jit(solution)/shard_map/all_to_all | solution.py:130
  117.8 17.8 %collective-permute-start.10 = (f32[8,1,1024]{2,0,1:T(8,128)S(1)}, f32[8,1,1024]{2,0,1:T(8,128)S(1)}, u32[]{:S(2)}, u32[]{:S(2)}) collective-permute-start(f32[8,1,1024]{2,0,1:T(8,128)S(1)} %get-tuple-element.41), channel_id=1, source_target_pairs={{0,1},{1,2},{2,3},{3,4},{4,5},{5,6},{6,7},{7,8},{8,9},{9,10},{10,1... | collective-permute-start | bytes 98312 | tf_op jit(solution)/shard_map/ppermute | solution.py:30
  121.3 14.3 %collective-permute-start.11 = (f32[8,1,1024]{2,0,1:T(8,128)S(1)}, f32[8,1,1024]{2,0,1:T(8,128)S(1)}, u32[]{:S(2)}, u32[]{:S(2)}) collective-permute-start(f32[8,1,1024]{2,0,1:T(8,128)S(1)} %get-tuple-element.42), channel_id=1, source_target_pairs={{1,0},{2,1},{3,2},{4,3},{5,4},{6,5},{7,6},{8,7},{9,8},{10,9},{11,1... | collective-permute-start | bytes 98312 | tf_op jit(solution)/shard_map/ppermute | solution.py:31
  141.8 3.9 %collective-permute-start.12 = (f32[1,16,1024]{2,0,1:T(1,128)S(1)}, f32[1,16,1024]{2,0,1:T(1,128)S(1)}, u32[]{:S(2)}, u32[]{:S(2)}) collective-permute-start(f32[1,16,1024]{2,0,1:T(1,128)S(1)} %get-tuple-element.39), channel_id=1, source_target_pairs={{0,32},{32,64},{64,96},{96,128},{128,160},{160,192},{192,224},{1,3... | collective-permute-start | bytes 196616 | tf_op jit(solution)/shard_map/ppermute | solution.py:30
  144.4 5.0 %collective-permute-start.13 = (f32[1,16,1024]{2,0,1:T(1,128)S(1)}, f32[1,16,1024]{2,0,1:T(1,128)S(1)}, u32[]{:S(2)}, u32[]{:S(2)}) collective-permute-start(f32[1,16,1024]{2,0,1:T(1,128)S(1)} %get-tuple-element.40), channel_id=1, source_target_pairs={{32,0},{64,32},{96,64},{128,96},{160,128},{192,160},{224,192},{33,... | collective-permute-start | bytes 196616 | tf_op jit(solution)/shard_map/ppermute | solution.py:31
  150.7 21.9 %all-to-all-start.3 = ((f32[256,1,3]{2,1,0:T(1,128)}), f32[256,1,3]{2,1,0:T(1,128)S(1)}, u32[]{:S(2)}, u32[]{:S(2)}) async-start(f32[256,1,3]{2,1,0:T(1,128)} %broadcast_in_dim.303), calls=%async_computation.3 | async-start | bytes 262144 | tf_op jit(solution)/shard_map/all_to_all | solution.py:130
  159.7 17.1 %collective-permute-start.14 = (f32[8,1,1024]{2,0,1:T(8,128)S(1)}, f32[8,1,1024]{2,0,1:T(8,128)S(1)}, u32[]{:S(2)}, u32[]{:S(2)}) collective-permute-start(f32[8,1,1024]{2,0,1:T(8,128)S(1)} %get-tuple-element.34), channel_id=1, source_target_pairs={{0,1},{1,2},{2,3},{3,4},{4,5},{5,6},{6,7},{7,8},{8,9},{9,10},{10,1... | collective-permute-start | bytes 98312 | tf_op jit(solution)/shard_map/ppermute | solution.py:30
  163.2 13.6 %collective-permute-start.15 = (f32[8,1,1024]{2,0,1:T(8,128)S(1)}, f32[8,1,1024]{2,0,1:T(8,128)S(1)}, u32[]{:S(2)}, u32[]{:S(2)}) collective-permute-start(f32[8,1,1024]{2,0,1:T(8,128)S(1)} %get-tuple-element.35), channel_id=1, source_target_pairs={{1,0},{2,1},{3,2},{4,3},{5,4},{6,5},{7,6},{8,7},{9,8},{10,9},{11,1... | collective-permute-start | bytes 98312 | tf_op jit(solution)/shard_map/ppermute | solution.py:31

commit v6 on v4

--- a/solution.py
+++ b/solution.py
@@ -128,7 +128,7 @@
     count = lax.axis_size(axes)
     spread = jnp.broadcast_to(values[None], (count,) + values.shape)
     gathered = lax.all_to_all(spread, axes, 0, 0, tiled=True)
-    return jnp.sum(gathered, axis=0)
+    return jnp.sum(gathered, axis=0)[:, None, None, None]
 
 
 def spread_points(arrived, abscissa, extent0, extent1, extent2):

time: 179 us -> 179 us (level)
  no operation moved by 1% of the time
where the time goes in v6:
time: 179 us; the launch traced here: 178 us
  starting transfers between devices  79.8 us (45%)
  waiting for transfers between devices  44.1 us (25%)
  matrix products  18.9 us (11%)
  other arithmetic  14.3 us (8%)
  local copies, waits for them, and re-layouts  10.7 us (6%)
  between operations  9.77 us (5%)
    all_to_all x3, starting transfers between devices, mesh_sum(): gathered = lax.all_to_all(spread, axes, 0, 0, tiled=True)  31.2 us
    ppermute x8, starting transfers between devices, with_halo(): before = lax.ppermute(last, axis, up)  26.6 us
    all_to_all x3, waiting for transfers between devices, mesh_sum(): gathered = lax.all_to_all(spread, axes, 0, 0, tiled=True)  21.8 us
    ppermute x8, waiting for transfers between devices, with_halo(): after = lax.ppermute(first, axis, down)  18.7 us
    ppermute x8, starting transfers between devices, with_halo(): after = lax.ppermute(first, axis, down)  13.5 us
    all_to_all x1, starting transfers between devices, project_points(): lax.all_to_all(outgoing, 'span', split_axis=0, concat_axis=0, tiled=True)  8.58 us
    dot_general x7, matrix products, derive(): result = jnp.einsum('ia,xayz->xiyz', matrix, blocks, precision=highest)  6.51 us
    dot_general x7, matrix products, derive(): jnp.einsum('ib,xbz->xiz', tiled_matrix, grid_field, precision=highest)  5.93 us
  transfers between devices with their start and end apart: 20, of which 9 were waited for; matrix products, arithmetic and copies ran while one was open for 4% of the time, Pallas kernels for 0%

profile of v6, /device:TPU:1, one launch (start us, length us, event | category | flops | bytes accessed | tf_op | source)
XLA Modules:
  0.0 177.6 jit_solution(8294819425017665487)
XLA Ops:
  0.6 0.7 convert_bitcast_fusion.1
  1.3 0.9 convert_reduce_fusion
  2.2 0.7 convert_bitcast_fusion
  3.0 0.8 select_reduce_fusion
  3.8 0.7 broadcast_multiply_fusion.7
  4.5 0.7 maximum_bitcast_fusion
  5.3 0.9 scatter_custom_fusion
  6.2 0.8 copy.305
  6.9 8.6 %all-to-all-start = ((f32[32,8,8]{1,2,0:T(8,128)}), f32[32,8,8]{1,2,0:T(8,128)S(1)}, u32[]{:S(2)}, u32[]{:S(2)}) async-start(f32[32,8,8]{1,2,0:T(8,128)} %copy.305), calls=%async_computation | async-start | bytes 262144 | tf_op jit(solution)/shard_map/all_to_all | solution.py:183
  16.4 0.7 broadcast_multiply_fusion.6
  17.1 0.8 broadcast_multiply_fusion.3
  17.9 0.9 broadcast_multiply_fusion
  19.6 3.5 %all-to-all-done = f32[32,8,8]{1,2,0:T(8,128)S(1)} async-done(((f32[32,8,8]{1,2,0:T(8,128)}), f32[32,8,8]{1,2,0:T(8,128)S(1)}, u32[]{:S(2)}, u32[]{:S(2)}) %all-to-all-start) | async-done | bytes 8224 | tf_op jit(solution)/shard_map/all_to_all | solution.py:183
  23.5 1.7 fusion.20
  25.5 0.7 fusion.46
  26.3 0.8 convolution_bitcast_fusion.12
  27.1 1.2 fusion.1
  28.4 3.5 %collective-permute-start = (f32[1,16,1024]{2,0,1:T(1,128)S(1)}, f32[1,16,1024]{2,0,1:T(1,128)S(1)}, u32[]{:S(2)}, u32[]{:S(2)}) collective-permute-start(f32[1,16,1024]{2,0,1:T(1,128)S(1)} %get-tuple-element.54), channel_id=1, source_target_pairs={{0,32},{32,64},{64,96},{96,128},{128,160},{160,192},{192,224},{1,3... | collective-permute-start | bytes 196616 | tf_op jit(solution)/shard_map/ppermute | solution.py:30
  31.9 1.3 collective-permute-start.1
  33.2 3.9 %collective-permute-done.1 = f32[1,16,1024]{2,0,1:T(1,128)S(1)} collective-permute-done((f32[1,16,1024]{2,0,1:T(1,128)S(1)}, f32[1,16,1024]{2,0,1:T(1,128)S(1)}, u32[]{:S(2)}, u32[]{:S(2)}) %collective-permute-start.1) | collective-permute-done | bytes 65568 | tf_op jit(solution)/shard_map/ppermute | solution.py:31
  37.4 3.8 %collective-permute-start.2 = (f32[8,1,1024]{2,0,1:T(8,128)S(1)}, f32[8,1,1024]{2,0,1:T(8,128)S(1)}, u32[]{:S(2)}, u32[]{:S(2)}) collective-permute-start(f32[8,1,1024]{2,0,1:T(8,128)S(1)} %get-tuple-element.52), channel_id=1, source_target_pairs={{0,1},{1,2},{2,3},{3,4},{4,5},{5,6},{6,7},{7,8},{8,9},{9,10},{10,1... | collective-permute-start | bytes 98312 | tf_op jit(solution)/shard_map/ppermute | solution.py:30
  41.2 2.1 %collective-permute-start.3 = (f32[8,1,1024]{2,0,1:T(8,128)S(1)}, f32[8,1,1024]{2,0,1:T(8,128)S(1)}, u32[]{:S(2)}, u32[]{:S(2)}) collective-permute-start(f32[8,1,1024]{2,0,1:T(8,128)S(1)} %get-tuple-element.53), channel_id=1, source_target_pairs={{1,0},{2,1},{3,2},{4,3},{5,4},{6,5},{7,6},{8,7},{9,8},{10,9},{11,1... | collective-permute-start | bytes 98312 | tf_op jit(solution)/shard_map/ppermute | solution.py:31
  43.9 2.4 %collective-permute-done.3 = f32[8,1,1024]{2,0,1:T(8,128)S(1)} collective-permute-done((f32[8,1,1024]{2,0,1:T(8,128)S(1)}, f32[8,1,1024]{2,0,1:T(8,128)S(1)}, u32[]{:S(2)}, u32[]{:S(2)}) %collective-permute-start.3) | collective-permute-done | bytes 32800 | tf_op jit(solution)/shard_map/ppermute | solution.py:31
  46.9 0.9 fusion.2
  47.8 0.7 fusion.15
  49.1 0.9 fusion.99
  50.6 0.9 fusion.97
  51.5 0.9 fusion.5
  52.5 3.5 %collective-permute-start.4 = (f32[1,16,1024]{2,0,1:T(1,128)S(1)}, f32[1,16,1024]{2,0,1:T(1,128)S(1)}, u32[]{:S(2)}, u32[]{:S(2)}) collective-permute-start(f32[1,16,1024]{2,0,1:T(1,128)S(1)} %get-tuple-element.50), channel_id=1, source_target_pairs={{0,32},{32,64},{64,96},{96,128},{128,160},{160,192},{192,224},{1,3... | collective-permute-start | bytes 196616 | tf_op jit(solution)/shard_map/ppermute | solution.py:30
  56.1 1.3 collective-permute-start.5
  57.4 5.0 %collective-permute-done.5 = f32[1,16,1024]{2,0,1:T(1,128)S(1)} collective-permute-done((f32[1,16,1024]{2,0,1:T(1,128)S(1)}, f32[1,16,1024]{2,0,1:T(1,128)S(1)}, u32[]{:S(2)}, u32[]{:S(2)}) %collective-permute-start.5) | collective-permute-done | bytes 65568 | tf_op jit(solution)/shard_map/ppermute | solution.py:31
  62.9 0.7 broadcast_in_dim.304
  63.6 12.9 %all-to-all-start.1 = ((f32[256,1,2]{2,1,0:T(1,128)}), f32[256,1,2]{2,1,0:T(1,128)S(1)}, u32[]{:S(2)}, u32[]{:S(2)}) async-start(f32[256,1,2]{2,1,0:T(1,128)} %broadcast_in_dim.304), calls=%async_computation.1 | async-start | bytes 262144 | tf_op jit(solution)/shard_map/all_to_all | solution.py:130
  76.6 3.5 %collective-permute-start.6 = (f32[8,1,1024]{2,0,1:T(8,128)S(1)}, f32[8,1,1024]{2,0,1:T(8,128)S(1)}, u32[]{:S(2)}, u32[]{:S(2)}) collective-permute-start(f32[8,1,1024]{2,0,1:T(8,128)S(1)} %get-tuple-element.46), channel_id=1, source_target_pairs={{0,1},{1,2},{2,3},{3,4},{4,5},{5,6},{6,7},{7,8},{8,9},{9,10},{10,1... | collective-permute-start | bytes 98312 | tf_op jit(solution)/shard_map/ppermute | solution.py:30
  80.1 2.1 %collective-permute-start.7 = (f32[8,1,1024]{2,0,1:T(8,128)S(1)}, f32[8,1,1024]{2,0,1:T(8,128)S(1)}, u32[]{:S(2)}, u32[]{:S(2)}) collective-permute-start(f32[8,1,1024]{2,0,1:T(8,128)S(1)} %get-tuple-element.47), channel_id=1, source_target_pairs={{1,0},{2,1},{3,2},{4,3},{5,4},{6,5},{7,6},{8,7},{9,8},{10,9},{11,1... | collective-permute-start | bytes 98312 | tf_op jit(solution)/shard_map/ppermute | solution.py:31
  82.3 7.2 %all-to-all-done.1 = f32[256,1,2]{2,1,0:T(1,128)S(1)} async-done(((f32[256,1,2]{2,1,0:T(1,128)}), f32[256,1,2]{2,1,0:T(1,128)S(1)}, u32[]{:S(2)}, u32[]{:S(2)}) %all-to-all-start.1) | async-done | bytes 2080 | tf_op jit(solution)/shard_map/all_to_all | solution.py:130
  92.3 0.8 fusion.17
  93.1 0.9 fusion.95
  94.0 0.9 fusion.6
  96.0 0.9 fusion.93
  96.9 0.9 fusion.9
  97.9 2.5 %collective-permute-start.8 = (f32[1,16,1024]{2,0,1:T(1,128)S(1)}, f32[1,16,1024]{2,0,1:T(1,128)S(1)}, u32[]{:S(2)}, u32[]{:S(2)}) collective-permute-start(f32[1,16,1024]{2,0,1:T(1,128)S(1)} %get-tuple-element.44), channel_id=1, source_target_pairs={{0,32},{32,64},{64,96},{96,128},{128,160},{160,192},{192,224},{1,3... | collective-permute-start | bytes 196616 | tf_op jit(solution)/shard_map/ppermute | solution.py:30
  100.5 1.3 collective-permute-start.9
  101.8 3.7 %collective-permute-done.9 = f32[1,16,1024]{2,0,1:T(1,128)S(1)} collective-permute-done((f32[1,16,1024]{2,0,1:T(1,128)S(1)}, f32[1,16,1024]{2,0,1:T(1,128)S(1)}, u32[]{:S(2)}, u32[]{:S(2)}) %collective-permute-start.9) | collective-permute-done | bytes 65568 | tf_op jit(solution)/shard_map/ppermute | solution.py:31
  106.1 0.7 broadcast_in_dim.305
  106.8 9.3 %all-to-all-start.2 = ((f32[256,1,3]{2,1,0:T(1,128)}), f32[256,1,3]{2,1,0:T(1,128)S(1)}, u32[]{:S(2)}, u32[]{:S(2)}) async-start(f32[256,1,3]{2,1,0:T(1,128)} %broadcast_in_dim.305), calls=%async_computation.2 | async-start | bytes 262144 | tf_op jit(solution)/shard_map/all_to_all | solution.py:130
  116.1 3.5 %collective-permute-start.10 = (f32[8,1,1024]{2,0,1:T(8,128)S(1)}, f32[8,1,1024]{2,0,1:T(8,128)S(1)}, u32[]{:S(2)}, u32[]{:S(2)}) collective-permute-start(f32[8,1,1024]{2,0,1:T(8,128)S(1)} %get-tuple-element.39), channel_id=1, source_target_pairs={{0,1},{1,2},{2,3},{3,4},{4,5},{5,6},{6,7},{7,8},{8,9},{9,10},{10,1... | collective-permute-start | bytes 98312 | tf_op jit(solution)/shard_map/ppermute | solution.py:30
  119.6 2.2 %collective-permute-start.11 = (f32[8,1,1024]{2,0,1:T(8,128)S(1)}, f32[8,1,1024]{2,0,1:T(8,128)S(1)}, u32[]{:S(2)}, u32[]{:S(2)}) collective-permute-start(f32[8,1,1024]{2,0,1:T(8,128)S(1)} %get-tuple-element.40), channel_id=1, source_target_pairs={{1,0},{2,1},{3,2},{4,3},{5,4},{6,5},{7,6},{8,7},{9,8},{10,9},{11,1... | collective-permute-start | bytes 98312 | tf_op jit(solution)/shard_map/ppermute | solution.py:31
  121.8 7.2 %all-to-all-done.2 = f32[256,1,3]{2,1,0:T(1,128)S(1)} async-done(((f32[256,1,3]{2,1,0:T(1,128)}), f32[256,1,3]{2,1,0:T(1,128)S(1)}, u32[]{:S(2)}, u32[]{:S(2)}) %all-to-all-start.2) | async-done | bytes 3104 | tf_op jit(solution)/shard_map/all_to_all | solution.py:130
  134.3 0.8 fusion.19
  135.1 0.9 fusion.91
  136.0 0.9 fusion.10
  138.0 0.9 fusion.89
  138.9 0.9 fusion.13
  139.9 2.5 %collective-permute-start.12 = (f32[1,16,1024]{2,0,1:T(1,128)S(1)}, f32[1,16,1024]{2,0,1:T(1,128)S(1)}, u32[]{:S(2)}, u32[]{:S(2)}) collective-permute-start(f32[1,16,1024]{2,0,1:T(1,128)S(1)} %get-tuple-element.37), channel_id=1, source_target_pairs={{0,32},{32,64},{64,96},{96,128},{128,160},{160,192},{192,224},{1,3... | collective-permute-start | bytes 196616 | tf_op jit(solution)/shard_map/ppermute | solution.py:30
  142.5 1.3 collective-permute-start.13
  143.8 3.7 %collective-permute-done.13 = f32[1,16,1024]{2,0,1:T(1,128)S(1)} collective-permute-done((f32[1,16,1024]{2,0,1:T(1,128)S(1)}, f32[1,16,1024]{2,0,1:T(1,128)S(1)}, u32[]{:S(2)}, u32[]{:S(2)}) %collective-permute-start.13) | collective-permute-done | bytes 65568 | tf_op jit(solution)/shard_map/ppermute | solution.py:31
  148.1 0.7 broadcast_in_dim.306
  148.8 9.0 %all-to-all-start.3 = ((f32[256,1,3]{2,1,0:T(1,128)}), f32[256,1,3]{2,1,0:T(1,128)S(1)}, u32[]{:S(2)}, u32[]{:S(2)}) async-start(f32[256,1,3]{2,1,0:T(1,128)} %broadcast_in_dim.306), calls=%async_computation.3 | async-start | bytes 262144 | tf_op jit(solution)/shard_map/all_to_all | solution.py:130
  157.8 3.5 %collective-permute-start.14 = (f32[8,1,1024]{2,0,1:T(8,128)S(1)}, f32[8,1,1024]{2,0,1:T(8,128)S(1)}, u32[]{:S(2)}, u32[]{:S(2)}) collective-permute-start(f32[8,1,1024]{2,0,1:T(8,128)S(1)} %get-tuple-element.32), channel_id=1, source_target_pairs={{0,1},{1,2},{2,3},{3,4},{4,5},{5,6},{6,7},{7,8},{8,9},{9,10},{10,1... | collective-permute-start | bytes 98312 | tf_op jit(solution)/shard_map/ppermute | solution.py:30
  161.3 1.9 %collective-permute-start.15 = (f32[8,1,1024]{2,0,1:T(8,128)S(1)}, f32[8,1,1024]{2,0,1:T(8,128)S(1)}, u32[]{:S(2)}, u32[]{:S(2)}) collective-permute-start(f32[8,1,1024]{2,0,1:T(8,128)S(1)} %get-tuple-element.33), channel_id=1, source_target_pairs={{1,0},{2,1},{3,2},{4,3},{5,4},{6,5},{7,6},{8,7},{9,8},{10,9},{11,1... | collective-permute-start | bytes 98312 | tf_op jit(solution)/shard_map/ppermute | solution.py:31
  163.3 7.4 %all-to-all-done.3 = f32[256,1,3]{2,1,0:T(1,128)S(1)} async-done(((f32[256,1,3]{2,1,0:T(1,128)}), f32[256,1,3]{2,1,0:T(1,128)S(1)}, u32[]{:S(2)}, u32[]{:S(2)}) %all-to-all-start.3) | async-done | bytes 3104 | tf_op jit(solution)/shard_map/all_to_all | solution.py:130
  175.4 1.1 copy.346
  176.5 1.1 copy.345
  (90 shorter events, 13.8 us)
Async XLA Ops:
  0.6 18.3 %copy-start.3 = (f32[8]{0:T(128)S(1)}, f32[8]{0:T(128)}, u32[]{:S(2)}) copy-start(f32[8]{0:T(128)} %constant.206.clone) | copy-start | bytes 100
  6.9 16.2 %all-to-all-start = ((f32[32,8,8]{1,2,0:T(8,128)}), f32[32,8,8]{1,2,0:T(8,128)S(1)}, u32[]{:S(2)}, u32[]{:S(2)}) async-start(f32[32,8,8]{1,2,0:T(8,128)} %copy.305), calls=%async_computation | async-start | bytes 262144 | tf_op jit(solution)/shard_map/all_to_all | solution.py:183
  17.9 5.5 %copy-start.4 = (f32[8]{0:T(128)S(1)}, f32[8]{0:T(128)}, u32[]{:S(2)}) copy-start(f32[8]{0:T(128)} %constant.205.clone) | copy-start | bytes 100
  19.6 5.7 %copy-start.1 = (f32[3,8,16,1024]{3,2,1,0:T(8,128)S(1)}, f32[3,8,16,1024]{3,2,1,0:T(8,128)}, u32[]{:S(2)}) copy-start(f32[3,8,16,1024]{3,2,1,0:T(8,128)} %param.11) | copy-start | bytes 4718596
  25.4 1.6 copy-start.2
  28.4 4.9 %collective-permute-start = (f32[1,16,1024]{2,0,1:T(1,128)S(1)}, f32[1,16,1024]{2,0,1:T(1,128)S(1)}, u32[]{:S(2)}, u32[]{:S(2)}) collective-permute-start(f32[1,16,1024]{2,0,1:T(1,128)S(1)} %get-tuple-element.54), channel_id=1, source_target_pairs={{0,32},{32,64},{64,96},{96,128},{128,160},{160,192},{192,224},{1,3... | collective-permute-start | bytes 196616 | tf_op jit(solution)/shard_map/ppermute | solution.py:30
  31.9 5.2 %collective-permute-start.1 = (f32[1,16,1024]{2,0,1:T(1,128)S(1)}, f32[1,16,1024]{2,0,1:T(1,128)S(1)}, u32[]{:S(2)}, u32[]{:S(2)}) collective-permute-start(f32[1,16,1024]{2,0,1:T(1,128)S(1)} %get-tuple-element.55), channel_id=1, source_target_pairs={{32,0},{64,32},{96,64},{128,96},{160,128},{192,160},{224,192},{33,... | collective-permute-start | bytes 196616 | tf_op jit(solution)/shard_map/ppermute | solution.py:31
  37.4 6.6 %collective-permute-start.2 = (f32[8,1,1024]{2,0,1:T(8,128)S(1)}, f32[8,1,1024]{2,0,1:T(8,128)S(1)}, u32[]{:S(2)}, u32[]{:S(2)}) collective-permute-start(f32[8,1,1024]{2,0,1:T(8,128)S(1)} %get-tuple-element.52), channel_id=1, source_target_pairs={{0,1},{1,2},{2,3},{3,4},{4,5},{5,6},{6,7},{7,8},{8,9},{9,10},{10,1... | collective-permute-start | bytes 98312 | tf_op jit(solution)/shard_map/ppermute | solution.py:30
  41.2 5.2 %collective-permute-start.3 = (f32[8,1,1024]{2,0,1:T(8,128)S(1)}, f32[8,1,1024]{2,0,1:T(8,128)S(1)}, u32[]{:S(2)}, u32[]{:S(2)}) collective-permute-start(f32[8,1,1024]{2,0,1:T(8,128)S(1)} %get-tuple-element.53), channel_id=1, source_target_pairs={{1,0},{2,1},{3,2},{4,3},{5,4},{6,5},{7,6},{8,7},{9,8},{10,9},{11,1... | collective-permute-start | bytes 98312 | tf_op jit(solution)/shard_map/ppermute | solution.py:31
  43.9 3.0 %copy-start = (f32[8,16,1024]{2,1,0:T(8,128)S(1)}, f32[8,16,1024]{2,1,0:T(8,128)}, u32[]{:S(2)}) copy-start(f32[8,16,1024]{2,1,0:T(8,128)} %param.12) | copy-start | bytes 1572868
  52.5 4.9 %collective-permute-start.4 = (f32[1,16,1024]{2,0,1:T(1,128)S(1)}, f32[1,16,1024]{2,0,1:T(1,128)S(1)}, u32[]{:S(2)}, u32[]{:S(2)}) collective-permute-start(f32[1,16,1024]{2,0,1:T(1,128)S(1)} %get-tuple-element.50), channel_id=1, source_target_pairs={{0,32},{32,64},{64,96},{96,128},{128,160},{160,192},{192,224},{1,3... | collective-permute-start | bytes 196616 | tf_op jit(solution)/shard_map/ppermute | solution.py:30
  56.1 6.3 %collective-permute-start.5 = (f32[1,16,1024]{2,0,1:T(1,128)S(1)}, f32[1,16,1024]{2,0,1:T(1,128)S(1)}, u32[]{:S(2)}, u32[]{:S(2)}) collective-permute-start(f32[1,16,1024]{2,0,1:T(1,128)S(1)} %get-tuple-element.51), channel_id=1, source_target_pairs={{32,0},{64,32},{96,64},{128,96},{160,128},{192,160},{224,192},{33,... | collective-permute-start | bytes 196616 | tf_op jit(solution)/shard_map/ppermute | solution.py:31
  63.6 25.9 %all-to-all-start.1 = ((f32[256,1,2]{2,1,0:T(1,128)}), f32[256,1,2]{2,1,0:T(1,128)S(1)}, u32[]{:S(2)}, u32[]{:S(2)}) async-start(f32[256,1,2]{2,1,0:T(1,128)} %broadcast_in_dim.304), calls=%async_computation.1 | async-start | bytes 262144 | tf_op jit(solution)/shard_map/all_to_all | solution.py:130
  76.6 15.2 %collective-permute-start.6 = (f32[8,1,1024]{2,0,1:T(8,128)S(1)}, f32[8,1,1024]{2,0,1:T(8,128)S(1)}, u32[]{:S(2)}, u32[]{:S(2)}) collective-permute-start(f32[8,1,1024]{2,0,1:T(8,128)S(1)} %get-tuple-element.46), channel_id=1, source_target_pairs={{0,1},{1,2},{2,3},{3,4},{4,5},{5,6},{6,7},{7,8},{8,9},{9,10},{10,1... | collective-permute-start | bytes 98312 | tf_op jit(solution)/shard_map/ppermute | solution.py:30
  80.1 11.6 %collective-permute-start.7 = (f32[8,1,1024]{2,0,1:T(8,128)S(1)}, f32[8,1,1024]{2,0,1:T(8,128)S(1)}, u32[]{:S(2)}, u32[]{:S(2)}) collective-permute-start(f32[8,1,1024]{2,0,1:T(8,128)S(1)} %get-tuple-element.47), channel_id=1, source_target_pairs={{1,0},{2,1},{3,2},{4,3},{5,4},{6,5},{7,6},{8,7},{9,8},{10,9},{11,1... | collective-permute-start | bytes 98312 | tf_op jit(solution)/shard_map/ppermute | solution.py:31
  97.9 3.9 %collective-permute-start.8 = (f32[1,16,1024]{2,0,1:T(1,128)S(1)}, f32[1,16,1024]{2,0,1:T(1,128)S(1)}, u32[]{:S(2)}, u32[]{:S(2)}) collective-permute-start(f32[1,16,1024]{2,0,1:T(1,128)S(1)} %get-tuple-element.44), channel_id=1, source_target_pairs={{0,32},{32,64},{64,96},{96,128},{128,160},{160,192},{192,224},{1,3... | collective-permute-start | bytes 196616 | tf_op jit(solution)/shard_map/ppermute | solution.py:30
  100.5 5.0 %collective-permute-start.9 = (f32[1,16,1024]{2,0,1:T(1,128)S(1)}, f32[1,16,1024]{2,0,1:T(1,128)S(1)}, u32[]{:S(2)}, u32[]{:S(2)}) collective-permute-start(f32[1,16,1024]{2,0,1:T(1,128)S(1)} %get-tuple-element.45), channel_id=1, source_target_pairs={{32,0},{64,32},{96,64},{128,96},{160,128},{192,160},{224,192},{33,... | collective-permute-start | bytes 196616 | tf_op jit(solution)/shard_map/ppermute | solution.py:31
  106.8 22.2 %all-to-all-start.2 = ((f32[256,1,3]{2,1,0:T(1,128)}), f32[256,1,3]{2,1,0:T(1,128)S(1)}, u32[]{:S(2)}, u32[]{:S(2)}) async-start(f32[256,1,3]{2,1,0:T(1,128)} %broadcast_in_dim.305), calls=%async_computation.2 | async-start | bytes 262144 | tf_op jit(solution)/shard_map/all_to_all | solution.py:130
  116.1 17.7 %collective-permute-start.10 = (f32[8,1,1024]{2,0,1:T(8,128)S(1)}, f32[8,1,1024]{2,0,1:T(8,128)S(1)}, u32[]{:S(2)}, u32[]{:S(2)}) collective-permute-start(f32[8,1,1024]{2,0,1:T(8,128)S(1)} %get-tuple-element.39), channel_id=1, source_target_pairs={{0,1},{1,2},{2,3},{3,4},{4,5},{5,6},{6,7},{7,8},{8,9},{9,10},{10,1... | collective-permute-start | bytes 98312 | tf_op jit(solution)/shard_map/ppermute | solution.py:30
  119.6 14.1 %collective-permute-start.11 = (f32[8,1,1024]{2,0,1:T(8,128)S(1)}, f32[8,1,1024]{2,0,1:T(8,128)S(1)}, u32[]{:S(2)}, u32[]{:S(2)}) collective-permute-start(f32[8,1,1024]{2,0,1:T(8,128)S(1)} %get-tuple-element.40), channel_id=1, source_target_pairs={{1,0},{2,1},{3,2},{4,3},{5,4},{6,5},{7,6},{8,7},{9,8},{10,9},{11,1... | collective-permute-start | bytes 98312 | tf_op jit(solution)/shard_map/ppermute | solution.py:31
  139.9 3.9 %collective-permute-start.12 = (f32[1,16,1024]{2,0,1:T(1,128)S(1)}, f32[1,16,1024]{2,0,1:T(1,128)S(1)}, u32[]{:S(2)}, u32[]{:S(2)}) collective-permute-start(f32[1,16,1024]{2,0,1:T(1,128)S(1)} %get-tuple-element.37), channel_id=1, source_target_pairs={{0,32},{32,64},{64,96},{96,128},{128,160},{160,192},{192,224},{1,3... | collective-permute-start | bytes 196616 | tf_op jit(solution)/shard_map/ppermute | solution.py:30
  142.5 5.0 %collective-permute-start.13 = (f32[1,16,1024]{2,0,1:T(1,128)S(1)}, f32[1,16,1024]{2,0,1:T(1,128)S(1)}, u32[]{:S(2)}, u32[]{:S(2)}) collective-permute-start(f32[1,16,1024]{2,0,1:T(1,128)S(1)} %get-tuple-element.38), channel_id=1, source_target_pairs={{32,0},{64,32},{96,64},{128,96},{160,128},{192,160},{224,192},{33,... | collective-permute-start | bytes 196616 | tf_op jit(solution)/shard_map/ppermute | solution.py:31
  148.8 21.9 %all-to-all-start.3 = ((f32[256,1,3]{2,1,0:T(1,128)}), f32[256,1,3]{2,1,0:T(1,128)S(1)}, u32[]{:S(2)}, u32[]{:S(2)}) async-start(f32[256,1,3]{2,1,0:T(1,128)} %broadcast_in_dim.306), calls=%async_computation.3 | async-start | bytes 262144 | tf_op jit(solution)/shard_map/all_to_all | solution.py:130
  157.8 17.0 %collective-permute-start.14 = (f32[8,1,1024]{2,0,1:T(8,128)S(1)}, f32[8,1,1024]{2,0,1:T(8,128)S(1)}, u32[]{:S(2)}, u32[]{:S(2)}) collective-permute-start(f32[8,1,1024]{2,0,1:T(8,128)S(1)} %get-tuple-element.32), channel_id=1, source_target_pairs={{0,1},{1,2},{2,3},{3,4},{4,5},{5,6},{6,7},{7,8},{8,9},{9,10},{10,1... | collective-permute-start | bytes 98312 | tf_op jit(solution)/shard_map/ppermute | solution.py:30
  161.3 13.5 %collective-permute-start.15 = (f32[8,1,1024]{2,0,1:T(8,128)S(1)}, f32[8,1,1024]{2,0,1:T(8,128)S(1)}, u32[]{:S(2)}, u32[]{:S(2)}) collective-permute-start(f32[8,1,1024]{2,0,1:T(8,128)S(1)} %get-tuple-element.33), channel_id=1, source_target_pairs={{1,0},{2,1},{3,2},{4,3},{5,4},{6,5},{7,6},{8,7},{9,8},{10,9},{11,1... | collective-permute-start | bytes 98312 | tf_op jit(solution)/shard_map/ppermute | solution.py:31
